TPU v7x, 32 devices: a whole 2x2x4 slice. The times are simulated.
32 devices in a mesh: gx: 8 (over z, x), gy: 4 (over y, core).
Axes of the slice: x: 2, y: 2, z: 4, core: 2. Of those that a mesh axis runs over, the one named last changes fastest.
Arguments:
- adjoint: float32 [3, 128, 64, 128], P(None, 'gx', 'gy'), may hold values from -4 to 4
- base_flow: float32 [3, 128, 64, 128], P(None, 'gx', 'gy'), may hold values from -4 to 4
- metric: float32 [64], P('gy'), may hold values from 0.1 to 1
- smoothing: float32 [64], P('gy'), may hold values from 1.5 to 16
Outputs:
- adjoint_next: float32 [3, 128, 64, 128], P(None, 'gx', 'gy')
- wall_gradient: float32 [2, 128, 128], P(None, 'gx')
All inputs are finite; a program needn't handle non-finite values.
Results may differ from a plain program's by a relative error of at most 0.000071.
Values sent between devices are 32-bit elements; how exact they have to be, the bound alone decides.
No kernel may reach another device: no remote copies, remote signals or barrier semaphores. Data moves between devices by JAX's collectives and lax.ppermute only.
A program may use at most 64 MiB of HBM per device.

v0:
```python
import jax
import jax.numpy as jnp
from jax import lax
from jax.sharding import PartitionSpec as P

step_size = 0.5
highest = lax.Precision.HIGHEST


def padded_2(x, sides, width):
    for axis, dim in sides:
        size, length = (lax.axis_size(axis), x.shape[dim])
        up = [(i, (i + 1) % size) for i in range(size - 1)]
        down = [(j, i) for i, j in up]
        last = lax.slice_in_dim(x, length - width, length, axis=dim)
        first = lax.slice_in_dim(x, 0, width, axis=dim)
        before = lax.ppermute(last, axis, up)
        after = lax.ppermute(first, axis, down)
        x = jnp.concatenate([before, x, after], axis=dim)
    return x


def carried_in(value, axis, join, neutral, backward):
    count, mine = (lax.axis_size(axis), lax.axis_index(axis))
    pieces = jax.tree.map(lambda part: lax.all_gather(part, axis), value)
    if backward:
        pieces = jax.tree.map(lambda part: part[::-1], pieces)
        mine = count - 1 - mine
    total = jax.tree.map(
        lambda part, zero: jnp.full_like(part, 0) + jnp.asarray(zero, part.dtype), value, neutral
    )

    def step(position, total):
        longer = join(total, jax.tree.map(lambda part: part[position], pieces))
        return jax.tree.map(lambda new, old: jnp.where(position < mine, new, old), longer, total)

    return lax.fori_loop(0, count - 1, step, total)


def derivative(padded, metric, direction):
    if direction == 0:
        return 0.5 * (padded[2:, 1:-1] - padded[:-2, 1:-1])
    if direction == 1:
        return metric[None, :, None] * (padded[1:-1, 2:] - padded[1:-1, :-2])
    center = padded[1:-1, 1:-1]
    return 0.5 * (jnp.roll(center, -1, axis=2) - jnp.roll(center, 1, axis=2))


def advect(padded, adjoint, base_flow, metric):
    results = []
    for component in range(3):
        running = jnp.zeros(adjoint.shape[1:], jnp.float32)
        for direction in range(3):
            running = running - base_flow[direction] * derivative(
                padded[component], metric, direction
            )
            running = running + adjoint[direction] * derivative(
                padded[3 + direction], metric, component
            )
        results.append(step_size * running)
    return jnp.stack(results)


def compose(earlier, following):
    return (following[0] * earlier[0], following[0] * earlier[1] + following[1])


def local(adjoint, base_flow, metric, smoothing):
    fields = jnp.concatenate([adjoint, base_flow], axis=0)
    padded = padded_2(fields, (("gx", 1), ("gy", 2)), 1)
    increment = advect(padded, adjoint, base_flow, metric)
    cell_count = adjoint.shape[1]
    decay_rate = 1.0 / (cell_count * smoothing)
    positions = jnp.arange(cell_count, dtype=jnp.float32)
    offsets = positions[:, None] - positions[None, :]
    powers = jnp.where(
        offsets[None] >= 0.0,
        jnp.exp(-jnp.maximum(offsets, 0.0)[None] * decay_rate[:, None, None]),
        0.0,
    )
    local_forward = jnp.einsum("jik,ckjz->cijz", powers, increment, precision=highest)
    block_decay = jnp.exp(-cell_count * decay_rate)[None, :, None]
    lead_power = jnp.exp(-(positions[:, None] + 1.0) * decay_rate[None, :])
    tail_power = jnp.exp(-(cell_count - positions[:, None]) * decay_rate[None, :])
    last_forward = local_forward[:, -1]
    identity = (jnp.ones_like(block_decay), jnp.zeros_like(last_forward))
    inflow = carried_in((block_decay, last_forward), "gx", compose, identity, False)[1]
    carried = local_forward + lead_power[None, :, :, None] * inflow[:, None]
    swept = jnp.einsum("jki,ckjz->cijz", powers, carried, precision=highest)
    return_flow = carried_in((block_decay, swept[:, 0]), "gx", compose, identity, True)[1]
    swept_full = swept + tail_power[None, :, :, None] * return_flow[:, None]
    shrink = jnp.expm1(-decay_rate) ** 2
    adjoint_next = adjoint + shrink[None, None, :, None] * swept_full
    index_y = lax.axis_index("gy")
    count_y = lax.axis_size("gy")
    lower_wall = jnp.where(index_y == 0, 2.0 * metric[0] * adjoint_next[1, :, 0, :], 0.0)
    upper_wall = jnp.where(
        index_y == count_y - 1, -2.0 * metric[-1] * adjoint_next[1, :, -1, :], 0.0
    )
    inverse = 1.0 / metric
    weighted = jnp.einsum("xjz,j->xz", adjoint_next[0], inverse, precision=highest)
    wall_sums, weight_total = lax.psum(
        (jnp.stack([lower_wall, upper_wall, weighted]), jnp.sum(inverse)), "gy"
    )
    bulk_mean = wall_sums[2] / weight_total
    wall_gradient = wall_sums[:2] + bulk_mean[None]
    return (adjoint_next, wall_gradient)


def solution(mesh):
    in_specs = (P(None, "gx", "gy", None), P(None, "gx", "gy", None), P("gy"), P("gy"))
    out_specs = (P(None, "gx", "gy", None), P(None, "gx", None))
    return jax.shard_map(local, mesh=mesh, in_specs=in_specs, out_specs=out_specs, check_vma=False)
```

profile of v0, /device:TPU:0, one launch (start us, length us, event | category | flops | bytes accessed | tf_op | source)
XLA Modules:
  0.0 111.5 jit_solution(7190147289389000831)
XLA Ops:
  0.7 1.2 %fusion.96 = (f32[3,16,16,128]{3,1,2,0:T(8,128)S(1)}, f32[6,16,16,128]{3,1,2,0:T(8,128)S(1)}) fusion(f32[3,16,16,128]{3,2,1,0:T(8,128)} %param.8), kind=kLoop, calls=%fused_computation.156 | loop fusion | bytes 1179648 | tf_op args[0]
  2.1 4.9 %collective-permute-start = (f32[6,1,16,128]{3,1,2,0:T(1,128)S(1)}, f32[6,1,16,128]{3,1,2,0:T(1,128)S(1)}, u32[]{:S(2)}, u32[]{:S(2)}) collective-permute-start(f32[6,1,16,128]{3,1,2,0:T(1,128)S(1)} %get-tuple-element.284), channel_id=1, source_target_pairs={{0,4},{4,8},{8,12},{12,16},{16,20},{20,24},{24,28},{1,5},{5,9},{9,... | collective-permute-start | bytes 147464 | tf_op jit(solution)/shard_map/ppermute | solution.py:17
  7.0 1.3 %collective-permute-start.1 = (f32[6,1,16,128]{3,1,2,0:T(1,128)S(1)}, f32[6,1,16,128]{3,1,2,0:T(1,128)S(1)}, u32[]{:S(2)}, u32[]{:S(2)}) collective-permute-start(f32[6,1,16,128]{3,1,2,0:T(1,128)S(1)} %get-tuple-element.285), channel_id=1, source_target_pairs={{4,0},{8,4},{12,8},{16,12},{20,16},{24,20},{28,24},{5,1},{9,5},{13... | collective-permute-start | bytes 147464 | tf_op jit(solution)/shard_map/ppermute | solution.py:18
  8.3 0.7 fusion.94
  9.0 0.6 dynamic-slice
  10.4 0.6 fusion.110
  11.0 1.9 %collective-permute-done.1 = f32[6,1,16,128]{3,1,2,0:T(1,128)S(1)} collective-permute-done((f32[6,1,16,128]{3,1,2,0:T(1,128)S(1)}, f32[6,1,16,128]{3,1,2,0:T(1,128)S(1)}, u32[]{:S(2)}, u32[]{:S(2)}) %collective-permute-start.1) | collective-permute-done | bytes 49184 | tf_op jit(solution)/shard_map/ppermute | solution.py:18
  13.0 1.3 %collective-permute-start.2 = (f32[6,18,1,128]{3,1,2,0:T(8,128)S(1)}, f32[6,18,1,128]{3,1,2,0:T(8,128)S(1)}, u32[]{:S(2)}, u32[]{:S(2)}) collective-permute-start(f32[6,18,1,128]{3,1,2,0:T(8,128)S(1)} %get-tuple-element.282), channel_id=1, source_target_pairs={{0,1},{1,2},{2,3},{4,5},{5,6},{6,7},{8,9},{9,10},{10,11},{12,13},{... | collective-permute-start | bytes 165896 | tf_op jit(solution)/shard_map/ppermute | solution.py:17
  14.3 1.3 %collective-permute-start.3 = (f32[6,18,1,128]{3,1,2,0:T(8,128)S(1)}, f32[6,18,1,128]{3,1,2,0:T(8,128)S(1)}, u32[]{:S(2)}, u32[]{:S(2)}) collective-permute-start(f32[6,18,1,128]{3,1,2,0:T(8,128)S(1)} %get-tuple-element.283), channel_id=1, source_target_pairs={{1,0},{2,1},{3,2},{5,4},{6,5},{7,6},{9,8},{10,9},{11,10},{13,12},{... | collective-permute-start | bytes 165896 | tf_op jit(solution)/shard_map/ppermute | solution.py:18
  15.6 20.9 %all-reduce = f32[128]{0:T(128)S(1)} all-reduce(f32[128]{0:T(128)S(1)} %exponential_dynamic-update-slice_fusion), channel_id=2, replica_groups=mesh['gx'=8,'gy'=4] {'gx'}, use_global_device_ids=true, to_apply=%add | all-reduce | flops 128 | bytes 1024
  39.0 0.2 fusion.45
  39.2 0.3 fusion.27
  39.5 0.4 fusion.18
  39.9 0.6 convolution_bitcast_fusion.1
  40.5 26.3 %all-gather.1 = f32[24,1,16,128]{3,1,0,2:T(1,128)S(1)} all-gather(f32[3,1,16,128]{3,1,0,2:T(1,128)S(1)} %slice.412), channel_id=3, replica_groups=mesh['gx'=8,'gy'=4] {'gx'}, dimensions={0}, use_global_device_ids=true | all-gather | bytes 221184 | tf_op jit(solution)/shard_map/all_gather | solution.py:25
  66.9 0.6 while.28
  67.6 0.6 convolution_bitcast_fusion
  68.2 26.3 %all-gather.2 = f32[24,1,16,128]{3,1,0,2:T(1,128)S(1)} all-gather(f32[3,1,16,128]{3,1,0,2:T(1,128)S(1)} %slice.413), channel_id=4, replica_groups=mesh['gx'=8,'gy'=4] {'gx'}, dimensions={0}, use_global_device_ids=true | all-gather | bytes 221184 | tf_op jit(solution)/shard_map/all_gather | solution.py:25
  94.6 0.6 while.29
  95.4 0.9 copy.47
  96.3 0.2 fusion.73
  96.6 13.7 %all-reduce.1 = (f32[3,16,128]{2,1,0:T(8,128)S(1)}, f32[]{:T(128)}) all-reduce(f32[3,16,128]{2,1,0:T(8,128)S(1)} %pad_maximum_fusion.4, f32[]{:T(128)} %fusion.94), channel_id=1, replica_groups=mesh['gx'=8,'gy'=4] {'gy'}, use_global_device_ids=true, to_apply=%region_4.5 | all-reduce | flops 6145 | bytes 49160 | tf_op jit(solution)/shard_map/psum | solution.py:102
  110.3 0.6 fusion.83
  110.9 0.6 slice_add_fusion
  (75 shorter events, 3.2 us)
Async XLA Ops:
  0.6 8.4 %copy-start.4 = (u32[32]{0:T(128)S(1)}, u32[32]{0:T(128)}, u32[]{:S(2)}) copy-start(u32[32]{0:T(128)} %constant.83) | copy-start | bytes 388
  0.6 1.2 %copy-start.1 = (f32[3,16,16,128]{3,2,1,0:T(8,128)S(1)}, f32[3,16,16,128]{3,2,1,0:T(8,128)}, u32[]{:S(2)}) copy-start(f32[3,16,16,128]{3,2,1,0:T(8,128)} %param.9) | copy-start | bytes 1179652
  0.7 7.6 %copy-start.3 = (f32[16]{0:T(128)S(1)}, f32[16]{0:T(128)}, u32[]{:S(2)}) copy-start(f32[16]{0:T(128)} %param.11) | copy-start | bytes 196
  0.7 7.7 %copy-start.2 = (f32[16]{0:T(128)S(1)}, f32[16]{0:T(128)}, u32[]{:S(2)}) copy-start(f32[16]{0:T(128)} %param.10) | copy-start | bytes 196
  2.1 9.0 %collective-permute-start = (f32[6,1,16,128]{3,1,2,0:T(1,128)S(1)}, f32[6,1,16,128]{3,1,2,0:T(1,128)S(1)}, u32[]{:S(2)}, u32[]{:S(2)}) collective-permute-start(f32[6,1,16,128]{3,1,2,0:T(1,128)S(1)} %get-tuple-element.284), channel_id=1, source_target_pairs={{0,4},{4,8},{8,12},{12,16},{16,20},{20,24},{24,28},{1,5},{5,9},{9,... | collective-permute-start | bytes 147464 | tf_op jit(solution)/shard_map/ppermute | solution.py:17
  7.0 6.0 %collective-permute-start.1 = (f32[6,1,16,128]{3,1,2,0:T(1,128)S(1)}, f32[6,1,16,128]{3,1,2,0:T(1,128)S(1)}, u32[]{:S(2)}, u32[]{:S(2)}) collective-permute-start(f32[6,1,16,128]{3,1,2,0:T(1,128)S(1)} %get-tuple-element.285), channel_id=1, source_target_pairs={{4,0},{8,4},{12,8},{16,12},{20,16},{24,20},{28,24},{5,1},{9,5},{13... | collective-permute-start | bytes 147464 | tf_op jit(solution)/shard_map/ppermute | solution.py:18
  13.0 24.8 %collective-permute-start.2 = (f32[6,18,1,128]{3,1,2,0:T(8,128)S(1)}, f32[6,18,1,128]{3,1,2,0:T(8,128)S(1)}, u32[]{:S(2)}, u32[]{:S(2)}) collective-permute-start(f32[6,18,1,128]{3,1,2,0:T(8,128)S(1)} %get-tuple-element.282), channel_id=1, source_target_pairs={{0,1},{1,2},{2,3},{4,5},{5,6},{6,7},{8,9},{9,10},{10,11},{12,13},{... | collective-permute-start | bytes 165896 | tf_op jit(solution)/shard_map/ppermute | solution.py:17
  14.3 23.5 %collective-permute-start.3 = (f32[6,18,1,128]{3,1,2,0:T(8,128)S(1)}, f32[6,18,1,128]{3,1,2,0:T(8,128)S(1)}, u32[]{:S(2)}, u32[]{:S(2)}) collective-permute-start(f32[6,18,1,128]{3,1,2,0:T(8,128)S(1)} %get-tuple-element.283), channel_id=1, source_target_pairs={{1,0},{2,1},{3,2},{5,4},{6,5},{7,6},{9,8},{10,9},{11,10},{13,12},{... | collective-permute-start | bytes 165896 | tf_op jit(solution)/shard_map/ppermute | solution.py:18
  67.5 27.7 %copy-start = (f32[3,16,16,128]{3,2,1,0:T(8,128)S(1)}, f32[3,16,16,128]{3,2,1,0:T(8,128)}, u32[]{:S(2)}) copy-start(f32[3,16,16,128]{3,2,1,0:T(8,128)} %param.8) | copy-start | bytes 1179652
where the time goes:
time: 112 us
  blocking collectives  87.3 us (78%)
  starting transfers between devices  8.75 us (8%)
  local copies, waits for them, and re-layouts  4.69 us (4%)
  other arithmetic  4.58 us (4%)
  between operations  2.8 us (2%)
  waiting for transfers between devices  1.91 us (2%)
  matrix products  1.45 us (1%)
    all_gather x2, blocking collectives, carried_in(): pieces = jax.tree.map(lambda part: lax.all_gather(part, axis), value)  52.7 us
    unnamed x1, blocking collectives  20.9 us
    psum x1, blocking collectives, local(): lax.psum((jnp.stack([lower_wall, upper_wall, weighted]), jnp.sum(inverse)...  13.7 us
    ppermute x2, starting transfers between devices, padded_2(): before = lax.ppermute(last, axis, up)  6.17 us
    unnamed x15, local copies, waits for them, and re-layouts  2.78 us
    ppermute x2, starting transfers between devices, padded_2(): after = lax.ppermute(first, axis, down)  2.58 us
  transfers between devices with their start and end apart: 4, of which 1 were waited for; matrix products, arithmetic and copies ran while one was open for 2% of the time, Pallas kernels for 0%

commit v1 on v0

v1 whole, which is shorter than its diff:
```python
import jax
import jax.numpy as jnp
from jax import lax
from jax.sharding import PartitionSpec as P

step_size = 0.5
highest = lax.Precision.HIGHEST
CX = 16
DIRECT_LIMIT = 8


def shift(x, axis, size, step):
    if step > 0:
        pairs = [(j, j + step) for j in range(size - step)]
    else:
        pairs = [(j - step, j) for j in range(size + step)]
    return lax.ppermute(x, axis, pairs)


def halo(f, halves, dim):
    lo, hi = halves
    return (
        jnp.concatenate([lo, lax.slice_in_dim(f, 0, f.shape[dim] - 1, axis=dim)], axis=dim),
        jnp.concatenate([lax.slice_in_dim(f, 1, f.shape[dim], axis=dim), hi], axis=dim),
    )


def increments(adjoint, base_flow, xh, yh, metric):
    m = metric[None, :, None]
    nb = 3

    def diffs(k, f):
        bx, ax = xh[0][k], xh[1][k]
        by, ay = yh[0][k], yh[1][k]
        prev_x, next_x = halo(f, (bx, ax), 0)
        prev_y, next_y = halo(f, (by, ay), 1)
        dx = 0.5 * (next_x - prev_x)
        dy = m * (next_y - prev_y)
        dz = 0.5 * (jnp.roll(f, -1, axis=2) - jnp.roll(f, 1, axis=2))
        return (dx, dy, dz)

    d_adj = [diffs(c, adjoint[c]) for c in range(3)]
    d_base = [diffs(nb + d, base_flow[d]) for d in range(3)]
    results = []
    for c in range(3):
        running = jnp.zeros(adjoint.shape[1:], jnp.float32)
        for d in range(3):
            running = running - base_flow[d] * d_adj[c][d]
            running = running + adjoint[d] * d_base[d][c]
        results.append(step_size * running)
    return jnp.stack(results)


def gx_carries(L, U, A, G, i):
    if G <= DIRECT_LIMIT:
        payload = jnp.stack([L, U])
        inflow = jnp.zeros_like(L)
        ret = jnp.zeros_like(U)
        for k in range(1, G):
            got = lax.ppermute(payload, "gx", [(j, (j + k) % G) for j in range(G)])
            upstream = i >= k
            w_up = A ** (k - 1)
            w_down = A ** (G - k - 1)
            inflow = inflow + jnp.where(upstream, w_up * got[0], 0.0)
            ret = ret + jnp.where(upstream, 0.0, w_down * got[1])
        return inflow, ret
    inflow = shift(L, "gx", G, 1)
    ret = shift(U, "gx", G, -1)
    step = 1
    ratio = A
    while step < G:
        inflow = inflow + ratio * shift(inflow, "gx", G, step)
        ret = ret + ratio * shift(ret, "gx", G, -step)
        ratio = ratio * ratio
        step *= 2
    return inflow, ret


def local(adjoint, base_flow, metric, smoothing):
    G, i = lax.axis_size("gx"), lax.axis_index("gx")
    Gy, g = lax.axis_size("gy"), lax.axis_index("gy")
    n = adjoint.shape[1]

    x_lo = jnp.concatenate([adjoint[:, :1], base_flow[:, :1]])
    x_hi = jnp.concatenate([adjoint[:, -1:], base_flow[:, -1:]])
    y_lo = jnp.concatenate([adjoint[:, :, :1], base_flow[:, :, :1]])
    y_hi = jnp.concatenate([adjoint[:, :, -1:], base_flow[:, :, -1:]])
    xh = (shift(x_hi, "gx", G, 1), shift(x_lo, "gx", G, -1))
    yh = (shift(y_hi, "gy", Gy, 1), shift(y_lo, "gy", Gy, -1))

    increment = increments(adjoint, base_flow, xh, yh, metric)

    rate = 1.0 / (CX * smoothing)
    positions = jnp.arange(n, dtype=jnp.float32)
    offsets = positions[:, None] - positions[None, :]
    powers = jnp.where(
        offsets[None] >= 0.0,
        jnp.exp(-jnp.maximum(offsets, 0.0)[None] * rate[:, None, None]),
        0.0,
    )
    local_forward = jnp.einsum("jik,ckjz->cijz", powers, increment, precision=highest)
    local_back = jnp.einsum("jki,ckjz->cijz", powers, local_forward, precision=highest)

    A = jnp.exp(-n * rate)[None, :, None]
    lead = jnp.exp(-(positions[:, None] + 1.0) * rate[None, :])
    tail = jnp.exp(-(n - positions[:, None]) * rate[None, :])
    back_lead = jnp.einsum("jki,kj->ij", powers, lead, precision=highest)
    c = back_lead[0][None, :, None]
    two_block = jnp.expm1(-2.0 * n * rate)[None, :, None]

    def geo(m):
        return jnp.expm1(-2.0 * n * m * rate)[None, :, None] / two_block

    L = local_forward[:, -1]
    S = local_back[:, 0]
    downstream = (G - 1 - i).astype(jnp.float32)
    geo_here = geo(downstream)
    U = S + c * A * geo_here * L
    inflow, R = gx_carries(L, U, A, G, i)
    ret = R + c * geo_here * (L + A * inflow)

    swept = (
        local_back
        + back_lead[None, :, :, None] * inflow[:, None]
        + tail[None, :, :, None] * ret[:, None]
    )
    shrink = jnp.expm1(-rate) ** 2
    adjoint_next = adjoint + shrink[None, None, :, None] * swept

    lower_wall = jnp.where(g == 0, 2.0 * metric[0] * adjoint_next[1, :, 0, :], 0.0)
    upper_wall = jnp.where(g == Gy - 1, -2.0 * metric[-1] * adjoint_next[1, :, -1, :], 0.0)
    inverse = 1.0 / metric
    weighted = jnp.einsum("xjz,j->xz", adjoint_next[0], inverse, precision=highest)
    total_inv = jnp.broadcast_to(jnp.sum(inverse), weighted.shape)
    part = jnp.stack([lower_wall, upper_wall, weighted, total_inv])
    pieces = [part] + [
        lax.ppermute(part, "gy", [(j, (j + k) % Gy) for j in range(Gy)]) for k in range(1, Gy)
    ]
    stacked = jnp.stack(pieces)
    total = None
    for s in range(Gy):
        piece = lax.dynamic_index_in_dim(stacked, (g - s) % Gy, axis=0, keepdims=False)
        total = piece if total is None else total + piece
    bulk_mean = total[2] / total[3]
    wall_gradient = total[:2] + bulk_mean[None]
    return (adjoint_next, wall_gradient)


def solution(mesh):
    in_specs = (P(None, "gx", "gy", None), P(None, "gx", "gy", None), P("gy"), P("gy"))
    out_specs = (P(None, "gx", "gy", None), P(None, "gx", None))
    return jax.shard_map(local, mesh=mesh, in_specs=in_specs, out_specs=out_specs, check_vma=False)
```

time: 112 us -> 80.2 us (0.72)
  blocking collectives: 87.3 us -> 0 us
  local copies, waits for them, and re-layouts: 4.69 us -> 36.4 us
  starting transfers between devices: 8.75 us -> 26.5 us
  other arithmetic: 4.58 us -> 9.05 us
    all_gather x2 -> x0, blocking collectives: 52.7 us -> none  [carried_in(): pieces = jax.tree.map(lambda part: lax.all_gather(part, axis), value)]
    unnamed x1 -> x0, blocking collectives: 20.9 us -> none
    ppermute x4 -> x14, starting transfers between devices: 8.75 us -> 26.5 us  [the longest x4 12.3 us: shift(): return lax.ppermute(x, axis, pairs)]
    psum x1 -> x0, blocking collectives: 13.7 us -> none  [local(): lax.psum((jnp.stack([lower_wall, upper_wall, weighted]), jnp.sum(inverse)...]
    concatenate x0 -> x24, local copies, waits for them, and re-layouts: none -> 12.3 us  [the longest x18 7.98 us: diffs(): dz = 0.5 * (jnp.roll(f, -1, axis=2) - jnp.roll(f, 1, axis=2))]
    slice x9 -> x31, local copies, waits for them, and re-layouts: 0.97 us -> 10.5 us  [the longest x18 2.68 us: diffs(): dz = 0.5 * (jnp.roll(f, -1, axis=2) - jnp.roll(f, 1, axis=2))]
    unnamed x15 -> x125, local copies, waits for them, and re-layouts: 2.78 us -> 11.9 us
    mul x0 -> x6, other arithmetic: none -> 4.05 us  [the longest x3 2.79 us: increments(): results.append(step_size * running)]
  transfers between devices with their start and end apart: 4 -> 14, of which waited for: 1 -> 5; matrix products, arithmetic and copies ran while one was open for 2% -> 39% of each run, Pallas kernels for 0% -> 0%
where the time goes in v1:
time: 80.2 us; the launch traced here: 79.2 us
  local copies, waits for them, and re-layouts  36.4 us (45%)
  starting transfers between devices  26.5 us (33%)
  other arithmetic  9.05 us (11%)
  between operations  2.77 us (3%)
  waiting for transfers between devices  2.65 us (3%)
  matrix products  1.79 us (2%)
    ppermute x4, starting transfers between devices, shift(): return lax.ppermute(x, axis, pairs)  12.3 us
    unnamed x125, local copies, waits for them, and re-layouts  11.9 us
    ppermute x7, starting transfers between devices, gx_carries(): got = lax.ppermute(payload, 'gx', [(j, (j + k) % G) for j in range(G)])  11.8 us
    concatenate x18, local copies, waits for them, and re-layouts, diffs(): dz = 0.5 * (jnp.roll(f, -1, axis=2) - jnp.roll(f, 1, axis=2))  7.98 us
    concatenate x5, local copies, waits for them, and re-layouts, halo(): jnp.concatenate([lo, lax.slice_in_dim(f, 0, f.shape[dim] - 1, axis=dim)],...  3.57 us
    mul x3, other arithmetic, increments(): results.append(step_size * running)  2.79 us
    slice x18, local copies, waits for them, and re-layouts, diffs(): dz = 0.5 * (jnp.roll(f, -1, axis=2) - jnp.roll(f, 1, axis=2))  2.68 us
    ppermute x3, starting transfers between devices, local(): lax.ppermute(part, 'gy', [(j, (j + k) % Gy) for j in range(Gy)])  2.41 us
  transfers between devices with their start and end apart: 14, of which 5 were waited for; matrix products, arithmetic and copies ran while one was open for 39% of the time, Pallas kernels for 0%

profile of v1, /device:TPU:0, one launch (start us, length us, event | category | flops | bytes accessed | tf_op | source)
XLA Modules:
  0.0 79.2 jit_solution(15972036498370103010)
XLA Ops:
  0.7 0.8 %fusion.145 = (f32[3,1,16,128]{3,2,1,0:T(8,128)S(1)}, f32[3,1,16,128]{3,2,1,0:T(8,128)S(1)}) fusion(f32[3,16,16,128]{3,2,1,0:T(8,128)} %param.4), kind=kLoop, calls=%fused_computation.261 | loop fusion | bytes 98304 | tf_op jit(solution)/shard_map/slice | solution.py:85
  2.9 1.3 %collective-permute-start = (f32[6,1,16,128]{3,1,2,0:T(1,128)}, f32[6,1,16,128]{3,1,2,0:T(1,128)}, u32[]{:S(2)}, u32[]{:S(2)}) collective-permute-start(f32[6,1,16,128]{3,1,2,0:T(1,128)} %pad_maximum_fusion.1), channel_id=1, source_target_pairs={{4,0},{8,4},{12,8},{16,12},{20,16},{24,20},{28,24},{5,1},{9,5},{13... | collective-permute-start | bytes 147464 | tf_op jit(solution)/shard_map/ppermute | solution.py:17
  4.9 6.1 %collective-permute-start.1 = (f32[6,1,16,128]{3,1,2,0:T(1,128)}, f32[6,1,16,128]{3,1,2,0:T(1,128)}, u32[]{:S(2)}, u32[]{:S(2)}) collective-permute-start(f32[6,1,16,128]{3,1,2,0:T(1,128)} %pad_maximum_fusion.2), channel_id=1, source_target_pairs={{0,4},{4,8},{8,12},{12,16},{16,20},{20,24},{24,28},{1,5},{5,9},{9,... | collective-permute-start | bytes 147464 | tf_op jit(solution)/shard_map/ppermute | solution.py:17
  11.0 1.1 %fusion.144 = (f32[3,16,1,128]{3,2,1,0:T(1,128)S(1)}, f32[3,16,1,128]{3,2,1,0:T(1,128)S(1)}) fusion(f32[3,16,16,128]{3,2,1,0:T(8,128)} %param.5), kind=kLoop, calls=%fused_computation.260 | loop fusion | bytes 98304 | tf_op jit(solution)/shard_map/slice | solution.py:87
  12.7 1.3 %collective-permute-start.2 = (f32[6,16,1,128]{3,1,2,0:T(8,128)}, f32[6,16,1,128]{3,1,2,0:T(8,128)}, u32[]{:S(2)}, u32[]{:S(2)}) collective-permute-start(f32[6,16,1,128]{3,1,2,0:T(8,128)} %pad_maximum_fusion.3), channel_id=1, source_target_pairs={{1,0},{2,1},{3,2},{5,4},{6,5},{7,6},{9,8},{10,9},{11,10},{13,12},{... | collective-permute-start | bytes 147464 | tf_op jit(solution)/shard_map/ppermute | solution.py:17
  14.6 3.6 %collective-permute-start.3 = (f32[6,16,1,128]{3,1,2,0:T(8,128)}, f32[6,16,1,128]{3,1,2,0:T(8,128)}, u32[]{:S(2)}, u32[]{:S(2)}) collective-permute-start(f32[6,16,1,128]{3,1,2,0:T(8,128)} %pad_maximum_fusion.4), channel_id=1, source_target_pairs={{0,1},{1,2},{2,3},{4,5},{5,6},{6,7},{8,9},{9,10},{10,11},{12,13},{... | collective-permute-start | bytes 147464 | tf_op jit(solution)/shard_map/ppermute | solution.py:17
  22.7 0.9 %fusion.139 = (f32[1,15,16,128]{3,2,1,0:T(8,128)}, f32[1,15,16,128]{3,2,1,0:T(8,128)}, f32[1,15,16,128]{3,2,1,0:T(8,128)}, f32[1,15,16,128]{3,2,1,0:T(8,128)}, f...) fusion(f32[3,16,16,128]{3,2,1,0:T(8,128)S(1)} %copy-done), kind=kLoop, calls=%fused_computation.255 | loop fusion | bytes 1474560 | tf_op jit(solution)/shard_map/slice | solution.py:24
  27.6 0.9 %fusion.140 = (f32[1,15,16,128]{3,2,1,0:T(8,128)}, f32[1,15,16,128]{3,2,1,0:T(8,128)}, f32[1,15,16,128]{3,2,1,0:T(8,128)}, f32[1,15,16,128]{3,2,1,0:T(8,128)}, f...) fusion(f32[3,16,16,128]{3,2,1,0:T(8,128)S(1)} %copy-done.1), kind=kLoop, calls=%fused_computation.256 | loop fusion | bytes 1474560 | tf_op jit(solution)/shard_map/slice | solution.py:24
  35.7 0.8 %copy.1631 = f32[1,16,16,1]{3,1,2,0:T(8,128)} copy(f32[1,16,16,1]{2,1,3,0:T(8,128)S(1)} %bitcast.521) | data formatting | bytes 2048 | tf_op jit(solution)/shard_map/jit(_roll_static)/concatenate | solution.py:39
  40.5 0.9 %copy-done.18 = f32[1,15,16,128]{3,2,1,0:T(8,128)S(1)} copy-done((f32[1,15,16,128]{3,2,1,0:T(8,128)S(1)}, f32[1,15,16,128]{3,2,1,0:T(8,128)}, u32[]{:S(2)}) %copy-start.18) | copy-done | bytes 122904
  42.7 0.9 %copy-done.16 = f32[1,15,16,128]{3,2,1,0:T(8,128)S(1)} copy-done((f32[1,15,16,128]{3,2,1,0:T(8,128)S(1)}, f32[1,15,16,128]{3,2,1,0:T(8,128)}, u32[]{:S(2)}) %copy-start.16) | copy-done | bytes 122904
  43.6 1.0 %copy.1694 = f32[1,15,16,128]{3,1,2,0:T(8,128)S(1)} copy(f32[1,15,16,128]{3,2,1,0:T(8,128)} %get-tuple-element.46) | data formatting | bytes 245760
  45.1 0.8 %fusion.153 = (f32[1,1,16,128]{3,1,2,0:T(1,128)S(1)}, f32[1,1,16,128]{3,1,2,0:T(1,128)S(1)}, f32[1,1,16,128]{3,1,2,0:T(1,128)S(1)}, f32[1,1,16,128]{3,1,2,0:T(1,...) fusion(f32[6,1,16,128]{3,1,2,0:T(1,128)} %collective-permute-done), kind=kLoop, calls=%fused_computation.269 | loop fusion | bytes 98304 | tf_op jit(solution)/shard_map/slice | solution.py:33
  48.6 1.7 %fusion.35 = f32[1,16,16,128]{3,1,0,2:T(8,128)S(1)} fusion(f32[1,1,16,128]{3,1,2,0:T(1,128)S(1)} %get-tuple-element.103, f32[1,15,16,128]{3,1,2,0:T(8,128)S(1)} %copy-done.6, f32[1,15,16,128]{3,1,2,0:T(8,128)S(1)} %copy-done.7, f32[1,1,16,128]{3,1,2,0:T(1,128)S(1)} %get-tuple-element.109, f32[1,16,16,1]{3,1,2,0:T(8,128)S(1)} %copy-done.4, ...), kind=kLoop, calls=%fused_computation.50 | loop fusion | flops 1212416 | bytes 2490432 | tf_op jit(solution)/shard_map/mul | solution.py:50
  54.1 3.0 %collective-permute-start.10 = (f32[2,3,16,128]{3,2,1,0:T(8,128)S(1)}, f32[2,3,16,128]{3,2,1,0:T(8,128)S(1)}, u32[]{:S(2)}, u32[]{:S(2)}) collective-permute-start(f32[2,3,16,128]{3,2,1,0:T(8,128)S(1)} %pad_maximum_fusion.5), channel_id=1, source_target_pairs={{0,28},{4,0},{8,4},{12,8},{16,12},{20,16},{24,20},{28,24},{1,29},{... | collective-permute-start | bytes 147464 | tf_op jit(solution)/shard_map/ppermute | solution.py:60
  57.7 1.0 %collective-permute-start.5 = (f32[2,3,16,128]{3,2,1,0:T(8,128)S(1)}, f32[2,3,16,128]{3,2,1,0:T(8,128)S(1)}, u32[]{:S(2)}, u32[]{:S(2)}) collective-permute-start(f32[2,3,16,128]{3,2,1,0:T(8,128)S(1)} %pad_maximum_fusion.5), channel_id=1, source_target_pairs={{0,8},{4,12},{8,16},{12,20},{16,24},{20,28},{24,0},{28,4},{1,9},{5... | collective-permute-start | bytes 147464 | tf_op jit(solution)/shard_map/ppermute | solution.py:60
  58.7 3.9 %collective-permute-start.6 = (f32[2,3,16,128]{3,2,1,0:T(8,128)S(1)}, f32[2,3,16,128]{3,2,1,0:T(8,128)S(1)}, u32[]{:S(2)}, u32[]{:S(2)}) collective-permute-start(f32[2,3,16,128]{3,2,1,0:T(8,128)S(1)} %pad_maximum_fusion.5), channel_id=1, source_target_pairs={{0,12},{4,16},{8,20},{12,24},{16,28},{20,0},{24,4},{28,8},{1,13},{... | collective-permute-start | bytes 147464 | tf_op jit(solution)/shard_map/ppermute | solution.py:60
  62.6 1.2 %collective-permute-start.7 = (f32[2,3,16,128]{3,2,1,0:T(8,128)S(1)}, f32[2,3,16,128]{3,2,1,0:T(8,128)S(1)}, u32[]{:S(2)}, u32[]{:S(2)}) collective-permute-start(f32[2,3,16,128]{3,2,1,0:T(8,128)S(1)} %pad_maximum_fusion.5), channel_id=1, source_target_pairs={{0,16},{4,20},{8,24},{12,28},{16,0},{20,4},{24,8},{28,12},{1,17},{... | collective-permute-start | bytes 147464 | tf_op jit(solution)/shard_map/ppermute | solution.py:60
  63.8 1.5 %collective-permute-start.8 = (f32[2,3,16,128]{3,2,1,0:T(8,128)S(1)}, f32[2,3,16,128]{3,2,1,0:T(8,128)S(1)}, u32[]{:S(2)}, u32[]{:S(2)}) collective-permute-start(f32[2,3,16,128]{3,2,1,0:T(8,128)S(1)} %pad_maximum_fusion.5), channel_id=1, source_target_pairs={{0,20},{4,24},{8,28},{12,0},{16,4},{20,8},{24,12},{28,16},{1,21},{... | collective-permute-start | bytes 147464 | tf_op jit(solution)/shard_map/ppermute | solution.py:60
  65.3 1.2 %collective-permute-start.9 = (f32[2,3,16,128]{3,2,1,0:T(8,128)S(1)}, f32[2,3,16,128]{3,2,1,0:T(8,128)S(1)}, u32[]{:S(2)}, u32[]{:S(2)}) collective-permute-start(f32[2,3,16,128]{3,2,1,0:T(8,128)S(1)} %pad_maximum_fusion.5), channel_id=1, source_target_pairs={{0,24},{4,28},{8,0},{12,4},{16,8},{20,12},{24,16},{28,20},{1,25},{... | collective-permute-start | bytes 147464 | tf_op jit(solution)/shard_map/ppermute | solution.py:60
  74.2 1.0 %collective-permute-start.12 = (f32[4,16,128]{2,1,0:T(8,128)S(1)}, f32[4,16,128]{2,1,0:T(8,128)S(1)}, u32[]{:S(2)}, u32[]{:S(2)}) collective-permute-start(f32[4,16,128]{2,1,0:T(8,128)S(1)} %get-tuple-element.127), channel_id=1, source_target_pairs={{0,2},{1,3},{2,0},{3,1},{4,6},{5,7},{6,4},{7,5},{8,10},{9,11},{10,... | collective-permute-start | bytes 98312 | tf_op jit(solution)/shard_map/ppermute | solution.py:137
  75.2 1.4 %collective-permute-start.13 = (f32[4,16,128]{2,1,0:T(8,128)S(1)}, f32[4,16,128]{2,1,0:T(8,128)S(1)}, u32[]{:S(2)}, u32[]{:S(2)}) collective-permute-start(f32[4,16,128]{2,1,0:T(8,128)S(1)} %get-tuple-element.127), channel_id=1, source_target_pairs={{0,3},{1,0},{2,1},{3,2},{4,7},{5,4},{6,5},{7,6},{8,11},{9,8},{10,9... | collective-permute-start | bytes 98312 | tf_op jit(solution)/shard_map/ppermute | solution.py:137
  76.6 0.9 %copy.1679 = f32[3,16,16,128]{3,2,1,0:T(8,128)} copy(f32[3,16,16,128]{3,1,0,2:T(8,128)S(1)} %copy_add_fusion) | data formatting | bytes 786432
  77.5 1.0 %collective-permute-done.12 = f32[4,16,128]{2,1,0:T(8,128)S(1)} collective-permute-done((f32[4,16,128]{2,1,0:T(8,128)S(1)}, f32[4,16,128]{2,1,0:T(8,128)S(1)}, u32[]{:S(2)}, u32[]{:S(2)}) %collective-permute-start.12) | collective-permute-done | bytes 32800 | tf_op jit(solution)/shard_map/ppermute | solution.py:137
  (225 shorter events, 38.2 us)
Async XLA Ops:
  0.6 10.3 %copy-start = (f32[3,16,16,128]{3,2,1,0:T(8,128)S(1)}, f32[3,16,16,128]{3,2,1,0:T(8,128)}, u32[]{:S(2)}) copy-start(f32[3,16,16,128]{3,2,1,0:T(8,128)} %param.4) | copy-start | bytes 1179652
  0.6 17.6 %copy-start.1 = (f32[3,16,16,128]{3,2,1,0:T(8,128)S(1)}, f32[3,16,16,128]{3,2,1,0:T(8,128)}, u32[]{:S(2)}) copy-start(f32[3,16,16,128]{3,2,1,0:T(8,128)} %param.5) | copy-start | bytes 1179652
  2.9 42.2 %collective-permute-start = (f32[6,1,16,128]{3,1,2,0:T(1,128)}, f32[6,1,16,128]{3,1,2,0:T(1,128)}, u32[]{:S(2)}, u32[]{:S(2)}) collective-permute-start(f32[6,1,16,128]{3,1,2,0:T(1,128)} %pad_maximum_fusion.1), channel_id=1, source_target_pairs={{4,0},{8,4},{12,8},{16,12},{20,16},{24,20},{28,24},{5,1},{9,5},{13... | collective-permute-start | bytes 147464 | tf_op jit(solution)/shard_map/ppermute | solution.py:17
  4.9 41.1 %collective-permute-start.1 = (f32[6,1,16,128]{3,1,2,0:T(1,128)}, f32[6,1,16,128]{3,1,2,0:T(1,128)}, u32[]{:S(2)}, u32[]{:S(2)}) collective-permute-start(f32[6,1,16,128]{3,1,2,0:T(1,128)} %pad_maximum_fusion.2), channel_id=1, source_target_pairs={{0,4},{4,8},{8,12},{12,16},{16,20},{20,24},{24,28},{1,5},{5,9},{9,... | collective-permute-start | bytes 147464 | tf_op jit(solution)/shard_map/ppermute | solution.py:17
  12.7 34.1 %collective-permute-start.2 = (f32[6,16,1,128]{3,1,2,0:T(8,128)}, f32[6,16,1,128]{3,1,2,0:T(8,128)}, u32[]{:S(2)}, u32[]{:S(2)}) collective-permute-start(f32[6,16,1,128]{3,1,2,0:T(8,128)} %pad_maximum_fusion.3), channel_id=1, source_target_pairs={{1,0},{2,1},{3,2},{5,4},{6,5},{7,6},{9,8},{10,9},{11,10},{13,12},{... | collective-permute-start | bytes 147464 | tf_op jit(solution)/shard_map/ppermute | solution.py:17
  14.6 33.0 %collective-permute-start.3 = (f32[6,16,1,128]{3,1,2,0:T(8,128)}, f32[6,16,1,128]{3,1,2,0:T(8,128)}, u32[]{:S(2)}, u32[]{:S(2)}) collective-permute-start(f32[6,16,1,128]{3,1,2,0:T(8,128)} %pad_maximum_fusion.4), channel_id=1, source_target_pairs={{0,1},{1,2},{2,3},{4,5},{5,6},{6,7},{8,9},{9,10},{10,11},{12,13},{... | collective-permute-start | bytes 147464 | tf_op jit(solution)/shard_map/ppermute | solution.py:17
  43.6 4.8 %copy-start.14 = (f32[1,16,16,127]{3,1,2,0:T(8,128)S(1)}, f32[1,16,16,127]{3,1,2,0:T(8,128)}, u32[]{:S(2)}) copy-start(f32[1,16,16,127]{3,1,2,0:T(8,128)} %get-tuple-element.100) | copy-start | bytes 390148
  43.6 4.8 %copy-start.15 = (f32[1,16,16,127]{3,1,2,0:T(8,128)S(1)}, f32[1,16,16,127]{3,1,2,0:T(8,128)}, u32[]{:S(2)}) copy-start(f32[1,16,16,127]{3,1,2,0:T(8,128)} %get-tuple-element.101) | copy-start | bytes 390148
  44.7 3.7 %copy-start.13 = (f32[1,16,16,127]{3,1,2,0:T(8,128)S(1)}, f32[1,16,16,127]{3,1,2,0:T(8,128)}, u32[]{:S(2)}) copy-start(f32[1,16,16,127]{3,1,2,0:T(8,128)} %get-tuple-element.95) | copy-start | bytes 390148
  44.7 3.7 %copy-start.41 = (f32[16]{0:T(128)S(1)}, f32[16]{0:T(128)}, u32[]{:S(2)}) copy-start(f32[16]{0:T(128)} %param.6) | copy-start | bytes 196
  44.7 3.7 %copy-start.11 = (f32[1,16,16,127]{3,1,2,0:T(8,128)S(1)}, f32[1,16,16,127]{3,1,2,0:T(8,128)}, u32[]{:S(2)}) copy-start(f32[1,16,16,127]{3,1,2,0:T(8,128)} %get-tuple-element.91) | copy-start | bytes 390148
  54.0 16.7 %copy-start.48 = (f32[16]{0:T(128)S(1)}, f32[16]{0:T(128)}, u32[]{:S(2)}) copy-start(f32[16]{0:T(128)} %get-tuple-element.135) | copy-start | bytes 196
  54.0 16.7 %copy-start.49 = (f32[16]{0:T(128)S(1)}, f32[16]{0:T(128)}, u32[]{:S(2)}) copy-start(f32[16]{0:T(128)} %get-tuple-element.136) | copy-start | bytes 196
  54.0 16.7 %copy-start.50 = (f32[16]{0:T(128)S(1)}, f32[16]{0:T(128)}, u32[]{:S(2)}) copy-start(f32[16]{0:T(128)} %get-tuple-element.139) | copy-start | bytes 196
  54.1 9.7 %collective-permute-start.10 = (f32[2,3,16,128]{3,2,1,0:T(8,128)S(1)}, f32[2,3,16,128]{3,2,1,0:T(8,128)S(1)}, u32[]{:S(2)}, u32[]{:S(2)}) collective-permute-start(f32[2,3,16,128]{3,2,1,0:T(8,128)S(1)} %pad_maximum_fusion.5), channel_id=1, source_target_pairs={{0,28},{4,0},{8,4},{12,8},{16,12},{20,16},{24,20},{28,24},{1,29},{... | collective-permute-start | bytes 147464 | tf_op jit(solution)/shard_map/ppermute | solution.py:60
  57.1 8.2 %collective-permute-start.4 = (f32[2,3,16,128]{3,2,1,0:T(8,128)S(1)}, f32[2,3,16,128]{3,2,1,0:T(8,128)S(1)}, u32[]{:S(2)}, u32[]{:S(2)}) collective-permute-start(f32[2,3,16,128]{3,2,1,0:T(8,128)S(1)} %pad_maximum_fusion.5), channel_id=1, source_target_pairs={{0,4},{4,8},{8,12},{12,16},{16,20},{20,24},{24,28},{28,0},{1,5},{5... | collective-permute-start | bytes 147464 | tf_op jit(solution)/shard_map/ppermute | solution.py:60
  57.7 11.4 %collective-permute-start.5 = (f32[2,3,16,128]{3,2,1,0:T(8,128)S(1)}, f32[2,3,16,128]{3,2,1,0:T(8,128)S(1)}, u32[]{:S(2)}, u32[]{:S(2)}) collective-permute-start(f32[2,3,16,128]{3,2,1,0:T(8,128)S(1)} %pad_maximum_fusion.5), channel_id=1, source_target_pairs={{0,8},{4,12},{8,16},{12,20},{16,24},{20,28},{24,0},{28,4},{1,9},{5... | collective-permute-start | bytes 147464 | tf_op jit(solution)/shard_map/ppermute | solution.py:60
  58.7 10.4 %collective-permute-start.6 = (f32[2,3,16,128]{3,2,1,0:T(8,128)S(1)}, f32[2,3,16,128]{3,2,1,0:T(8,128)S(1)}, u32[]{:S(2)}, u32[]{:S(2)}) collective-permute-start(f32[2,3,16,128]{3,2,1,0:T(8,128)S(1)} %pad_maximum_fusion.5), channel_id=1, source_target_pairs={{0,12},{4,16},{8,20},{12,24},{16,28},{20,0},{24,4},{28,8},{1,13},{... | collective-permute-start | bytes 147464 | tf_op jit(solution)/shard_map/ppermute | solution.py:60
  62.6 7.1 %collective-permute-start.7 = (f32[2,3,16,128]{3,2,1,0:T(8,128)S(1)}, f32[2,3,16,128]{3,2,1,0:T(8,128)S(1)}, u32[]{:S(2)}, u32[]{:S(2)}) collective-permute-start(f32[2,3,16,128]{3,2,1,0:T(8,128)S(1)} %pad_maximum_fusion.5), channel_id=1, source_target_pairs={{0,16},{4,20},{8,24},{12,28},{16,0},{20,4},{24,8},{28,12},{1,17},{... | collective-permute-start | bytes 147464 | tf_op jit(solution)/shard_map/ppermute | solution.py:60
  63.8 6.4 %collective-permute-start.8 = (f32[2,3,16,128]{3,2,1,0:T(8,128)S(1)}, f32[2,3,16,128]{3,2,1,0:T(8,128)S(1)}, u32[]{:S(2)}, u32[]{:S(2)}) collective-permute-start(f32[2,3,16,128]{3,2,1,0:T(8,128)S(1)} %pad_maximum_fusion.5), channel_id=1, source_target_pairs={{0,20},{4,24},{8,28},{12,0},{16,4},{20,8},{24,12},{28,16},{1,21},{... | collective-permute-start | bytes 147464 | tf_op jit(solution)/shard_map/ppermute | solution.py:60
  65.3 5.4 %collective-permute-start.9 = (f32[2,3,16,128]{3,2,1,0:T(8,128)S(1)}, f32[2,3,16,128]{3,2,1,0:T(8,128)S(1)}, u32[]{:S(2)}, u32[]{:S(2)}) collective-permute-start(f32[2,3,16,128]{3,2,1,0:T(8,128)S(1)} %pad_maximum_fusion.5), channel_id=1, source_target_pairs={{0,24},{4,28},{8,0},{12,4},{16,8},{20,12},{24,16},{28,20},{1,25},{... | collective-permute-start | bytes 147464 | tf_op jit(solution)/shard_map/ppermute | solution.py:60
  74.2 3.3 %collective-permute-start.11 = (f32[4,16,128]{2,1,0:T(8,128)S(1)}, f32[4,16,128]{2,1,0:T(8,128)S(1)}, u32[]{:S(2)}, u32[]{:S(2)}) collective-permute-start(f32[4,16,128]{2,1,0:T(8,128)S(1)} %get-tuple-element.127), channel_id=1, source_target_pairs={{0,1},{1,2},{2,3},{3,0},{4,5},{5,6},{6,7},{7,4},{8,9},{9,10},{10,1... | collective-permute-start | bytes 98312 | tf_op jit(solution)/shard_map/ppermute | solution.py:137
  74.2 4.3 %collective-permute-start.12 = (f32[4,16,128]{2,1,0:T(8,128)S(1)}, f32[4,16,128]{2,1,0:T(8,128)S(1)}, u32[]{:S(2)}, u32[]{:S(2)}) collective-permute-start(f32[4,16,128]{2,1,0:T(8,128)S(1)} %get-tuple-element.127), channel_id=1, source_target_pairs={{0,2},{1,3},{2,0},{3,1},{4,6},{5,7},{6,4},{7,5},{8,10},{9,11},{10,... | collective-permute-start | bytes 98312 | tf_op jit(solution)/shard_map/ppermute | solution.py:137
  75.2 3.3 %collective-permute-start.13 = (f32[4,16,128]{2,1,0:T(8,128)S(1)}, f32[4,16,128]{2,1,0:T(8,128)S(1)}, u32[]{:S(2)}, u32[]{:S(2)}) collective-permute-start(f32[4,16,128]{2,1,0:T(8,128)S(1)} %get-tuple-element.127), channel_id=1, source_target_pairs={{0,3},{1,0},{2,1},{3,2},{4,7},{5,4},{6,5},{7,6},{8,11},{9,8},{10,9... | collective-permute-start | bytes 98312 | tf_op jit(solution)/shard_map/ppermute | solution.py:137
  (45 other events, 74.4 us)

commit v2 on v1

v2 whole, which is shorter than its diff:
```python
import functools
import jax
import jax.numpy as jnp
from jax import lax
from jax.experimental import pallas as pl
from jax.experimental.pallas import tpu as pltpu
from jax.sharding import PartitionSpec as P

step_size = 0.5
CX = 16
DIRECT_LIMIT = 8


def shift(x, axis, size, step):
    if step > 0:
        pairs = [(j, j + step) for j in range(size - step)]
    else:
        pairs = [(j - step, j) for j in range(size + step)]
    return lax.ppermute(x, axis, pairs)


def f32(shape):
    return jax.ShapeDtypeStruct(shape, jnp.float32)


def edges_kernel(adj_ref, base_ref, xlo_ref, xhi_ref, ylo_ref, yhi_ref):
    n, ny = adj_ref.shape[1], adj_ref.shape[2]
    for k in range(6):
        ref, c = (adj_ref, k) if k < 3 else (base_ref, k - 3)
        xlo_ref[k] = ref[c, 0]
        xhi_ref[k] = ref[c, n - 1]
        for x in range(n):
            ylo_ref[k, x : x + 1, :] = ref[c, x, 0:1, :]
            yhi_ref[k, x : x + 1, :] = ref[c, x, ny - 1 : ny, :]


def sweep_kernel(adj_ref, base_ref, xlo_ref, xhi_ref, ylo_ref, yhi_ref, coef_ref, sw_ref, pay_ref):
    n, ny, nz = adj_ref.shape[1], adj_ref.shape[2], adj_ref.shape[3]
    metric = coef_ref[0]
    decay = coef_ref[1]
    gain = coef_ref[2]
    row = lax.broadcasted_iota(jnp.int32, (ny, nz), 0)

    def field(k, x):
        if x < 0:
            return xlo_ref[k]
        if x >= n:
            return xhi_ref[k]
        return adj_ref[k, x] if k < 3 else base_ref[k - 3, x]

    forward = [None] * 3
    for x in range(n):
        grads = []
        for k in range(6):
            cur = field(k, x)
            dx = 0.5 * (field(k, x + 1) - field(k, x - 1))
            up = jnp.where(row == ny - 1, yhi_ref[k, x : x + 1, :], pltpu.roll(cur, ny - 1, 0))
            down = jnp.where(row == 0, ylo_ref[k, x : x + 1, :], pltpu.roll(cur, 1, 0))
            dy = metric * (up - down)
            dz = 0.5 * (pltpu.roll(cur, nz - 1, 1) - pltpu.roll(cur, 1, 1))
            grads.append((dx, dy, dz))
        adj = [field(d, x) for d in range(3)]
        base = [field(3 + d, x) for d in range(3)]
        for c in range(3):
            running = None
            for d in range(3):
                term = -(base[d] * grads[c][d])
                running = term if running is None else running + term
                running = running + adj[d] * grads[3 + d][c]
            inc = step_size * running
            forward[c] = inc if x == 0 else inc + decay * forward[c]
            sw_ref[c, x] = forward[c]
    back = [None] * 3
    for x in range(n - 1, -1, -1):
        for c in range(3):
            f = sw_ref[c, x]
            back[c] = f if x == n - 1 else f + decay * back[c]
            sw_ref[c, x] = back[c]
    for c in range(3):
        pay_ref[0, c] = forward[c]
        pay_ref[1, c] = back[c] + gain * forward[c]


def finish_kernel(adj_ref, sw_ref, pay_ref, inflow_ref, rest_ref, coef_ref, out_ref, part_ref):
    n, ny = adj_ref.shape[1], adj_ref.shape[2]
    rate = coef_ref[0]
    decay = coef_ref[1]
    shrink = coef_ref[2]
    inverse = coef_ref[3]
    low_w = coef_ref[4]
    high_w = coef_ref[5]
    near = coef_ref[6]
    ratio = coef_ref[7]
    ret = [rest_ref[c] + near * (pay_ref[0, c] + ratio * inflow_ref[c]) for c in range(3)]
    inflow = [inflow_ref[c] for c in range(3)]
    back_lead = None
    for x in range(n - 1, -1, -1):
        lead = jnp.exp(-(x + 1.0) * rate)
        back_lead = lead if back_lead is None else lead + decay * back_lead
        tail = jnp.exp(-(n - x) * rate)
        vals = []
        for c in range(3):
            v = adj_ref[c, x] + shrink * (sw_ref[c, x] + back_lead * inflow[c] + tail * ret[c])
            out_ref[c, x] = v
            vals.append(v)
        part_ref[0, x : x + 1, :] = (low_w * vals[1])[0:1, :]
        part_ref[1, x : x + 1, :] = (high_w * vals[1])[ny - 1 : ny, :]
        part_ref[2, x : x + 1, :] = jnp.sum(vals[0] * inverse, axis=0, keepdims=True)
    part_ref[3] = jnp.broadcast_to(jnp.sum(inverse, axis=0, keepdims=True), part_ref.shape[1:])


def gx_carries(L, U, A, G, i):
    if G <= DIRECT_LIMIT:
        payload = jnp.stack([L, U])
        inflow = jnp.zeros_like(L)
        ret = jnp.zeros_like(U)
        for k in range(1, G):
            got = lax.ppermute(payload, "gx", [(j, (j + k) % G) for j in range(G)])
            upstream = i >= k
            inflow = inflow + jnp.where(upstream, A ** (k - 1) * got[0], 0.0)
            ret = ret + jnp.where(upstream, 0.0, A ** (G - k - 1) * got[1])
        return inflow, ret
    inflow = shift(L, "gx", G, 1)
    ret = shift(U, "gx", G, -1)
    step = 1
    ratio = A
    while step < G:
        inflow = inflow + ratio * shift(inflow, "gx", G, step)
        ret = ret + ratio * shift(ret, "gx", G, -step)
        ratio = ratio * ratio
        step *= 2
    return inflow, ret


def local(adjoint, base_flow, metric, smoothing):
    G, i = lax.axis_size("gx"), lax.axis_index("gx")
    Gy, g = lax.axis_size("gy"), lax.axis_index("gy")
    _, n, ny, nz = adjoint.shape

    xlo, xhi, ylo, yhi = pl.pallas_call(
        edges_kernel,
        out_shape=(f32((6, ny, nz)), f32((6, ny, nz)), f32((6, n, nz)), f32((6, n, nz))),
    )(adjoint, base_flow)
    x_before = shift(xhi, "gx", G, 1)
    x_after = shift(xlo, "gx", G, -1)
    y_before = shift(yhi, "gy", Gy, 1)
    y_after = shift(ylo, "gy", Gy, -1)

    rate = 1.0 / (CX * smoothing)
    decay = jnp.exp(-rate)
    A = jnp.exp(-n * rate)
    c = jnp.sum(jnp.exp(-(2.0 * jnp.arange(n, dtype=jnp.float32)[:, None] + 1.0) * rate[None, :]), axis=0)
    two_block = jnp.expm1(-2.0 * n * rate)
    downstream = (G - 1 - i).astype(jnp.float32)
    geo_here = jnp.expm1(-2.0 * n * downstream * rate) / two_block

    def rows(*vs):
        return jnp.broadcast_to(jnp.stack(vs)[:, :, None], (len(vs), ny, nz))

    coef_a = rows(metric, decay, c * A * geo_here)
    sw, payload = pl.pallas_call(
        sweep_kernel,
        out_shape=(f32(adjoint.shape), f32((2, 3, ny, nz))),
    )(adjoint, base_flow, x_before, x_after, y_before, y_after, coef_a)

    A3 = A[None, :, None]
    inflow, rest = gx_carries(payload[0], payload[1], A3, G, i)

    low_w = jnp.where(g == 0, 2.0 * metric[0], 0.0) + jnp.zeros_like(metric)
    high_w = jnp.where(g == Gy - 1, -2.0 * metric[-1], 0.0) + jnp.zeros_like(metric)
    coef_b = rows(rate, decay, jnp.expm1(-rate) ** 2, 1.0 / metric, low_w, high_w, c * geo_here, A)
    adjoint_next, part = pl.pallas_call(
        finish_kernel,
        out_shape=(f32(adjoint.shape), f32((4, n, nz))),
    )(adjoint, sw, payload, inflow, rest, coef_b)

    pieces = [part] + [
        lax.ppermute(part, "gy", [(j, (j + k) % Gy) for j in range(Gy)]) for k in range(1, Gy)
    ]
    stacked = jnp.stack(pieces)
    total = None
    for s in range(Gy):
        piece = lax.dynamic_index_in_dim(stacked, (g - s) % Gy, axis=0, keepdims=False)
        total = piece if total is None else total + piece
    bulk_mean = total[2] / total[3]
    wall_gradient = total[:2] + bulk_mean[None]
    return (adjoint_next, wall_gradient)


def solution(mesh):
    in_specs = (P(None, "gx", "gy", None), P(None, "gx", "gy", None), P("gy"), P("gy"))
    out_specs = (P(None, "gx", "gy", None), P(None, "gx", None))
    return jax.shard_map(local, mesh=mesh, in_specs=in_specs, out_specs=out_specs, check_vma=False)
```

time: 80.2 us -> 47 us (0.59)
  local copies, waits for them, and re-layouts: 36.4 us -> 2.68 us
  other arithmetic: 9.05 us -> 2.19 us
  Pallas kernels: 0 us -> 6.36 us
  waiting for transfers between devices: 2.65 us -> 6.69 us
  matrix products: 1.79 us -> 0 us
    concatenate x24 -> x0, local copies, waits for them, and re-layouts: 12.3 us -> none  [the longest x18 7.98 us: diffs(): dz = 0.5 * (jnp.roll(f, -1, axis=2) - jnp.roll(f, 1, axis=2))]
    unnamed x125 -> x14, local copies, waits for them, and re-layouts: 11.9 us -> 0.68 us
    slice x32 -> x1, local copies, waits for them, and re-layouts: 11.2 us -> 0.58 us  [local(): metric[-1]]
    pallas_call x0 -> x3, Pallas kernels: none -> 6.36 us  [the longest x1 2.52 us: local(): pl.pallas_call(sweep_kernel, out_shape=(f32(adjoint.shape), f32((2, 3, ny...]
    mul x6 -> x0, other arithmetic: 4.05 us -> none  [the longest x3 2.79 us: increments(): results.append(step_size * running)]
    ppermute x4, starting transfers between devices: 12.3 us -> 8.91 us  [shift(): return lax.ppermute(x, axis, pairs)]
    ppermute x4, waiting for transfers between devices: 0.01 us -> 2.75 us  [shift(): return lax.ppermute(x, axis, pairs)]
    concatenate x4 -> x0, other arithmetic: 2.57 us -> none  [the longest x1 0.67 us: local(): x_hi = jnp.concatenate([adjoint[:, -1:], base_flow[:, -1:]])]
  transfers between devices with their start and end apart: 14 -> 14, of which waited for: 5 -> 6; matrix products, arithmetic and copies ran while one was open for 39% -> 2% of each run, Pallas kernels for 0% -> 0%
where the time goes in v2:
time: 47 us; the launch traced here: 46.7 us
  starting transfers between devices  26.7 us (57%)
  waiting for transfers between devices  6.69 us (14%)
  Pallas kernels  6.36 us (14%)
  local copies, waits for them, and re-layouts  2.68 us (6%)
  other arithmetic  2.19 us (5%)
  between operations  2.1 us (4%)
    ppermute x7, starting transfers between devices, gx_carries(): got = lax.ppermute(payload, 'gx', [(j, (j + k) % G) for j in range(G)])  13.4 us
    ppermute x4, starting transfers between devices, shift(): return lax.ppermute(x, axis, pairs)  8.91 us
    ppermute x3, starting transfers between devices, local(): lax.ppermute(part, 'gy', [(j, (j + k) % Gy) for j in range(Gy)])  4.42 us
    ppermute x4, waiting for transfers between devices, shift(): return lax.ppermute(x, axis, pairs)  2.75 us
    pallas_call x1, Pallas kernels, local(): pl.pallas_call(sweep_kernel, out_shape=(f32(adjoint.shape), f32((2, 3, ny...  2.52 us
    ppermute x7, waiting for transfers between devices, gx_carries(): got = lax.ppermute(payload, 'gx', [(j, (j + k) % G) for j in range(G)])  2.02 us
    pallas_call x1, Pallas kernels, local(): pl.pallas_call(finish_kernel, out_shape=(f32(adjoint.shape), f32((4, n, n...  2.01 us
    ppermute x3, waiting for transfers between devices, local(): lax.ppermute(part, 'gy', [(j, (j + k) % Gy) for j in range(Gy)])  1.91 us
  transfers between devices with their start and end apart: 14, of which 6 were waited for; matrix products, arithmetic and copies ran while one was open for 2% of the time, Pallas kernels for 0%

profile of v2, /device:TPU:0, one launch (start us, length us, event | category | flops | bytes accessed | tf_op | source)
XLA Modules:
  0.0 46.7 jit_solution(17488042316752249614)
XLA Ops:
  0.6 1.8 %shard_map.59 = (f32[6,16,128]{2,1,0:T(8,128)}, f32[6,16,128]{2,1,0:T(8,128)}, f32[6,16,128]{2,1,0:T(8,128)}, f32[6,16,128]{2,1,0:T(8,128)}) custom-call(f32[3,16,16,128]{3,2,1,0:T(8,128)} %adj_ref.5, f32[3,16,16,128]{3,2,1,0:T(8,128)} %base_ref.3), custom_call_target="tpu_custom_call" | custom-call | tf_op jit(solution)/shard_map/pallas_call | solution.py:140
  2.5 4.9 %collective-permute-start = (f32[6,16,128]{2,1,0:T(8,128)}, f32[6,16,128]{2,1,0:T(8,128)S(1)}, u32[]{:S(2)}, u32[]{:S(2)}) collective-permute-start(f32[6,16,128]{2,1,0:T(8,128)} %get-tuple-element.10), channel_id=1, source_target_pairs={{0,4},{4,8},{8,12},{12,16},{16,20},{20,24},{24,28},{1,5},{5,9},{9,... | collective-permute-start | bytes 147464 | tf_op jit(solution)/shard_map/ppermute | solution.py:19
  7.3 1.3 %collective-permute-start.1 = (f32[6,16,128]{2,1,0:T(8,128)}, f32[6,16,128]{2,1,0:T(8,128)S(1)}, u32[]{:S(2)}, u32[]{:S(2)}) collective-permute-start(f32[6,16,128]{2,1,0:T(8,128)} %get-tuple-element.11), channel_id=1, source_target_pairs={{4,0},{8,4},{12,8},{16,12},{20,16},{24,20},{28,24},{5,1},{9,5},{13... | collective-permute-start | bytes 147464 | tf_op jit(solution)/shard_map/ppermute | solution.py:19
  8.6 1.5 %collective-permute-start.2 = (f32[6,16,128]{2,1,0:T(8,128)}, f32[6,16,128]{2,1,0:T(8,128)S(1)}, u32[]{:S(2)}, u32[]{:S(2)}) collective-permute-start(f32[6,16,128]{2,1,0:T(8,128)} %get-tuple-element.12), channel_id=1, source_target_pairs={{0,1},{1,2},{2,3},{4,5},{5,6},{6,7},{8,9},{9,10},{10,11},{12,13},{... | collective-permute-start | bytes 147464 | tf_op jit(solution)/shard_map/ppermute | solution.py:19
  10.1 1.3 %collective-permute-start.3 = (f32[6,16,128]{2,1,0:T(8,128)}, f32[6,16,128]{2,1,0:T(8,128)S(1)}, u32[]{:S(2)}, u32[]{:S(2)}) collective-permute-start(f32[6,16,128]{2,1,0:T(8,128)} %get-tuple-element.13), channel_id=1, source_target_pairs={{1,0},{2,1},{3,2},{5,4},{6,5},{7,6},{9,8},{10,9},{11,10},{13,12},{... | collective-permute-start | bytes 147464 | tf_op jit(solution)/shard_map/ppermute | solution.py:19
  12.3 1.3 %collective-permute-done.1.xhi_ref = f32[6,16,128]{2,1,0:T(8,128)S(1)} collective-permute-done((f32[6,16,128]{2,1,0:T(8,128)}, f32[6,16,128]{2,1,0:T(8,128)S(1)}, u32[]{:S(2)}, u32[]{:S(2)}) %collective-permute-start.1) | collective-permute-done | bytes 49184 | tf_op jit(solution)/shard_map/ppermute | solution.py:19
  13.5 1.5 %collective-permute-done.3.yhi_ref = f32[6,16,128]{2,1,0:T(8,128)S(1)} collective-permute-done((f32[6,16,128]{2,1,0:T(8,128)}, f32[6,16,128]{2,1,0:T(8,128)S(1)}, u32[]{:S(2)}, u32[]{:S(2)}) %collective-permute-start.3) | collective-permute-done | bytes 49184 | tf_op jit(solution)/shard_map/ppermute | solution.py:19
  15.0 0.7 %broadcast_in_dim.38.coef_ref = f32[3,16,128]{2,1,0:T(8,128)} broadcast(f32[3,16]{1,0:T(4,128)S(1)} %pad_maximum_fusion.1), dimensions={0,1} | broadcast | bytes 24768 | tf_op jit(solution)/shard_map/broadcast_in_dim | solution.py:158
  15.7 2.5 %shard_map.60 = (f32[3,16,16,128]{3,2,1,0:T(8,128)}, f32[2,3,16,128]{3,2,1,0:T(8,128)}) custom-call(f32[3,16,16,128]{3,2,1,0:T(8,128)} %adj_ref.5, f32[3,16,16,128]{3,2,1,0:T(8,128)} %base_ref.3, f32[6,16,128]{2,1,0:T(8,128)} %copy-done, f32[6,16,128]{2,1,0:T(8,128)} %copy-done.1, f32[6,16,128]{2,1,0:T(8,128)} %copy-done.2, f32[6,16,128]{2,1,0:T(8,128)} %copy-done.3, ...), custom_call_target="tpu_custom_call" | custom-call | tf_op jit(solution)/shard_map/pallas_call | solution.py:161
  18.2 5.7 %collective-permute-start.10 = (f32[2,3,16,128]{3,2,1,0:T(8,128)}, f32[2,3,16,128]{3,2,1,0:T(8,128)S(1)}, u32[]{:S(2)}, u32[]{:S(2)}) collective-permute-start(f32[2,3,16,128]{3,2,1,0:T(8,128)} %get-tuple-element.15.pay_ref), channel_id=1, source_target_pairs={{0,28},{4,0},{8,4},{12,8},{16,12},{20,16},{24,20},{28,24},{1,29},{... | collective-permute-start | bytes 147464 | tf_op jit(solution)/shard_map/ppermute | solution.py:118
  23.9 2.5 %collective-permute-start.6 = (f32[2,3,16,128]{3,2,1,0:T(8,128)}, f32[2,3,16,128]{3,2,1,0:T(8,128)S(1)}, u32[]{:S(2)}, u32[]{:S(2)}) collective-permute-start(f32[2,3,16,128]{3,2,1,0:T(8,128)} %get-tuple-element.15.pay_ref), channel_id=1, source_target_pairs={{0,12},{4,16},{8,20},{12,24},{16,28},{20,0},{24,4},{28,8},{1,13},{... | collective-permute-start | bytes 147464 | tf_op jit(solution)/shard_map/ppermute | solution.py:118
  26.4 2.8 %collective-permute-start.7 = (f32[2,3,16,128]{3,2,1,0:T(8,128)}, f32[2,3,16,128]{3,2,1,0:T(8,128)S(1)}, u32[]{:S(2)}, u32[]{:S(2)}) collective-permute-start(f32[2,3,16,128]{3,2,1,0:T(8,128)} %get-tuple-element.15.pay_ref), channel_id=1, source_target_pairs={{0,16},{4,20},{8,24},{12,28},{16,0},{20,4},{24,8},{28,12},{1,17},{... | collective-permute-start | bytes 147464 | tf_op jit(solution)/shard_map/ppermute | solution.py:118
  29.2 1.1 %collective-permute-start.8 = (f32[2,3,16,128]{3,2,1,0:T(8,128)}, f32[2,3,16,128]{3,2,1,0:T(8,128)S(1)}, u32[]{:S(2)}, u32[]{:S(2)}) collective-permute-start(f32[2,3,16,128]{3,2,1,0:T(8,128)} %get-tuple-element.15.pay_ref), channel_id=1, source_target_pairs={{0,20},{4,24},{8,28},{12,0},{16,4},{20,8},{24,12},{28,16},{1,21},{... | collective-permute-start | bytes 147464 | tf_op jit(solution)/shard_map/ppermute | solution.py:118
  30.9 1.3 %collective-permute-start.9 = (f32[2,3,16,128]{3,2,1,0:T(8,128)}, f32[2,3,16,128]{3,2,1,0:T(8,128)S(1)}, u32[]{:S(2)}, u32[]{:S(2)}) collective-permute-start(f32[2,3,16,128]{3,2,1,0:T(8,128)} %get-tuple-element.15.pay_ref), channel_id=1, source_target_pairs={{0,24},{4,28},{8,0},{12,4},{16,8},{20,12},{24,16},{28,20},{1,25},{... | collective-permute-start | bytes 147464 | tf_op jit(solution)/shard_map/ppermute | solution.py:118
  34.2 1.4 %collective-permute-done.6 = f32[2,3,16,128]{3,2,1,0:T(8,128)S(1)} collective-permute-done((f32[2,3,16,128]{3,2,1,0:T(8,128)}, f32[2,3,16,128]{3,2,1,0:T(8,128)S(1)}, u32[]{:S(2)}, u32[]{:S(2)}) %collective-permute-start.6) | collective-permute-done | bytes 49184 | tf_op jit(solution)/shard_map/ppermute | solution.py:118
  35.6 0.7 %fusion.1.rest_ref = f32[3,16,128]{2,1,0:T(8,128)} fusion(f32[2,3,16,128]{3,2,1,0:T(8,128)S(1)} %collective-permute-done.10, f32[2,3,16,128]{3,2,1,0:T(8,128)S(1)} %collective-permute-done.9, f32[2,3,16,128]{3,2,1,0:T(8,128)S(1)} %collective-permute-done.8, f32[2,3,16,128]{3,2,1,0:T(8,128)S(1)} %collective-permute-done.7, ...), kind=kLoop, calls=%fused_computation.4 | loop fusion | flops 116736 | bytes 196999 | tf_op jit(solution)/shard_map/add | solution.py:121
  36.3 0.7 %fusion.21.inflow_ref = f32[3,16,128]{2,1,0:T(8,128)} fusion(f32[2,3,16,128]{3,2,1,0:T(8,128)S(1)} %collective-permute-done.10, f32[2,3,16,128]{3,2,1,0:T(8,128)S(1)} %collective-permute-done.9, f32[2,3,16,128]{3,2,1,0:T(8,128)S(1)} %collective-permute-done.8, f32[2,3,16,128]{3,2,1,0:T(8,128)S(1)} %collective-permute-done.7, ...), kind=kLoop, calls=%fused_computation.31 | loop fusion | flops 116736 | bytes 196999 | tf_op jit(solution)/shard_map/add | solution.py:120
  37.0 0.7 %broadcast_in_dim.42.coef_ref = f32[8,16,128]{2,1,0:T(8,128)} broadcast(f32[8,16]{1,0:T(8,128)S(1)} %stack.61), dimensions={0,1} | broadcast | bytes 66048 | tf_op jit(solution)/shard_map/broadcast_in_dim | solution.py:158
  37.7 2.0 %shard_map.61 = (f32[3,16,16,128]{3,2,1,0:T(8,128)}, f32[4,16,128]{2,1,0:T(8,128)}) custom-call(f32[3,16,16,128]{3,2,1,0:T(8,128)} %adj_ref.5, f32[3,16,16,128]{3,2,1,0:T(8,128)} %get-tuple-element.14.sw_ref, f32[2,3,16,128]{3,2,1,0:T(8,128)} %get-tuple-element.15.pay_ref, f32[3,16,128]{2,1,0:T(8,128)} %fusion.21.inflow_ref, f32[3,16,128]{2,1,0:T(8,128)} %fusion.1.rest_ref, ...), custom_call_target="tpu_custom_call" | custom-call | tf_op jit(solution)/shard_map/pallas_call | solution.py:172
  39.7 1.3 %collective-permute-start.11 = (f32[4,16,128]{2,1,0:T(8,128)}, f32[4,16,128]{2,1,0:T(8,128)S(1)}, u32[]{:S(2)}, u32[]{:S(2)}) collective-permute-start(f32[4,16,128]{2,1,0:T(8,128)} %get-tuple-element.17), channel_id=1, source_target_pairs={{0,1},{1,2},{2,3},{3,0},{4,5},{5,6},{6,7},{7,4},{8,9},{9,10},{10,1... | collective-permute-start | bytes 98312 | tf_op jit(solution)/shard_map/ppermute | solution.py:178
  41.0 1.6 %collective-permute-start.12 = (f32[4,16,128]{2,1,0:T(8,128)}, f32[4,16,128]{2,1,0:T(8,128)S(1)}, u32[]{:S(2)}, u32[]{:S(2)}) collective-permute-start(f32[4,16,128]{2,1,0:T(8,128)} %get-tuple-element.17), channel_id=1, source_target_pairs={{0,2},{1,3},{2,0},{3,1},{4,6},{5,7},{6,4},{7,5},{8,10},{9,11},{10,... | collective-permute-start | bytes 98312 | tf_op jit(solution)/shard_map/ppermute | solution.py:178
  42.6 1.5 %collective-permute-start.13 = (f32[4,16,128]{2,1,0:T(8,128)}, f32[4,16,128]{2,1,0:T(8,128)S(1)}, u32[]{:S(2)}, u32[]{:S(2)}) collective-permute-start(f32[4,16,128]{2,1,0:T(8,128)} %get-tuple-element.17), channel_id=1, source_target_pairs={{0,3},{1,0},{2,1},{3,2},{4,7},{5,4},{6,5},{7,6},{8,11},{9,8},{10,9... | collective-permute-start | bytes 98312 | tf_op jit(solution)/shard_map/ppermute | solution.py:178
  44.1 1.0 %collective-permute-done.12 = f32[4,16,128]{2,1,0:T(8,128)S(1)} collective-permute-done((f32[4,16,128]{2,1,0:T(8,128)}, f32[4,16,128]{2,1,0:T(8,128)S(1)}, u32[]{:S(2)}, u32[]{:S(2)}) %collective-permute-start.12) | collective-permute-done | bytes 32800 | tf_op jit(solution)/shard_map/ppermute | solution.py:178
  45.2 0.9 %collective-permute-done.13 = f32[4,16,128]{2,1,0:T(8,128)S(1)} collective-permute-done((f32[4,16,128]{2,1,0:T(8,128)}, f32[4,16,128]{2,1,0:T(8,128)S(1)}, u32[]{:S(2)}, u32[]{:S(2)}) %collective-permute-start.13) | collective-permute-done | bytes 32800 | tf_op jit(solution)/shard_map/ppermute | solution.py:178
  (39 shorter events, 2.7 us)
Async XLA Ops:
  2.5 9.8 %collective-permute-start = (f32[6,16,128]{2,1,0:T(8,128)}, f32[6,16,128]{2,1,0:T(8,128)S(1)}, u32[]{:S(2)}, u32[]{:S(2)}) collective-permute-start(f32[6,16,128]{2,1,0:T(8,128)} %get-tuple-element.10), channel_id=1, source_target_pairs={{0,4},{4,8},{8,12},{12,16},{16,20},{20,24},{24,28},{1,5},{5,9},{9,... | collective-permute-start | bytes 147464 | tf_op jit(solution)/shard_map/ppermute | solution.py:19
  7.3 6.2 %collective-permute-start.1 = (f32[6,16,128]{2,1,0:T(8,128)}, f32[6,16,128]{2,1,0:T(8,128)S(1)}, u32[]{:S(2)}, u32[]{:S(2)}) collective-permute-start(f32[6,16,128]{2,1,0:T(8,128)} %get-tuple-element.11), channel_id=1, source_target_pairs={{4,0},{8,4},{12,8},{16,12},{20,16},{24,20},{28,24},{5,1},{9,5},{13... | collective-permute-start | bytes 147464 | tf_op jit(solution)/shard_map/ppermute | solution.py:19
  8.6 4.9 %collective-permute-start.2 = (f32[6,16,128]{2,1,0:T(8,128)}, f32[6,16,128]{2,1,0:T(8,128)S(1)}, u32[]{:S(2)}, u32[]{:S(2)}) collective-permute-start(f32[6,16,128]{2,1,0:T(8,128)} %get-tuple-element.12), channel_id=1, source_target_pairs={{0,1},{1,2},{2,3},{4,5},{5,6},{6,7},{8,9},{9,10},{10,11},{12,13},{... | collective-permute-start | bytes 147464 | tf_op jit(solution)/shard_map/ppermute | solution.py:19
  10.1 1.3 %copy-start.6 = (f32[16]{0:T(128)S(1)}, f32[16]{0:T(128)}, u32[]{:S(2)}) copy-start(f32[16]{0:T(128)} %param.7) | copy-start | bytes 196
  10.1 4.9 %collective-permute-start.3 = (f32[6,16,128]{2,1,0:T(8,128)}, f32[6,16,128]{2,1,0:T(8,128)S(1)}, u32[]{:S(2)}, u32[]{:S(2)}) collective-permute-start(f32[6,16,128]{2,1,0:T(8,128)} %get-tuple-element.13), channel_id=1, source_target_pairs={{1,0},{2,1},{3,2},{5,4},{6,5},{7,6},{9,8},{10,9},{11,10},{13,12},{... | collective-permute-start | bytes 147464 | tf_op jit(solution)/shard_map/ppermute | solution.py:19
  11.6 0.7 %copy-start.5 = (f32[16]{0:T(128)S(1)}, f32[16]{0:T(128)}, u32[]{:S(2)}) copy-start(f32[16]{0:T(128)} %param.6) | copy-start | bytes 196
  12.3 3.4 %copy-start = (f32[6,16,128]{2,1,0:T(8,128)}, f32[6,16,128]{2,1,0:T(8,128)S(1)}, u32[]{:S(2)}) copy-start(f32[6,16,128]{2,1,0:T(8,128)S(1)} %collective-permute-done.xlo_ref) | copy-start | bytes 147460
  13.5 2.2 %copy-start.1 = (f32[6,16,128]{2,1,0:T(8,128)}, f32[6,16,128]{2,1,0:T(8,128)S(1)}, u32[]{:S(2)}) copy-start(f32[6,16,128]{2,1,0:T(8,128)S(1)} %collective-permute-done.1.xhi_ref) | copy-start | bytes 147460
  13.5 2.2 %copy-start.2 = (f32[6,16,128]{2,1,0:T(8,128)}, f32[6,16,128]{2,1,0:T(8,128)S(1)}, u32[]{:S(2)}) copy-start(f32[6,16,128]{2,1,0:T(8,128)S(1)} %collective-permute-done.2.ylo_ref) | copy-start | bytes 147460
  15.0 0.7 %copy-start.3 = (f32[6,16,128]{2,1,0:T(8,128)}, f32[6,16,128]{2,1,0:T(8,128)S(1)}, u32[]{:S(2)}) copy-start(f32[6,16,128]{2,1,0:T(8,128)S(1)} %collective-permute-done.3.yhi_ref) | copy-start | bytes 147460
  18.2 11.0 %collective-permute-start.10 = (f32[2,3,16,128]{3,2,1,0:T(8,128)}, f32[2,3,16,128]{3,2,1,0:T(8,128)S(1)}, u32[]{:S(2)}, u32[]{:S(2)}) collective-permute-start(f32[2,3,16,128]{3,2,1,0:T(8,128)} %get-tuple-element.15.pay_ref), channel_id=1, source_target_pairs={{0,28},{4,0},{8,4},{12,8},{16,12},{20,16},{24,20},{28,24},{1,29},{... | collective-permute-start | bytes 147464 | tf_op jit(solution)/shard_map/ppermute | solution.py:118
  23.9 7.0 %collective-permute-start.4 = (f32[2,3,16,128]{3,2,1,0:T(8,128)}, f32[2,3,16,128]{3,2,1,0:T(8,128)S(1)}, u32[]{:S(2)}, u32[]{:S(2)}) collective-permute-start(f32[2,3,16,128]{3,2,1,0:T(8,128)} %get-tuple-element.15.pay_ref), channel_id=1, source_target_pairs={{0,4},{4,8},{8,12},{12,16},{16,20},{20,24},{24,28},{28,0},{1,5},{5... | collective-permute-start | bytes 147464 | tf_op jit(solution)/shard_map/ppermute | solution.py:118
  23.9 10.2 %collective-permute-start.5 = (f32[2,3,16,128]{3,2,1,0:T(8,128)}, f32[2,3,16,128]{3,2,1,0:T(8,128)S(1)}, u32[]{:S(2)}, u32[]{:S(2)}) collective-permute-start(f32[2,3,16,128]{3,2,1,0:T(8,128)} %get-tuple-element.15.pay_ref), channel_id=1, source_target_pairs={{0,8},{4,12},{8,16},{12,20},{16,24},{20,28},{24,0},{28,4},{1,9},{5... | collective-permute-start | bytes 147464 | tf_op jit(solution)/shard_map/ppermute | solution.py:118
  23.9 11.6 %collective-permute-start.6 = (f32[2,3,16,128]{3,2,1,0:T(8,128)}, f32[2,3,16,128]{3,2,1,0:T(8,128)S(1)}, u32[]{:S(2)}, u32[]{:S(2)}) collective-permute-start(f32[2,3,16,128]{3,2,1,0:T(8,128)} %get-tuple-element.15.pay_ref), channel_id=1, source_target_pairs={{0,12},{4,16},{8,20},{12,24},{16,28},{20,0},{24,4},{28,8},{1,13},{... | collective-permute-start | bytes 147464 | tf_op jit(solution)/shard_map/ppermute | solution.py:118
  26.4 9.2 %collective-permute-start.7 = (f32[2,3,16,128]{3,2,1,0:T(8,128)}, f32[2,3,16,128]{3,2,1,0:T(8,128)S(1)}, u32[]{:S(2)}, u32[]{:S(2)}) collective-permute-start(f32[2,3,16,128]{3,2,1,0:T(8,128)} %get-tuple-element.15.pay_ref), channel_id=1, source_target_pairs={{0,16},{4,20},{8,24},{12,28},{16,0},{20,4},{24,8},{28,12},{1,17},{... | collective-permute-start | bytes 147464 | tf_op jit(solution)/shard_map/ppermute | solution.py:118
  29.2 6.3 %collective-permute-start.8 = (f32[2,3,16,128]{3,2,1,0:T(8,128)}, f32[2,3,16,128]{3,2,1,0:T(8,128)S(1)}, u32[]{:S(2)}, u32[]{:S(2)}) collective-permute-start(f32[2,3,16,128]{3,2,1,0:T(8,128)} %get-tuple-element.15.pay_ref), channel_id=1, source_target_pairs={{0,20},{4,24},{8,28},{12,0},{16,4},{20,8},{24,12},{28,16},{1,21},{... | collective-permute-start | bytes 147464 | tf_op jit(solution)/shard_map/ppermute | solution.py:118
  30.9 4.7 %collective-permute-start.9 = (f32[2,3,16,128]{3,2,1,0:T(8,128)}, f32[2,3,16,128]{3,2,1,0:T(8,128)S(1)}, u32[]{:S(2)}, u32[]{:S(2)}) collective-permute-start(f32[2,3,16,128]{3,2,1,0:T(8,128)} %get-tuple-element.15.pay_ref), channel_id=1, source_target_pairs={{0,24},{4,28},{8,0},{12,4},{16,8},{20,12},{24,16},{28,20},{1,25},{... | collective-permute-start | bytes 147464 | tf_op jit(solution)/shard_map/ppermute | solution.py:118
  39.7 4.4 %collective-permute-start.11 = (f32[4,16,128]{2,1,0:T(8,128)}, f32[4,16,128]{2,1,0:T(8,128)S(1)}, u32[]{:S(2)}, u32[]{:S(2)}) collective-permute-start(f32[4,16,128]{2,1,0:T(8,128)} %get-tuple-element.17), channel_id=1, source_target_pairs={{0,1},{1,2},{2,3},{3,0},{4,5},{5,6},{6,7},{7,4},{8,9},{9,10},{10,1... | collective-permute-start | bytes 98312 | tf_op jit(solution)/shard_map/ppermute | solution.py:178
  41.0 4.1 %collective-permute-start.12 = (f32[4,16,128]{2,1,0:T(8,128)}, f32[4,16,128]{2,1,0:T(8,128)S(1)}, u32[]{:S(2)}, u32[]{:S(2)}) collective-permute-start(f32[4,16,128]{2,1,0:T(8,128)} %get-tuple-element.17), channel_id=1, source_target_pairs={{0,2},{1,3},{2,0},{3,1},{4,6},{5,7},{6,4},{7,5},{8,10},{9,11},{10,... | collective-permute-start | bytes 98312 | tf_op jit(solution)/shard_map/ppermute | solution.py:178
  42.6 3.4 %collective-permute-start.13 = (f32[4,16,128]{2,1,0:T(8,128)}, f32[4,16,128]{2,1,0:T(8,128)S(1)}, u32[]{:S(2)}, u32[]{:S(2)}) collective-permute-start(f32[4,16,128]{2,1,0:T(8,128)} %get-tuple-element.17), channel_id=1, source_target_pairs={{0,3},{1,0},{2,1},{3,2},{4,7},{5,4},{6,5},{7,6},{8,11},{9,8},{10,9... | collective-permute-start | bytes 98312 | tf_op jit(solution)/shard_map/ppermute | solution.py:178
  44.1 1.9 %copy-start.4 = (f32[4,16,128]{2,1,0:T(8,128)S(1)}, f32[4,16,128]{2,1,0:T(8,128)}, u32[]{:S(2)}) copy-start(f32[4,16,128]{2,1,0:T(8,128)} %get-tuple-element.17) | copy-start | bytes 98308

commit v3 on v2

--- a/solution.py
+++ b/solution.py
@@ -1,4 +1,3 @@
-import functools
 import jax
 import jax.numpy as jnp
 from jax import lax
@@ -23,18 +22,28 @@
     return jax.ShapeDtypeStruct(shape, jnp.float32)
 
 
-def edges_kernel(adj_ref, base_ref, xlo_ref, xhi_ref, ylo_ref, yhi_ref):
+ANY = pl.BlockSpec(memory_space=pl.ANY)
+SMEM = pl.BlockSpec(memory_space=pltpu.SMEM)
+
+
+def edges_kernel(adj_ref, base_ref, xlo_ref, xhi_ref, ylo_ref, yhi_ref, sems):
     n, ny = adj_ref.shape[1], adj_ref.shape[2]
-    for k in range(6):
-        ref, c = (adj_ref, k) if k < 3 else (base_ref, k - 3)
-        xlo_ref[k] = ref[c, 0]
-        xhi_ref[k] = ref[c, n - 1]
-        for x in range(n):
-            ylo_ref[k, x : x + 1, :] = ref[c, x, 0:1, :]
-            yhi_ref[k, x : x + 1, :] = ref[c, x, ny - 1 : ny, :]
-
-
-def sweep_kernel(adj_ref, base_ref, xlo_ref, xhi_ref, ylo_ref, yhi_ref, coef_ref, sw_ref, pay_ref):
+    copies = []
+    for s, src in enumerate((adj_ref, base_ref)):
+        dst = pl.ds(3 * s, 3)
+        copies += [
+            pltpu.make_async_copy(src.at[:, 0], xlo_ref.at[dst], sems.at[4 * s]),
+            pltpu.make_async_copy(src.at[:, n - 1], xhi_ref.at[dst], sems.at[4 * s + 1]),
+            pltpu.make_async_copy(src.at[:, :, 0], ylo_ref.at[dst], sems.at[4 * s + 2]),
+            pltpu.make_async_copy(src.at[:, :, ny - 1], yhi_ref.at[dst], sems.at[4 * s + 3]),
+        ]
+    for cp in copies:
+        cp.start()
+    for cp in copies:
+        cp.wait()
+
+
+def sweep_kernel(G, direct, idx_ref, adj_ref, base_ref, xlo_ref, xhi_ref, ylo_ref, yhi_ref, coef_ref, sw_ref, own_ref, *send_refs):
     n, ny, nz = adj_ref.shape[1], adj_ref.shape[2], adj_ref.shape[3]
     metric = coef_ref[0]
     decay = coef_ref[1]
@@ -76,23 +85,47 @@
             f = sw_ref[c, x]
             back[c] = f if x == n - 1 else f + decay * back[c]
             sw_ref[c, x] = back[c]
+    i = idx_ref[0]
     for c in range(3):
-        pay_ref[0, c] = forward[c]
-        pay_ref[1, c] = back[c] + gain * forward[c]
-
-
-def finish_kernel(adj_ref, sw_ref, pay_ref, inflow_ref, rest_ref, coef_ref, out_ref, part_ref):
+        carry_up = forward[c]
+        carry_down = back[c] + gain * forward[c]
+        own_ref[0, c] = carry_up
+        own_ref[1, c] = carry_down
+        if direct:
+            for k in range(1, G):
+                send_refs[k - 1][c] = jnp.where(i + k < G, carry_up, carry_down)
+
+
+def finish_kernel(G, direct, idx_ref, adj_ref, sw_ref, own_ref, coef_ref, *rest):
     n, ny = adj_ref.shape[1], adj_ref.shape[2]
-    rate = coef_ref[0]
+    out_ref, part_ref = rest[-2], rest[-1]
+    got = rest[:-2]
+    rate = coef_ref[3]
     decay = coef_ref[1]
-    shrink = coef_ref[2]
-    inverse = coef_ref[3]
-    low_w = coef_ref[4]
-    high_w = coef_ref[5]
-    near = coef_ref[6]
-    ratio = coef_ref[7]
-    ret = [rest_ref[c] + near * (pay_ref[0, c] + ratio * inflow_ref[c]) for c in range(3)]
-    inflow = [inflow_ref[c] for c in range(3)]
+    shrink = coef_ref[4]
+    inverse = coef_ref[5]
+    low_w = coef_ref[6]
+    high_w = coef_ref[7]
+    near = coef_ref[8]
+    ratio = coef_ref[9]
+    block_rate = n * rate
+    i = idx_ref[0]
+    inflow, later = [], []
+    for c in range(3):
+        if direct:
+            a = jnp.zeros_like(rate)
+            b = jnp.zeros_like(rate)
+            for k in range(1, G):
+                upstream = i >= k
+                power = jnp.where(upstream, k - 1, G - k - 1).astype(jnp.float32)
+                term = jnp.exp(-power * block_rate) * got[k - 1][c]
+                a = a + jnp.where(upstream, term, 0.0)
+                b = b + jnp.where(upstream, 0.0, term)
+        else:
+            a = got[0][c]
+            b = got[1][c]
+        inflow.append(a)
+        later.append(b + near * (own_ref[0, c] + ratio * a))
     back_lead = None
     for x in range(n - 1, -1, -1):
         lead = jnp.exp(-(x + 1.0) * rate)
@@ -100,7 +133,7 @@
         tail = jnp.exp(-(n - x) * rate)
         vals = []
         for c in range(3):
-            v = adj_ref[c, x] + shrink * (sw_ref[c, x] + back_lead * inflow[c] + tail * ret[c])
+            v = adj_ref[c, x] + shrink * (sw_ref[c, x] + back_lead * inflow[c] + tail * later[c])
             out_ref[c, x] = v
             vals.append(v)
         part_ref[0, x : x + 1, :] = (low_w * vals[1])[0:1, :]
@@ -109,37 +142,32 @@
     part_ref[3] = jnp.broadcast_to(jnp.sum(inverse, axis=0, keepdims=True), part_ref.shape[1:])
 
 
-def gx_carries(L, U, A, G, i):
-    if G <= DIRECT_LIMIT:
-        payload = jnp.stack([L, U])
-        inflow = jnp.zeros_like(L)
-        ret = jnp.zeros_like(U)
-        for k in range(1, G):
-            got = lax.ppermute(payload, "gx", [(j, (j + k) % G) for j in range(G)])
-            upstream = i >= k
-            inflow = inflow + jnp.where(upstream, A ** (k - 1) * got[0], 0.0)
-            ret = ret + jnp.where(upstream, 0.0, A ** (G - k - 1) * got[1])
-        return inflow, ret
+def scan_carries(L, U, A, G):
     inflow = shift(L, "gx", G, 1)
-    ret = shift(U, "gx", G, -1)
+    later = shift(U, "gx", G, -1)
     step = 1
     ratio = A
     while step < G:
         inflow = inflow + ratio * shift(inflow, "gx", G, step)
-        ret = ret + ratio * shift(ret, "gx", G, -step)
+        later = later + ratio * shift(later, "gx", G, -step)
         ratio = ratio * ratio
         step *= 2
-    return inflow, ret
+    return inflow, later
 
 
 def local(adjoint, base_flow, metric, smoothing):
     G, i = lax.axis_size("gx"), lax.axis_index("gx")
     Gy, g = lax.axis_size("gy"), lax.axis_index("gy")
     _, n, ny, nz = adjoint.shape
+    direct = G <= DIRECT_LIMIT
+    idx = jnp.reshape(i, (1,)).astype(jnp.int32)
 
     xlo, xhi, ylo, yhi = pl.pallas_call(
         edges_kernel,
         out_shape=(f32((6, ny, nz)), f32((6, ny, nz)), f32((6, n, nz)), f32((6, n, nz))),
+        in_specs=[ANY, ANY],
+        out_specs=(ANY, ANY, ANY, ANY),
+        scratch_shapes=[pltpu.SemaphoreType.DMA((8,))],
     )(adjoint, base_flow)
     x_before = shift(xhi, "gx", G, 1)
     x_after = shift(xlo, "gx", G, -1)
@@ -153,26 +181,32 @@
     two_block = jnp.expm1(-2.0 * n * rate)
     downstream = (G - 1 - i).astype(jnp.float32)
     geo_here = jnp.expm1(-2.0 * n * downstream * rate) / two_block
-
-    def rows(*vs):
-        return jnp.broadcast_to(jnp.stack(vs)[:, :, None], (len(vs), ny, nz))
-
-    coef_a = rows(metric, decay, c * A * geo_here)
-    sw, payload = pl.pallas_call(
-        sweep_kernel,
-        out_shape=(f32(adjoint.shape), f32((2, 3, ny, nz))),
-    )(adjoint, base_flow, x_before, x_after, y_before, y_after, coef_a)
-
-    A3 = A[None, :, None]
-    inflow, rest = gx_carries(payload[0], payload[1], A3, G, i)
-
     low_w = jnp.where(g == 0, 2.0 * metric[0], 0.0) + jnp.zeros_like(metric)
     high_w = jnp.where(g == Gy - 1, -2.0 * metric[-1], 0.0) + jnp.zeros_like(metric)
-    coef_b = rows(rate, decay, jnp.expm1(-rate) ** 2, 1.0 / metric, low_w, high_w, c * geo_here, A)
+    vs = (metric, decay, c * A * geo_here, rate, jnp.expm1(-rate) ** 2, 1.0 / metric, low_w, high_w, c * geo_here, A)
+    coef = jnp.broadcast_to(jnp.stack(vs)[:, :, None], (len(vs), ny, nz))
+
+    plane = f32((3, ny, nz))
+    sends = G - 1 if direct else 0
+    outs = pl.pallas_call(
+        lambda *r: sweep_kernel(G, direct, *r),
+        out_shape=(f32(adjoint.shape), f32((2, 3, ny, nz))) + (plane,) * sends,
+        in_specs=[SMEM] + [pl.BlockSpec(memory_space=pltpu.VMEM)] * 7,
+    )(idx, adjoint, base_flow, x_before, x_after, y_before, y_after, coef)
+    sw, own = outs[0], outs[1]
+
+    if direct:
+        got = [
+            lax.ppermute(outs[1 + k], "gx", [(j, (j + k) % G) for j in range(G)]) for k in range(1, G)
+        ]
+    else:
+        got = list(scan_carries(own[0], own[1], A[None, :, None], G))
+
     adjoint_next, part = pl.pallas_call(
-        finish_kernel,
+        lambda *r: finish_kernel(G, direct, *r),
         out_shape=(f32(adjoint.shape), f32((4, n, nz))),
-    )(adjoint, sw, payload, inflow, rest, coef_b)
+        in_specs=[SMEM] + [pl.BlockSpec(memory_space=pltpu.VMEM)] * (4 + len(got)),
+    )(idx, adjoint, sw, own, coef, *got)
 
     pieces = [part] + [
         lax.ppermute(part, "gy", [(j, (j + k) % Gy) for j in range(Gy)]) for k in range(1, Gy)

time: 47 us -> 51.5 us (1.096)
  Pallas kernels: 6.36 us -> 11.9 us
  other arithmetic: 2.19 us -> 0.78 us
  waiting for transfers between devices: 6.69 us -> 5.61 us
  starting transfers between devices: 26.7 us -> 27.7 us
    pallas_call x1, Pallas kernels: 1.83 us -> 7.13 us  [local(): pl.pallas_call(edges_kernel, out_shape=(f32((6, ny, nz)), f32((6, ny, nz)...]
    ppermute x4, waiting for transfers between devices: 2.75 us -> 0.8 us  [shift(): return lax.ppermute(x, axis, pairs)]
    add x2 -> x0, other arithmetic: 1.39 us -> none  [the longest x1 0.71 us: gx_carries(): ret = ret + jnp.where(upstream, 0.0, A ** (G - k - 1) * got[1])]
    ppermute x7, waiting for transfers between devices: 2.02 us -> 2.9 us  [local(): lax.ppermute(outs[1 + k], 'gx', [(j, (j + k) % G) for j in range(G)])]
    ppermute x3, starting transfers between devices: 4.42 us -> 5.16 us  [local(): lax.ppermute(part, 'gy', [(j, (j + k) % Gy) for j in range(Gy)])]
    broadcast_in_dim x2 -> x1, local copies, waits for them, and re-layouts: 1.39 us -> 0.73 us  [local(): coef = jnp.broadcast_to(jnp.stack(vs)[:, :, None], (len(vs), ny, nz))]
    unnamed x14 -> x28, local copies, waits for them, and re-layouts: 0.68 us -> 1.24 us
where the time goes in v3:
time: 51.5 us; the launch traced here: 50.8 us
  starting transfers between devices  27.7 us (54%)
  Pallas kernels  11.9 us (23%)
  waiting for transfers between devices  5.61 us (11%)
  local copies, waits for them, and re-layouts  2.64 us (5%)
  between operations  2.14 us (4%)
  other arithmetic  0.78 us (2%)
    ppermute x7, starting transfers between devices, local(): lax.ppermute(outs[1 + k], 'gx', [(j, (j + k) % G) for j in range(G)])  13.6 us
    ppermute x4, starting transfers between devices, shift(): return lax.ppermute(x, axis, pairs)  8.92 us
    pallas_call x1, Pallas kernels, local(): pl.pallas_call(edges_kernel, out_shape=(f32((6, ny, nz)), f32((6, ny, nz)...  7.13 us
    ppermute x3, starting transfers between devices, local(): lax.ppermute(part, 'gy', [(j, (j + k) % Gy) for j in range(Gy)])  5.16 us
    ppermute x7, waiting for transfers between devices, local(): lax.ppermute(outs[1 + k], 'gx', [(j, (j + k) % G) for j in range(G)])  2.9 us
    pallas_call x1, Pallas kernels, local(): pl.pallas_call(lambda *r: sweep_kernel(G, direct, *r), out_shape=(f32(adj...  2.66 us
    pallas_call x1, Pallas kernels, local(): pl.pallas_call(lambda *r: finish_kernel(G, direct, *r), out_shape=(f32(ad...  2.13 us
    ppermute x3, waiting for transfers between devices, local(): lax.ppermute(part, 'gy', [(j, (j + k) % Gy) for j in range(Gy)])  1.91 us
  transfers between devices with their start and end apart: 14, of which 6 were waited for; matrix products, arithmetic and copies ran while one was open for 2% of the time, Pallas kernels for 0%

profile of v3, /device:TPU:0, one launch (start us, length us, event | category | flops | bytes accessed | tf_op | source)
XLA Modules:
  0.0 50.8 jit_solution(9922142962627137691)
XLA Ops:
  0.6 7.1 %shard_map.59 = (f32[6,16,128]{2,1,0:T(8,128)}, f32[6,16,128]{2,1,0:T(8,128)}, f32[6,16,128]{2,1,0:T(8,128)}, f32[6,16,128]{2,1,0:T(8,128)}) custom-call(f32[3,16,16,128]{3,2,1,0:T(8,128)} %r_1_.3, f32[3,16,16,128]{3,2,1,0:T(8,128)} %r_2_.1), custom_call_target="tpu_custom_call" | custom-call | tf_op jit(solution)/shard_map/pallas_call | solution.py:165
  7.8 4.9 %collective-permute-start = (f32[6,16,128]{2,1,0:T(8,128)}, f32[6,16,128]{2,1,0:T(8,128)S(1)}, u32[]{:S(2)}, u32[]{:S(2)}) collective-permute-start(f32[6,16,128]{2,1,0:T(8,128)} %get-tuple-element.17), channel_id=1, source_target_pairs={{0,4},{4,8},{8,12},{12,16},{16,20},{20,24},{24,28},{1,5},{5,9},{9,... | collective-permute-start | bytes 147464 | tf_op jit(solution)/shard_map/ppermute | solution.py:18
  12.7 1.3 %collective-permute-start.1 = (f32[6,16,128]{2,1,0:T(8,128)}, f32[6,16,128]{2,1,0:T(8,128)S(1)}, u32[]{:S(2)}, u32[]{:S(2)}) collective-permute-start(f32[6,16,128]{2,1,0:T(8,128)} %get-tuple-element.18), channel_id=1, source_target_pairs={{4,0},{8,4},{12,8},{16,12},{20,16},{24,20},{28,24},{5,1},{9,5},{13... | collective-permute-start | bytes 147464 | tf_op jit(solution)/shard_map/ppermute | solution.py:18
  14.0 1.5 %collective-permute-start.2 = (f32[6,16,128]{2,1,0:T(8,128)}, f32[6,16,128]{2,1,0:T(8,128)S(1)}, u32[]{:S(2)}, u32[]{:S(2)}) collective-permute-start(f32[6,16,128]{2,1,0:T(8,128)} %get-tuple-element.19), channel_id=1, source_target_pairs={{0,1},{1,2},{2,3},{4,5},{5,6},{6,7},{8,9},{9,10},{10,11},{12,13},{... | collective-permute-start | bytes 147464 | tf_op jit(solution)/shard_map/ppermute | solution.py:18
  15.4 1.3 %collective-permute-start.3 = (f32[6,16,128]{2,1,0:T(8,128)}, f32[6,16,128]{2,1,0:T(8,128)S(1)}, u32[]{:S(2)}, u32[]{:S(2)}) collective-permute-start(f32[6,16,128]{2,1,0:T(8,128)} %get-tuple-element.20), channel_id=1, source_target_pairs={{1,0},{2,1},{3,2},{5,4},{6,5},{7,6},{9,8},{10,9},{11,10},{13,12},{... | collective-permute-start | bytes 147464 | tf_op jit(solution)/shard_map/ppermute | solution.py:18
  16.9 0.6 %copy-done.12 = f32[16]{0:T(128)S(1)} copy-done((f32[16]{0:T(128)S(1)}, f32[16]{0:T(128)}, u32[]{:S(2)}) %copy-start.12) | copy-done | bytes 88
  17.5 0.6 %fusion.3 = (f32[1]{0:T(128)}, f32[1]{0:T(128)}) fusion(f32[16]{0:T(128)S(1)} %copy-done.12), kind=kLoop, calls=%fused_computation.17 | loop fusion | bytes 16 | tf_op jit(solution)/shard_map/slice | solution.py:185
  19.6 0.8 %collective-permute-done.3.r_6_ = f32[6,16,128]{2,1,0:T(8,128)S(1)} collective-permute-done((f32[6,16,128]{2,1,0:T(8,128)}, f32[6,16,128]{2,1,0:T(8,128)S(1)}, u32[]{:S(2)}, u32[]{:S(2)}) %collective-permute-start.3) | collective-permute-done | bytes 49184 | tf_op jit(solution)/shard_map/ppermute | solution.py:18
  20.4 0.7 %broadcast_in_dim.5.r_7_.r_4_ = f32[10,16,128]{2,1,0:T(8,128)} broadcast(f32[10,16]{1,0:T(8,128)S(1)} %stack.55), dimensions={0,1} | broadcast | bytes 82560 | tf_op jit(solution)/shard_map/broadcast_in_dim | solution.py:187
  21.1 2.7 %shard_map.60 = (f32[3,16,16,128]{3,2,1,0:T(8,128)}, f32[2,3,16,128]{3,2,1,0:T(8,128)}, f32[3,16,128]{2,1,0:T(8,128)}, f32[3,16,128]{2,1,0:T(8,128)}, f32[3,16,1...) custom-call(s32[1]{0:T(128)} %bitcast.r_0_, ...), custom_call_target="tpu_custom_call" | custom-call | tf_op jit(solution)/shard_map/pallas_call | solution.py:191
  23.8 5.7 %collective-permute-start.10 = (f32[3,16,128]{2,1,0:T(8,128)}, f32[3,16,128]{2,1,0:T(8,128)S(1)}, u32[]{:S(2)}, u32[]{:S(2)}) collective-permute-start(f32[3,16,128]{2,1,0:T(8,128)} %get-tuple-element.29), channel_id=1, source_target_pairs={{0,28},{4,0},{8,4},{12,8},{16,12},{20,16},{24,20},{28,24},{1,29},{... | collective-permute-start | bytes 73736 | tf_op jit(solution)/shard_map/ppermute | solution.py:200
  29.4 2.5 %collective-permute-start.6 = (f32[3,16,128]{2,1,0:T(8,128)}, f32[3,16,128]{2,1,0:T(8,128)S(1)}, u32[]{:S(2)}, u32[]{:S(2)}) collective-permute-start(f32[3,16,128]{2,1,0:T(8,128)} %get-tuple-element.25), channel_id=1, source_target_pairs={{0,12},{4,16},{8,20},{12,24},{16,28},{20,0},{24,4},{28,8},{1,13},{... | collective-permute-start | bytes 73736 | tf_op jit(solution)/shard_map/ppermute | solution.py:200
  31.9 2.8 %collective-permute-start.7 = (f32[3,16,128]{2,1,0:T(8,128)}, f32[3,16,128]{2,1,0:T(8,128)S(1)}, u32[]{:S(2)}, u32[]{:S(2)}) collective-permute-start(f32[3,16,128]{2,1,0:T(8,128)} %get-tuple-element.26), channel_id=1, source_target_pairs={{0,16},{4,20},{8,24},{12,28},{16,0},{20,4},{24,8},{28,12},{1,17},{... | collective-permute-start | bytes 73736 | tf_op jit(solution)/shard_map/ppermute | solution.py:200
  34.7 1.1 %collective-permute-start.8 = (f32[3,16,128]{2,1,0:T(8,128)}, f32[3,16,128]{2,1,0:T(8,128)S(1)}, u32[]{:S(2)}, u32[]{:S(2)}) collective-permute-start(f32[3,16,128]{2,1,0:T(8,128)} %get-tuple-element.27), channel_id=1, source_target_pairs={{0,20},{4,24},{8,28},{12,0},{16,4},{20,8},{24,12},{28,16},{1,21},{... | collective-permute-start | bytes 73736 | tf_op jit(solution)/shard_map/ppermute | solution.py:200
  36.2 1.6 %collective-permute-start.9 = (f32[3,16,128]{2,1,0:T(8,128)}, f32[3,16,128]{2,1,0:T(8,128)S(1)}, u32[]{:S(2)}, u32[]{:S(2)}) collective-permute-start(f32[3,16,128]{2,1,0:T(8,128)} %get-tuple-element.28), channel_id=1, source_target_pairs={{0,24},{4,28},{8,0},{12,4},{16,8},{20,12},{24,16},{28,20},{1,25},{... | collective-permute-start | bytes 73736 | tf_op jit(solution)/shard_map/ppermute | solution.py:200
  37.8 1.9 %collective-permute-done.8.r_9_ = f32[3,16,128]{2,1,0:T(8,128)S(1)} collective-permute-done((f32[3,16,128]{2,1,0:T(8,128)}, f32[3,16,128]{2,1,0:T(8,128)S(1)}, u32[]{:S(2)}, u32[]{:S(2)}) %collective-permute-start.8) | collective-permute-done | bytes 24608 | tf_op jit(solution)/shard_map/ppermute | solution.py:200
  39.7 0.7 %collective-permute-done.9.r_10_ = f32[3,16,128]{2,1,0:T(8,128)S(1)} collective-permute-done((f32[3,16,128]{2,1,0:T(8,128)}, f32[3,16,128]{2,1,0:T(8,128)S(1)}, u32[]{:S(2)}, u32[]{:S(2)}) %collective-permute-start.9) | collective-permute-done | bytes 24608 | tf_op jit(solution)/shard_map/ppermute | solution.py:200
  40.4 0.6 %copy-done.11 = f32[3,16,128]{2,1,0:T(8,128)} copy-done((f32[3,16,128]{2,1,0:T(8,128)}, f32[3,16,128]{2,1,0:T(8,128)S(1)}, u32[]{:S(2)}) %copy-start.11) | copy-done | bytes 24600
  40.9 2.1 %shard_map.61 = (f32[3,16,16,128]{3,2,1,0:T(8,128)}, f32[4,16,128]{2,1,0:T(8,128)}) custom-call(s32[1]{0:T(128)} %bitcast.r_0_, f32[3,16,16,128]{3,2,1,0:T(8,128)} %r_1_.3, f32[3,16,16,128]{3,2,1,0:T(8,128)} %get-tuple-element.21.r_2_, f32[2,3,16,128]{3,2,1,0:T(8,128)} %get-tuple-element.22.r_3_, f32[10,16,128]{2,1,0:T(8,128)} %broadcast_in_dim.5.r_7_.r_4_, ...), custom_call_target="tpu_custom_call" | custom-call | tf_op jit(solution)/shard_map/pallas_call | solution.py:205
  43.2 3.6 %collective-permute-start.12 = (f32[4,16,128]{2,1,0:T(8,128)}, f32[4,16,128]{2,1,0:T(8,128)S(1)}, u32[]{:S(2)}, u32[]{:S(2)}) collective-permute-start(f32[4,16,128]{2,1,0:T(8,128)} %get-tuple-element.31), channel_id=1, source_target_pairs={{0,2},{1,3},{2,0},{3,1},{4,6},{5,7},{6,4},{7,5},{8,10},{9,11},{10,... | collective-permute-start | bytes 98312 | tf_op jit(solution)/shard_map/ppermute | solution.py:212
  46.8 1.4 %collective-permute-start.13 = (f32[4,16,128]{2,1,0:T(8,128)}, f32[4,16,128]{2,1,0:T(8,128)S(1)}, u32[]{:S(2)}, u32[]{:S(2)}) collective-permute-start(f32[4,16,128]{2,1,0:T(8,128)} %get-tuple-element.31), channel_id=1, source_target_pairs={{0,3},{1,0},{2,1},{3,2},{4,7},{5,4},{6,5},{7,6},{8,11},{9,8},{10,9... | collective-permute-start | bytes 98312 | tf_op jit(solution)/shard_map/ppermute | solution.py:212
  48.2 0.7 %collective-permute-done.12 = f32[4,16,128]{2,1,0:T(8,128)S(1)} collective-permute-done((f32[4,16,128]{2,1,0:T(8,128)}, f32[4,16,128]{2,1,0:T(8,128)S(1)}, u32[]{:S(2)}, u32[]{:S(2)}) %collective-permute-start.12) | collective-permute-done | bytes 32800 | tf_op jit(solution)/shard_map/ppermute | solution.py:212
  48.9 1.2 %collective-permute-done.13 = f32[4,16,128]{2,1,0:T(8,128)S(1)} collective-permute-done((f32[4,16,128]{2,1,0:T(8,128)}, f32[4,16,128]{2,1,0:T(8,128)S(1)}, u32[]{:S(2)}, u32[]{:S(2)}) %collective-permute-start.13) | collective-permute-done | bytes 32800 | tf_op jit(solution)/shard_map/ppermute | solution.py:212
  50.2 0.6 %fusion = f32[2,16,128]{2,1,0:T(8,128)} fusion(f32[1,4,16,128]{3,2,1,0:T(8,128)S(1)} %dynamic-slice_add_fusion, f32[16,128]{1,0:T(8,128)S(1)} %fusion.1), kind=kLoop, calls=%fused_computation.3 | loop fusion | flops 4096 | bytes 40960 | tf_op jit(solution)/shard_map/add | solution.py:220
  (49 shorter events, 0.8 us)
Async XLA Ops:
  7.8 11.7 %collective-permute-start = (f32[6,16,128]{2,1,0:T(8,128)}, f32[6,16,128]{2,1,0:T(8,128)S(1)}, u32[]{:S(2)}, u32[]{:S(2)}) collective-permute-start(f32[6,16,128]{2,1,0:T(8,128)} %get-tuple-element.17), channel_id=1, source_target_pairs={{0,4},{4,8},{8,12},{12,16},{16,20},{20,24},{24,28},{1,5},{5,9},{9,... | collective-permute-start | bytes 147464 | tf_op jit(solution)/shard_map/ppermute | solution.py:18
  12.7 6.9 %collective-permute-start.1 = (f32[6,16,128]{2,1,0:T(8,128)}, f32[6,16,128]{2,1,0:T(8,128)S(1)}, u32[]{:S(2)}, u32[]{:S(2)}) collective-permute-start(f32[6,16,128]{2,1,0:T(8,128)} %get-tuple-element.18), channel_id=1, source_target_pairs={{4,0},{8,4},{12,8},{16,12},{20,16},{24,20},{28,24},{5,1},{9,5},{13... | collective-permute-start | bytes 147464 | tf_op jit(solution)/shard_map/ppermute | solution.py:18
  14.0 5.6 %collective-permute-start.2 = (f32[6,16,128]{2,1,0:T(8,128)}, f32[6,16,128]{2,1,0:T(8,128)S(1)}, u32[]{:S(2)}, u32[]{:S(2)}) collective-permute-start(f32[6,16,128]{2,1,0:T(8,128)} %get-tuple-element.19), channel_id=1, source_target_pairs={{0,1},{1,2},{2,3},{4,5},{5,6},{6,7},{8,9},{9,10},{10,11},{12,13},{... | collective-permute-start | bytes 147464 | tf_op jit(solution)/shard_map/ppermute | solution.py:18
  15.4 1.3 %copy-start.13 = (f32[16]{0:T(128)S(1)}, f32[16]{0:T(128)}, u32[]{:S(2)}) copy-start(f32[16]{0:T(128)} %param.7) | copy-start | bytes 196
  15.4 4.9 %collective-permute-start.3 = (f32[6,16,128]{2,1,0:T(8,128)}, f32[6,16,128]{2,1,0:T(8,128)S(1)}, u32[]{:S(2)}, u32[]{:S(2)}) collective-permute-start(f32[6,16,128]{2,1,0:T(8,128)} %get-tuple-element.20), channel_id=1, source_target_pairs={{1,0},{2,1},{3,2},{5,4},{6,5},{7,6},{9,8},{10,9},{11,10},{13,12},{... | collective-permute-start | bytes 147464 | tf_op jit(solution)/shard_map/ppermute | solution.py:18
  19.5 1.6 %copy-start = (f32[6,16,128]{2,1,0:T(8,128)}, f32[6,16,128]{2,1,0:T(8,128)S(1)}, u32[]{:S(2)}) copy-start(f32[6,16,128]{2,1,0:T(8,128)S(1)} %collective-permute-done.r_3_) | copy-start | bytes 147460
  19.5 1.6 %copy-start.1 = (f32[6,16,128]{2,1,0:T(8,128)}, f32[6,16,128]{2,1,0:T(8,128)S(1)}, u32[]{:S(2)}) copy-start(f32[6,16,128]{2,1,0:T(8,128)S(1)} %collective-permute-done.1.r_4_) | copy-start | bytes 147460
  19.5 1.5 %copy-start.2 = (f32[6,16,128]{2,1,0:T(8,128)}, f32[6,16,128]{2,1,0:T(8,128)S(1)}, u32[]{:S(2)}) copy-start(f32[6,16,128]{2,1,0:T(8,128)S(1)} %collective-permute-done.2.r_5_) | copy-start | bytes 147460
  23.8 11.0 %collective-permute-start.10 = (f32[3,16,128]{2,1,0:T(8,128)}, f32[3,16,128]{2,1,0:T(8,128)S(1)}, u32[]{:S(2)}, u32[]{:S(2)}) collective-permute-start(f32[3,16,128]{2,1,0:T(8,128)} %get-tuple-element.29), channel_id=1, source_target_pairs={{0,28},{4,0},{8,4},{12,8},{16,12},{20,16},{24,20},{28,24},{1,29},{... | collective-permute-start | bytes 73736 | tf_op jit(solution)/shard_map/ppermute | solution.py:200
  29.4 6.7 %collective-permute-start.4 = (f32[3,16,128]{2,1,0:T(8,128)}, f32[3,16,128]{2,1,0:T(8,128)S(1)}, u32[]{:S(2)}, u32[]{:S(2)}) collective-permute-start(f32[3,16,128]{2,1,0:T(8,128)} %get-tuple-element.23), channel_id=1, source_target_pairs={{0,4},{4,8},{8,12},{12,16},{16,20},{20,24},{24,28},{28,0},{1,5},{5... | collective-permute-start | bytes 73736 | tf_op jit(solution)/shard_map/ppermute | solution.py:200
  29.4 8.3 %collective-permute-start.5 = (f32[3,16,128]{2,1,0:T(8,128)}, f32[3,16,128]{2,1,0:T(8,128)S(1)}, u32[]{:S(2)}, u32[]{:S(2)}) collective-permute-start(f32[3,16,128]{2,1,0:T(8,128)} %get-tuple-element.24), channel_id=1, source_target_pairs={{0,8},{4,12},{8,16},{12,20},{16,24},{20,28},{24,0},{28,4},{1,9},{5... | collective-permute-start | bytes 73736 | tf_op jit(solution)/shard_map/ppermute | solution.py:200
  29.4 8.3 %collective-permute-start.6 = (f32[3,16,128]{2,1,0:T(8,128)}, f32[3,16,128]{2,1,0:T(8,128)S(1)}, u32[]{:S(2)}, u32[]{:S(2)}) collective-permute-start(f32[3,16,128]{2,1,0:T(8,128)} %get-tuple-element.25), channel_id=1, source_target_pairs={{0,12},{4,16},{8,20},{12,24},{16,28},{20,0},{24,4},{28,8},{1,13},{... | collective-permute-start | bytes 73736 | tf_op jit(solution)/shard_map/ppermute | solution.py:200
  31.9 5.8 %collective-permute-start.7 = (f32[3,16,128]{2,1,0:T(8,128)}, f32[3,16,128]{2,1,0:T(8,128)S(1)}, u32[]{:S(2)}, u32[]{:S(2)}) collective-permute-start(f32[3,16,128]{2,1,0:T(8,128)} %get-tuple-element.26), channel_id=1, source_target_pairs={{0,16},{4,20},{8,24},{12,28},{16,0},{20,4},{24,8},{28,12},{1,17},{... | collective-permute-start | bytes 73736 | tf_op jit(solution)/shard_map/ppermute | solution.py:200
  34.7 5.6 %copy-start.5 = (f32[3,16,128]{2,1,0:T(8,128)}, f32[3,16,128]{2,1,0:T(8,128)S(1)}, u32[]{:S(2)}) copy-start(f32[3,16,128]{2,1,0:T(8,128)S(1)} %collective-permute-done.10.r_11_) | copy-start | bytes 73732
  34.7 4.9 %collective-permute-start.8 = (f32[3,16,128]{2,1,0:T(8,128)}, f32[3,16,128]{2,1,0:T(8,128)S(1)}, u32[]{:S(2)}, u32[]{:S(2)}) collective-permute-start(f32[3,16,128]{2,1,0:T(8,128)} %get-tuple-element.27), channel_id=1, source_target_pairs={{0,20},{4,24},{8,28},{12,0},{16,4},{20,8},{24,12},{28,16},{1,21},{... | collective-permute-start | bytes 73736 | tf_op jit(solution)/shard_map/ppermute | solution.py:200
  36.2 4.2 %copy-start.6 = (f32[3,16,128]{2,1,0:T(8,128)}, f32[3,16,128]{2,1,0:T(8,128)S(1)}, u32[]{:S(2)}) copy-start(f32[3,16,128]{2,1,0:T(8,128)S(1)} %collective-permute-done.4.r_5_) | copy-start | bytes 73732
  36.2 4.2 %collective-permute-start.9 = (f32[3,16,128]{2,1,0:T(8,128)}, f32[3,16,128]{2,1,0:T(8,128)S(1)}, u32[]{:S(2)}, u32[]{:S(2)}) collective-permute-start(f32[3,16,128]{2,1,0:T(8,128)} %get-tuple-element.28), channel_id=1, source_target_pairs={{0,24},{4,28},{8,0},{12,4},{16,8},{20,12},{24,16},{28,20},{1,25},{... | collective-permute-start | bytes 73736 | tf_op jit(solution)/shard_map/ppermute | solution.py:200
  37.7 2.6 %copy-start.7 = (f32[3,16,128]{2,1,0:T(8,128)}, f32[3,16,128]{2,1,0:T(8,128)S(1)}, u32[]{:S(2)}) copy-start(f32[3,16,128]{2,1,0:T(8,128)S(1)} %collective-permute-done.5.r_6_) | copy-start | bytes 73732
  37.7 2.6 %copy-start.8 = (f32[3,16,128]{2,1,0:T(8,128)}, f32[3,16,128]{2,1,0:T(8,128)S(1)}, u32[]{:S(2)}) copy-start(f32[3,16,128]{2,1,0:T(8,128)S(1)} %collective-permute-done.6.r_7_) | copy-start | bytes 73732
  37.8 2.6 %copy-start.9 = (f32[3,16,128]{2,1,0:T(8,128)}, f32[3,16,128]{2,1,0:T(8,128)S(1)}, u32[]{:S(2)}) copy-start(f32[3,16,128]{2,1,0:T(8,128)S(1)} %collective-permute-done.7.r_8_) | copy-start | bytes 73732
  43.1 5.2 %collective-permute-start.11 = (f32[4,16,128]{2,1,0:T(8,128)}, f32[4,16,128]{2,1,0:T(8,128)S(1)}, u32[]{:S(2)}, u32[]{:S(2)}) collective-permute-start(f32[4,16,128]{2,1,0:T(8,128)} %get-tuple-element.31), channel_id=1, source_target_pairs={{0,1},{1,2},{2,3},{3,0},{4,5},{5,6},{6,7},{7,4},{8,9},{9,10},{10,1... | collective-permute-start | bytes 98312 | tf_op jit(solution)/shard_map/ppermute | solution.py:212
  43.2 5.7 %collective-permute-start.12 = (f32[4,16,128]{2,1,0:T(8,128)}, f32[4,16,128]{2,1,0:T(8,128)S(1)}, u32[]{:S(2)}, u32[]{:S(2)}) collective-permute-start(f32[4,16,128]{2,1,0:T(8,128)} %get-tuple-element.31), channel_id=1, source_target_pairs={{0,2},{1,3},{2,0},{3,1},{4,6},{5,7},{6,4},{7,5},{8,10},{9,11},{10,... | collective-permute-start | bytes 98312 | tf_op jit(solution)/shard_map/ppermute | solution.py:212
  46.8 3.3 %collective-permute-start.13 = (f32[4,16,128]{2,1,0:T(8,128)}, f32[4,16,128]{2,1,0:T(8,128)S(1)}, u32[]{:S(2)}, u32[]{:S(2)}) collective-permute-start(f32[4,16,128]{2,1,0:T(8,128)} %get-tuple-element.31), channel_id=1, source_target_pairs={{0,3},{1,0},{2,1},{3,2},{4,7},{5,4},{6,5},{7,6},{8,11},{9,8},{10,9... | collective-permute-start | bytes 98312 | tf_op jit(solution)/shard_map/ppermute | solution.py:212
  48.2 1.9 %copy-start.4 = (f32[4,16,128]{2,1,0:T(8,128)S(1)}, f32[4,16,128]{2,1,0:T(8,128)}, u32[]{:S(2)}) copy-start(f32[4,16,128]{2,1,0:T(8,128)} %get-tuple-element.31) | copy-start | bytes 98308
  (4 other events, 2.7 us)

commit v4 on v3

--- a/solution.py
+++ b/solution.py
@@ -26,28 +26,26 @@
 SMEM = pl.BlockSpec(memory_space=pltpu.SMEM)
 
 
-def edges_kernel(adj_ref, base_ref, xlo_ref, xhi_ref, ylo_ref, yhi_ref, sems):
+def column(ref, k, ny, nz):
+    return jnp.broadcast_to(ref[:, k : k + 1], (ny, nz))
+
+
+def edges_kernel(adj_ref, base_ref, xlo_ref, xhi_ref, ylo_ref, yhi_ref):
     n, ny = adj_ref.shape[1], adj_ref.shape[2]
-    copies = []
-    for s, src in enumerate((adj_ref, base_ref)):
-        dst = pl.ds(3 * s, 3)
-        copies += [
-            pltpu.make_async_copy(src.at[:, 0], xlo_ref.at[dst], sems.at[4 * s]),
-            pltpu.make_async_copy(src.at[:, n - 1], xhi_ref.at[dst], sems.at[4 * s + 1]),
-            pltpu.make_async_copy(src.at[:, :, 0], ylo_ref.at[dst], sems.at[4 * s + 2]),
-            pltpu.make_async_copy(src.at[:, :, ny - 1], yhi_ref.at[dst], sems.at[4 * s + 3]),
-        ]
-    for cp in copies:
-        cp.start()
-    for cp in copies:
-        cp.wait()
+    for k in range(6):
+        ref, c = (adj_ref, k) if k < 3 else (base_ref, k - 3)
+        xlo_ref[k] = ref[c, 0]
+        xhi_ref[k] = ref[c, n - 1]
+        for x in range(n):
+            ylo_ref[k, x : x + 1, :] = ref[c, x, 0:1, :]
+            yhi_ref[k, x : x + 1, :] = ref[c, x, ny - 1 : ny, :]
 
 
 def sweep_kernel(G, direct, idx_ref, adj_ref, base_ref, xlo_ref, xhi_ref, ylo_ref, yhi_ref, coef_ref, sw_ref, own_ref, *send_refs):
     n, ny, nz = adj_ref.shape[1], adj_ref.shape[2], adj_ref.shape[3]
-    metric = coef_ref[0]
-    decay = coef_ref[1]
-    gain = coef_ref[2]
+    metric = column(coef_ref, 0, ny, nz)
+    decay = column(coef_ref, 1, ny, nz)
+    gain = column(coef_ref, 2, ny, nz)
     row = lax.broadcasted_iota(jnp.int32, (ny, nz), 0)
 
     def field(k, x):
@@ -85,7 +83,6 @@
             f = sw_ref[c, x]
             back[c] = f if x == n - 1 else f + decay * back[c]
             sw_ref[c, x] = back[c]
-    i = idx_ref[0]
     for c in range(3):
         carry_up = forward[c]
         carry_down = back[c] + gain * forward[c]
@@ -93,31 +90,31 @@
         own_ref[1, c] = carry_down
         if direct:
             for k in range(1, G):
-                send_refs[k - 1][c] = jnp.where(i + k < G, carry_up, carry_down)
+                send_refs[k - 1][c] = jnp.where(idx_ref[k] > 0, carry_up, carry_down)
 
 
 def finish_kernel(G, direct, idx_ref, adj_ref, sw_ref, own_ref, coef_ref, *rest):
     n, ny = adj_ref.shape[1], adj_ref.shape[2]
     out_ref, part_ref = rest[-2], rest[-1]
     got = rest[:-2]
-    rate = coef_ref[3]
-    decay = coef_ref[1]
-    shrink = coef_ref[4]
-    inverse = coef_ref[5]
-    low_w = coef_ref[6]
-    high_w = coef_ref[7]
-    near = coef_ref[8]
-    ratio = coef_ref[9]
+    nz = adj_ref.shape[3]
+    rate = column(coef_ref, 3, ny, nz)
+    decay = column(coef_ref, 1, ny, nz)
+    shrink = column(coef_ref, 4, ny, nz)
+    inverse = column(coef_ref, 5, ny, nz)
+    low_w = column(coef_ref, 6, ny, nz)
+    high_w = column(coef_ref, 7, ny, nz)
+    near = column(coef_ref, 8, ny, nz)
+    ratio = column(coef_ref, 9, ny, nz)
     block_rate = n * rate
-    i = idx_ref[0]
     inflow, later = [], []
     for c in range(3):
         if direct:
             a = jnp.zeros_like(rate)
             b = jnp.zeros_like(rate)
             for k in range(1, G):
-                upstream = i >= k
-                power = jnp.where(upstream, k - 1, G - k - 1).astype(jnp.float32)
+                upstream = idx_ref[k] == 0
+                power = idx_ref[G - 1 + k].astype(jnp.float32)
                 term = jnp.exp(-power * block_rate) * got[k - 1][c]
                 a = a + jnp.where(upstream, term, 0.0)
                 b = b + jnp.where(upstream, 0.0, term)
@@ -142,6 +139,22 @@
     part_ref[3] = jnp.broadcast_to(jnp.sum(inverse, axis=0, keepdims=True), part_ref.shape[1:])
 
 
+def is_pow2(size):
+    return size & (size - 1) == 0
+
+
+def partner_of(j, k, size):
+    if is_pow2(size):
+        return j ^ k
+    return (j + k) % size
+
+
+def slot_of(g, s, size):
+    if is_pow2(size):
+        return g ^ s
+    return (g - s) % size
+
+
 def scan_carries(L, U, A, G):
     inflow = shift(L, "gx", G, 1)
     later = shift(U, "gx", G, -1)
@@ -159,15 +172,15 @@
     G, i = lax.axis_size("gx"), lax.axis_index("gx")
     Gy, g = lax.axis_size("gy"), lax.axis_index("gy")
     _, n, ny, nz = adjoint.shape
-    direct = G <= DIRECT_LIMIT
-    idx = jnp.reshape(i, (1,)).astype(jnp.int32)
+    direct = G <= DIRECT_LIMIT and is_pow2(G)
+    partner = [partner_of(i, k, G) for k in range(1, G)] if direct else []
+    sends_up = [(p > i).astype(jnp.int32) for p in partner]
+    powers = [jnp.abs(p - i).astype(jnp.int32) - 1 for p in partner]
+    idx = jnp.stack([jnp.asarray(i, jnp.int32)] + sends_up + powers)
 
     xlo, xhi, ylo, yhi = pl.pallas_call(
         edges_kernel,
         out_shape=(f32((6, ny, nz)), f32((6, ny, nz)), f32((6, n, nz)), f32((6, n, nz))),
-        in_specs=[ANY, ANY],
-        out_specs=(ANY, ANY, ANY, ANY),
-        scratch_shapes=[pltpu.SemaphoreType.DMA((8,))],
     )(adjoint, base_flow)
     x_before = shift(xhi, "gx", G, 1)
     x_after = shift(xlo, "gx", G, -1)
@@ -184,7 +197,7 @@
     low_w = jnp.where(g == 0, 2.0 * metric[0], 0.0) + jnp.zeros_like(metric)
     high_w = jnp.where(g == Gy - 1, -2.0 * metric[-1], 0.0) + jnp.zeros_like(metric)
     vs = (metric, decay, c * A * geo_here, rate, jnp.expm1(-rate) ** 2, 1.0 / metric, low_w, high_w, c * geo_here, A)
-    coef = jnp.broadcast_to(jnp.stack(vs)[:, :, None], (len(vs), ny, nz))
+    coef = jnp.stack(vs, axis=1)
 
     plane = f32((3, ny, nz))
     sends = G - 1 if direct else 0
@@ -197,7 +210,8 @@
 
     if direct:
         got = [
-            lax.ppermute(outs[1 + k], "gx", [(j, (j + k) % G) for j in range(G)]) for k in range(1, G)
+            lax.ppermute(outs[1 + k], "gx", [(j, partner_of(j, k, G)) for j in range(G)])
+            for k in range(1, G)
         ]
     else:
         got = list(scan_carries(own[0], own[1], A[None, :, None], G))
@@ -209,12 +223,12 @@
     )(idx, adjoint, sw, own, coef, *got)
 
     pieces = [part] + [
-        lax.ppermute(part, "gy", [(j, (j + k) % Gy) for j in range(Gy)]) for k in range(1, Gy)
+        lax.ppermute(part, "gy", [(j, partner_of(j, k, Gy)) for j in range(Gy)]) for k in range(1, Gy)
     ]
     stacked = jnp.stack(pieces)
     total = None
     for s in range(Gy):
-        piece = lax.dynamic_index_in_dim(stacked, (g - s) % Gy, axis=0, keepdims=False)
+        piece = lax.dynamic_index_in_dim(stacked, slot_of(g, s, Gy), axis=0, keepdims=False)
         total = piece if total is None else total + piece
     bulk_mean = total[2] / total[3]
     wall_gradient = total[:2] + bulk_mean[None]

time: 51.5 us -> 51.3 us (level)
  Pallas kernels: 11.9 us -> 6.64 us
  waiting for transfers between devices: 5.61 us -> 9.35 us
  local copies, waits for them, and re-layouts: 2.64 us -> 5.66 us
  starting transfers between devices: 27.7 us -> 26.3 us
    pallas_call x1, Pallas kernels: 7.13 us -> 1.84 us  [local(): pl.pallas_call(edges_kernel, out_shape=(f32((6, ny, nz)), f32((6, ny, nz)...]
    ppermute x10, waiting for transfers between devices: 4.81 us -> 9.34 us  [the longest x7 5.83 us: local(): lax.ppermute(outs[1 + k], 'gx', [(j, partner_of(j, k, G)) for j in range(...]
    another operation x3 -> x12, local copies, waits for them, and re-layouts: 0.05 us -> 1.97 us  [the longest x11 1.35 us: local(): coef = jnp.stack(vs, axis=1)]
    unnamed x28, local copies, waits for them, and re-layouts: 1.24 us -> 3.1 us
    ppermute x10, starting transfers between devices: 18.8 us -> 17.4 us  [the longest x7 12.8 us: local(): lax.ppermute(outs[1 + k], 'gx', [(j, partner_of(j, k, G)) for j in range(...]
    ppermute x4, waiting for transfers between devices: 0.8 us -> 0.01 us  [shift(): return lax.ppermute(x, axis, pairs)]
    broadcast_in_dim x1 -> x0, local copies, waits for them, and re-layouts: 0.73 us -> none  [local(): coef = jnp.broadcast_to(jnp.stack(vs)[:, :, None], (len(vs), ny, nz))]
  transfers between devices with their start and end apart: 14 -> 14, of which waited for: 6 -> 5; matrix products, arithmetic and copies ran while one was open for 2% -> 5% of each run, Pallas kernels for 0% -> 0%
where the time goes in v4:
time: 51.3 us; the launch traced here: 51 us
  starting transfers between devices  26.3 us (51%)
  waiting for transfers between devices  9.35 us (18%)
  Pallas kernels  6.64 us (13%)
  local copies, waits for them, and re-layouts  5.66 us (11%)
  between operations  2.2 us (4%)
  other arithmetic  0.78 us (2%)
    ppermute x7, starting transfers between devices, local(): lax.ppermute(outs[1 + k], 'gx', [(j, partner_of(j, k, G)) for j in range(...  12.8 us
    ppermute x4, starting transfers between devices, shift(): return lax.ppermute(x, axis, pairs)  8.91 us
    ppermute x7, waiting for transfers between devices, local(): lax.ppermute(outs[1 + k], 'gx', [(j, partner_of(j, k, G)) for j in range(...  5.83 us
    ppermute x3, starting transfers between devices, local(): lax.ppermute(part, 'gy', [(j, partner_of(j, k, Gy)) for j in range(Gy)])  4.58 us
    ppermute x3, waiting for transfers between devices, local(): lax.ppermute(part, 'gy', [(j, partner_of(j, k, Gy)) for j in range(Gy)])  3.52 us
    unnamed x28, local copies, waits for them, and re-layouts  3.1 us
    pallas_call x1, Pallas kernels, local(): pl.pallas_call(lambda *r: sweep_kernel(G, direct, *r), out_shape=(f32(adj...  2.62 us
    pallas_call x1, Pallas kernels, local(): pl.pallas_call(lambda *r: finish_kernel(G, direct, *r), out_shape=(f32(ad...  2.18 us
  transfers between devices with their start and end apart: 14, of which 5 were waited for; matrix products, arithmetic and copies ran while one was open for 5% of the time, Pallas kernels for 0%

profile of v4, /device:TPU:0, one launch (start us, length us, event | category | flops | bytes accessed | tf_op | source)
XLA Modules:
  0.0 51.0 jit_solution(15422187668777985951)
XLA Ops:
  0.6 1.8 %shard_map.59 = (f32[6,16,128]{2,1,0:T(8,128)}, f32[6,16,128]{2,1,0:T(8,128)}, f32[6,16,128]{2,1,0:T(8,128)}, f32[6,16,128]{2,1,0:T(8,128)}) custom-call(f32[3,16,16,128]{3,2,1,0:T(8,128)} %r_1_.3, f32[3,16,16,128]{3,2,1,0:T(8,128)} %r_2_.1), custom_call_target="tpu_custom_call" | custom-call | tf_op jit(solution)/shard_map/pallas_call | solution.py:181
  2.5 4.9 %collective-permute-start = (f32[6,16,128]{2,1,0:T(8,128)}, f32[6,16,128]{2,1,0:T(8,128)S(1)}, u32[]{:S(2)}, u32[]{:S(2)}) collective-permute-start(f32[6,16,128]{2,1,0:T(8,128)} %get-tuple-element.17), channel_id=1, source_target_pairs={{0,4},{4,8},{8,12},{12,16},{16,20},{20,24},{24,28},{1,5},{5,9},{9,... | collective-permute-start | bytes 147464 | tf_op jit(solution)/shard_map/ppermute | solution.py:18
  7.3 1.3 %collective-permute-start.1 = (f32[6,16,128]{2,1,0:T(8,128)}, f32[6,16,128]{2,1,0:T(8,128)S(1)}, u32[]{:S(2)}, u32[]{:S(2)}) collective-permute-start(f32[6,16,128]{2,1,0:T(8,128)} %get-tuple-element.18), channel_id=1, source_target_pairs={{4,0},{8,4},{12,8},{16,12},{20,16},{24,20},{28,24},{5,1},{9,5},{13... | collective-permute-start | bytes 147464 | tf_op jit(solution)/shard_map/ppermute | solution.py:18
  8.6 1.5 %collective-permute-start.2 = (f32[6,16,128]{2,1,0:T(8,128)}, f32[6,16,128]{2,1,0:T(8,128)S(1)}, u32[]{:S(2)}, u32[]{:S(2)}) collective-permute-start(f32[6,16,128]{2,1,0:T(8,128)} %get-tuple-element.19), channel_id=1, source_target_pairs={{0,1},{1,2},{2,3},{4,5},{5,6},{6,7},{8,9},{9,10},{10,11},{12,13},{... | collective-permute-start | bytes 147464 | tf_op jit(solution)/shard_map/ppermute | solution.py:18
  10.1 1.3 %collective-permute-start.3 = (f32[6,16,128]{2,1,0:T(8,128)}, f32[6,16,128]{2,1,0:T(8,128)S(1)}, u32[]{:S(2)}, u32[]{:S(2)}) collective-permute-start(f32[6,16,128]{2,1,0:T(8,128)} %get-tuple-element.20), channel_id=1, source_target_pairs={{1,0},{2,1},{3,2},{5,4},{6,5},{7,6},{9,8},{10,9},{11,10},{13,12},{... | collective-permute-start | bytes 147464 | tf_op jit(solution)/shard_map/ppermute | solution.py:18
  11.4 0.6 %copy-done.13 = f32[16]{0:T(128)S(1)} copy-done((f32[16]{0:T(128)S(1)}, f32[16]{0:T(128)}, u32[]{:S(2)}) %copy-start.13) | copy-done | bytes 88
  12.2 0.6 %copy-done.12 = f32[16]{0:T(128)S(1)} copy-done((f32[16]{0:T(128)S(1)}, f32[16]{0:T(128)}, u32[]{:S(2)}) %copy-start.12) | copy-done | bytes 88
  12.9 0.6 %fusion.3 = (f32[1]{0:T(128)}, f32[1]{0:T(128)}) fusion(f32[16]{0:T(128)S(1)} %copy-done.12), kind=kLoop, calls=%fused_computation.17 | loop fusion | bytes 16 | tf_op jit(solution)/shard_map/slice | solution.py:198
  15.5 0.7 %stack.150.r_7_.r_4_ = f32[16,10]{1,0:T(8,128)} concatenate(f32[16,1]{1,0:T(8,128)S(1)} %copy.14, f32[16,1]{1,0:T(8,128)S(1)} %copy.15, f32[16,1]{1,0:T(8,128)S(1)} %copy.16, f32[16,1]{1,0:T(8,128)S(1)} %copy.17, f32[16,1]{1,0:T(8,128)S(1)} %copy.18, f32[16,1]{1,0:T(8,128)S(1)} %copy.19, f32[16,1]{1,0:T(8,128)S(1)} %stack.146, f32[16,1]{1,0:T(8,128)S(1)} %stack.147, ...), dimensions={1} | concatenate | bytes 1280 | tf_op jit(solution)/shard_map/stack | solution.py:200
  16.2 0.6 %stack.139.r_0_ = s32[15]{0:T(128)} concatenate(s32[1]{0:T(128)} %bitcast, s32[1]{0:T(128)} %bitcast.1, s32[1]{0:T(128)} %bitcast.2, s32[1]{0:T(128)} %bitcast.3, s32[1]{0:T(128)} %bitcast.4, s32[1]{0:T(128)} %bitcast.5, s32[1]{0:T(128)} %bitcast.6, s32[1]{0:T(128)} %bitcast.7, s32[1]{0:T(128)} %bitcast.8, s32[1]{0:T(128)} %bitcast.9, s32[1]{0:T(128)} %bitcast.10, s32[1]{0:T(128)} %bitcast.11, ...), dimensions={0} | concatenate | bytes 120 | tf_op jit(solution)/shard_map/stack | solution.py:179
  17.4 0.6 %copy-done.3 = f32[6,16,128]{2,1,0:T(8,128)} copy-done((f32[6,16,128]{2,1,0:T(8,128)}, f32[6,16,128]{2,1,0:T(8,128)S(1)}, u32[]{:S(2)}) %copy-start.3) | copy-done | bytes 49176
  18.1 2.6 %shard_map.60 = (f32[3,16,16,128]{3,2,1,0:T(8,128)}, f32[2,3,16,128]{3,2,1,0:T(8,128)}, f32[3,16,128]{2,1,0:T(8,128)}, f32[3,16,128]{2,1,0:T(8,128)}, f32[3,16,1...) custom-call(s32[15]{0:T(128)} %stack.139.r_0_, ...), custom_call_target="tpu_custom_call" | custom-call | tf_op jit(solution)/shard_map/pallas_call | solution.py:204
  20.7 5.6 %collective-permute-start.10 = (f32[3,16,128]{2,1,0:T(8,128)}, f32[3,16,128]{2,1,0:T(8,128)S(1)}, u32[]{:S(2)}, u32[]{:S(2)}) collective-permute-start(f32[3,16,128]{2,1,0:T(8,128)} %get-tuple-element.29), channel_id=1, source_target_pairs={{0,28},{4,24},{8,20},{12,16},{16,12},{20,8},{24,4},{28,0},{1,29},{... | collective-permute-start | bytes 73736 | tf_op jit(solution)/shard_map/ppermute | solution.py:213
  26.2 1.4 %collective-permute-start.4 = (f32[3,16,128]{2,1,0:T(8,128)}, f32[3,16,128]{2,1,0:T(8,128)S(1)}, u32[]{:S(2)}, u32[]{:S(2)}) collective-permute-start(f32[3,16,128]{2,1,0:T(8,128)} %get-tuple-element.23), channel_id=1, source_target_pairs={{0,4},{4,0},{8,12},{12,8},{16,20},{20,16},{24,28},{28,24},{1,5},{5... | collective-permute-start | bytes 73736 | tf_op jit(solution)/shard_map/ppermute | solution.py:213
  27.7 2.0 %collective-permute-start.6 = (f32[3,16,128]{2,1,0:T(8,128)}, f32[3,16,128]{2,1,0:T(8,128)S(1)}, u32[]{:S(2)}, u32[]{:S(2)}) collective-permute-start(f32[3,16,128]{2,1,0:T(8,128)} %get-tuple-element.25), channel_id=1, source_target_pairs={{0,12},{4,8},{8,4},{12,0},{16,28},{20,24},{24,20},{28,16},{1,13},{... | collective-permute-start | bytes 73736 | tf_op jit(solution)/shard_map/ppermute | solution.py:213
  29.7 3.8 %collective-permute-start.8 = (f32[3,16,128]{2,1,0:T(8,128)}, f32[3,16,128]{2,1,0:T(8,128)S(1)}, u32[]{:S(2)}, u32[]{:S(2)}) collective-permute-start(f32[3,16,128]{2,1,0:T(8,128)} %get-tuple-element.27), channel_id=1, source_target_pairs={{0,20},{4,16},{8,28},{12,24},{16,4},{20,0},{24,12},{28,8},{1,21},{... | collective-permute-start | bytes 73736 | tf_op jit(solution)/shard_map/ppermute | solution.py:213
  33.6 1.1 %collective-permute-done.7.r_8_ = f32[3,16,128]{2,1,0:T(8,128)S(1)} collective-permute-done((f32[3,16,128]{2,1,0:T(8,128)}, f32[3,16,128]{2,1,0:T(8,128)S(1)}, u32[]{:S(2)}, u32[]{:S(2)}) %collective-permute-start.7) | collective-permute-done | bytes 24608 | tf_op jit(solution)/shard_map/ppermute | solution.py:213
  34.7 2.1 %collective-permute-done.8.r_9_ = f32[3,16,128]{2,1,0:T(8,128)S(1)} collective-permute-done((f32[3,16,128]{2,1,0:T(8,128)}, f32[3,16,128]{2,1,0:T(8,128)S(1)}, u32[]{:S(2)}, u32[]{:S(2)}) %collective-permute-start.8) | collective-permute-done | bytes 24608 | tf_op jit(solution)/shard_map/ppermute | solution.py:213
  36.8 2.6 %collective-permute-done.9.r_10_ = f32[3,16,128]{2,1,0:T(8,128)S(1)} collective-permute-done((f32[3,16,128]{2,1,0:T(8,128)}, f32[3,16,128]{2,1,0:T(8,128)S(1)}, u32[]{:S(2)}, u32[]{:S(2)}) %collective-permute-start.9) | collective-permute-done | bytes 24608 | tf_op jit(solution)/shard_map/ppermute | solution.py:213
  40.0 2.2 %shard_map.61 = (f32[3,16,16,128]{3,2,1,0:T(8,128)}, f32[4,16,128]{2,1,0:T(8,128)}) custom-call(s32[15]{0:T(128)} %stack.139.r_0_, f32[3,16,16,128]{3,2,1,0:T(8,128)} %r_1_.3, f32[3,16,16,128]{3,2,1,0:T(8,128)} %get-tuple-element.21.r_2_, f32[2,3,16,128]{3,2,1,0:T(8,128)} %get-tuple-element.22.r_3_, f32[16,10]{1,0:T(8,128)} %stack.150.r_7_.r_4_, ...), custom_call_target="tpu_custom_call" | custom-call | tf_op jit(solution)/shard_map/pallas_call | solution.py:219
  42.3 4.4 %collective-permute-start.12 = (f32[4,16,128]{2,1,0:T(8,128)}, f32[4,16,128]{2,1,0:T(8,128)S(1)}, u32[]{:S(2)}, u32[]{:S(2)}) collective-permute-start(f32[4,16,128]{2,1,0:T(8,128)} %get-tuple-element.31), channel_id=1, source_target_pairs={{0,2},{1,3},{2,0},{3,1},{4,6},{5,7},{6,4},{7,5},{8,10},{9,11},{10,... | collective-permute-start | bytes 98312 | tf_op jit(solution)/shard_map/ppermute | solution.py:226
  46.8 2.2 %collective-permute-done.12 = f32[4,16,128]{2,1,0:T(8,128)S(1)} collective-permute-done((f32[4,16,128]{2,1,0:T(8,128)}, f32[4,16,128]{2,1,0:T(8,128)S(1)}, u32[]{:S(2)}, u32[]{:S(2)}) %collective-permute-start.12) | collective-permute-done | bytes 32800 | tf_op jit(solution)/shard_map/ppermute | solution.py:226
  48.9 1.4 %collective-permute-done.13 = f32[4,16,128]{2,1,0:T(8,128)S(1)} collective-permute-done((f32[4,16,128]{2,1,0:T(8,128)}, f32[4,16,128]{2,1,0:T(8,128)S(1)}, u32[]{:S(2)}, u32[]{:S(2)}) %collective-permute-start.13) | collective-permute-done | bytes 32800 | tf_op jit(solution)/shard_map/ppermute | solution.py:226
  50.4 0.6 %fusion = f32[2,16,128]{2,1,0:T(8,128)} fusion(f32[1,4,16,128]{3,2,1,0:T(8,128)S(1)} %dynamic-slice_add_fusion, f32[16,128]{1,0:T(8,128)S(1)} %fusion.1), kind=kLoop, calls=%fused_computation.3 | loop fusion | flops 4096 | bytes 40960 | tf_op jit(solution)/shard_map/add | solution.py:234
  (57 shorter events, 2.2 us)
Async XLA Ops:
  2.5 14.3 %collective-permute-start = (f32[6,16,128]{2,1,0:T(8,128)}, f32[6,16,128]{2,1,0:T(8,128)S(1)}, u32[]{:S(2)}, u32[]{:S(2)}) collective-permute-start(f32[6,16,128]{2,1,0:T(8,128)} %get-tuple-element.17), channel_id=1, source_target_pairs={{0,4},{4,8},{8,12},{12,16},{16,20},{20,24},{24,28},{1,5},{5,9},{9,... | collective-permute-start | bytes 147464 | tf_op jit(solution)/shard_map/ppermute | solution.py:18
  7.3 9.5 %collective-permute-start.1 = (f32[6,16,128]{2,1,0:T(8,128)}, f32[6,16,128]{2,1,0:T(8,128)S(1)}, u32[]{:S(2)}, u32[]{:S(2)}) collective-permute-start(f32[6,16,128]{2,1,0:T(8,128)} %get-tuple-element.18), channel_id=1, source_target_pairs={{4,0},{8,4},{12,8},{16,12},{20,16},{24,20},{28,24},{5,1},{9,5},{13... | collective-permute-start | bytes 147464 | tf_op jit(solution)/shard_map/ppermute | solution.py:18
  8.6 8.2 %collective-permute-start.2 = (f32[6,16,128]{2,1,0:T(8,128)}, f32[6,16,128]{2,1,0:T(8,128)S(1)}, u32[]{:S(2)}, u32[]{:S(2)}) collective-permute-start(f32[6,16,128]{2,1,0:T(8,128)} %get-tuple-element.19), channel_id=1, source_target_pairs={{0,1},{1,2},{2,3},{4,5},{5,6},{6,7},{8,9},{9,10},{10,11},{12,13},{... | collective-permute-start | bytes 147464 | tf_op jit(solution)/shard_map/ppermute | solution.py:18
  10.1 6.7 %collective-permute-start.3 = (f32[6,16,128]{2,1,0:T(8,128)}, f32[6,16,128]{2,1,0:T(8,128)S(1)}, u32[]{:S(2)}, u32[]{:S(2)}) collective-permute-start(f32[6,16,128]{2,1,0:T(8,128)} %get-tuple-element.20), channel_id=1, source_target_pairs={{1,0},{2,1},{3,2},{5,4},{6,5},{7,6},{9,8},{10,9},{11,10},{13,12},{... | collective-permute-start | bytes 147464 | tf_op jit(solution)/shard_map/ppermute | solution.py:18
  11.4 0.7 %copy-start.13 = (f32[16]{0:T(128)S(1)}, f32[16]{0:T(128)}, u32[]{:S(2)}) copy-start(f32[16]{0:T(128)} %param.7) | copy-start | bytes 196
  12.2 0.7 %copy-start.12 = (f32[16]{0:T(128)S(1)}, f32[16]{0:T(128)}, u32[]{:S(2)}) copy-start(f32[16]{0:T(128)} %param.6) | copy-start | bytes 196
  16.8 0.6 %copy-start.1 = (f32[6,16,128]{2,1,0:T(8,128)}, f32[6,16,128]{2,1,0:T(8,128)S(1)}, u32[]{:S(2)}) copy-start(f32[6,16,128]{2,1,0:T(8,128)S(1)} %collective-permute-done.1.r_4_) | copy-start | bytes 147460
  20.7 9.1 %collective-permute-start.10 = (f32[3,16,128]{2,1,0:T(8,128)}, f32[3,16,128]{2,1,0:T(8,128)S(1)}, u32[]{:S(2)}, u32[]{:S(2)}) collective-permute-start(f32[3,16,128]{2,1,0:T(8,128)} %get-tuple-element.29), channel_id=1, source_target_pairs={{0,28},{4,24},{8,20},{12,16},{16,12},{20,8},{24,4},{28,0},{1,29},{... | collective-permute-start | bytes 73736 | tf_op jit(solution)/shard_map/ppermute | solution.py:213
  26.2 7.3 %collective-permute-start.4 = (f32[3,16,128]{2,1,0:T(8,128)}, f32[3,16,128]{2,1,0:T(8,128)S(1)}, u32[]{:S(2)}, u32[]{:S(2)}) collective-permute-start(f32[3,16,128]{2,1,0:T(8,128)} %get-tuple-element.23), channel_id=1, source_target_pairs={{0,4},{4,0},{8,12},{12,8},{16,20},{20,16},{24,28},{28,24},{1,5},{5... | collective-permute-start | bytes 73736 | tf_op jit(solution)/shard_map/ppermute | solution.py:213
  27.7 5.9 %collective-permute-start.5 = (f32[3,16,128]{2,1,0:T(8,128)}, f32[3,16,128]{2,1,0:T(8,128)S(1)}, u32[]{:S(2)}, u32[]{:S(2)}) collective-permute-start(f32[3,16,128]{2,1,0:T(8,128)} %get-tuple-element.24), channel_id=1, source_target_pairs={{0,8},{4,12},{8,0},{12,4},{16,24},{20,28},{24,16},{28,20},{1,9},{5... | collective-permute-start | bytes 73736 | tf_op jit(solution)/shard_map/ppermute | solution.py:213
  27.7 5.9 %collective-permute-start.6 = (f32[3,16,128]{2,1,0:T(8,128)}, f32[3,16,128]{2,1,0:T(8,128)S(1)}, u32[]{:S(2)}, u32[]{:S(2)}) collective-permute-start(f32[3,16,128]{2,1,0:T(8,128)} %get-tuple-element.25), channel_id=1, source_target_pairs={{0,12},{4,8},{8,4},{12,0},{16,28},{20,24},{24,20},{28,16},{1,13},{... | collective-permute-start | bytes 73736 | tf_op jit(solution)/shard_map/ppermute | solution.py:213
  29.7 4.9 %collective-permute-start.7 = (f32[3,16,128]{2,1,0:T(8,128)}, f32[3,16,128]{2,1,0:T(8,128)S(1)}, u32[]{:S(2)}, u32[]{:S(2)}) collective-permute-start(f32[3,16,128]{2,1,0:T(8,128)} %get-tuple-element.26), channel_id=1, source_target_pairs={{0,16},{4,20},{8,24},{12,28},{16,0},{20,4},{24,8},{28,12},{1,17},{... | collective-permute-start | bytes 73736 | tf_op jit(solution)/shard_map/ppermute | solution.py:213
  29.7 9.7 %copy-start.5 = (f32[3,16,128]{2,1,0:T(8,128)}, f32[3,16,128]{2,1,0:T(8,128)S(1)}, u32[]{:S(2)}) copy-start(f32[3,16,128]{2,1,0:T(8,128)S(1)} %collective-permute-done.10.r_11_) | copy-start | bytes 73732
  29.7 7.0 %collective-permute-start.8 = (f32[3,16,128]{2,1,0:T(8,128)}, f32[3,16,128]{2,1,0:T(8,128)S(1)}, u32[]{:S(2)}, u32[]{:S(2)}) collective-permute-start(f32[3,16,128]{2,1,0:T(8,128)} %get-tuple-element.27), channel_id=1, source_target_pairs={{0,20},{4,16},{8,28},{12,24},{16,4},{20,0},{24,12},{28,8},{1,21},{... | collective-permute-start | bytes 73736 | tf_op jit(solution)/shard_map/ppermute | solution.py:213
  33.5 5.9 %copy-start.6 = (f32[3,16,128]{2,1,0:T(8,128)}, f32[3,16,128]{2,1,0:T(8,128)S(1)}, u32[]{:S(2)}) copy-start(f32[3,16,128]{2,1,0:T(8,128)S(1)} %collective-permute-done.4.r_5_) | copy-start | bytes 73732
  33.5 5.9 %collective-permute-start.9 = (f32[3,16,128]{2,1,0:T(8,128)}, f32[3,16,128]{2,1,0:T(8,128)S(1)}, u32[]{:S(2)}, u32[]{:S(2)}) collective-permute-start(f32[3,16,128]{2,1,0:T(8,128)} %get-tuple-element.28), channel_id=1, source_target_pairs={{0,24},{4,28},{8,16},{12,20},{16,8},{20,12},{24,0},{28,4},{1,25},{... | collective-permute-start | bytes 73736 | tf_op jit(solution)/shard_map/ppermute | solution.py:213
  33.5 5.9 %copy-start.7 = (f32[3,16,128]{2,1,0:T(8,128)}, f32[3,16,128]{2,1,0:T(8,128)S(1)}, u32[]{:S(2)}) copy-start(f32[3,16,128]{2,1,0:T(8,128)S(1)} %collective-permute-done.5.r_6_) | copy-start | bytes 73732
  33.6 5.8 %copy-start.8 = (f32[3,16,128]{2,1,0:T(8,128)}, f32[3,16,128]{2,1,0:T(8,128)S(1)}, u32[]{:S(2)}) copy-start(f32[3,16,128]{2,1,0:T(8,128)S(1)} %collective-permute-done.6.r_7_) | copy-start | bytes 73732
  34.7 4.8 %copy-start.9 = (f32[3,16,128]{2,1,0:T(8,128)}, f32[3,16,128]{2,1,0:T(8,128)S(1)}, u32[]{:S(2)}) copy-start(f32[3,16,128]{2,1,0:T(8,128)S(1)} %collective-permute-done.7.r_8_) | copy-start | bytes 73732
  36.8 2.7 %copy-start.10 = (f32[3,16,128]{2,1,0:T(8,128)}, f32[3,16,128]{2,1,0:T(8,128)S(1)}, u32[]{:S(2)}) copy-start(f32[3,16,128]{2,1,0:T(8,128)S(1)} %collective-permute-done.8.r_9_) | copy-start | bytes 73732
  42.2 8.1 %copy-start.4 = (f32[4,16,128]{2,1,0:T(8,128)S(1)}, f32[4,16,128]{2,1,0:T(8,128)}, u32[]{:S(2)}) copy-start(f32[4,16,128]{2,1,0:T(8,128)} %get-tuple-element.31) | copy-start | bytes 98308
  42.2 4.6 %collective-permute-start.11 = (f32[4,16,128]{2,1,0:T(8,128)}, f32[4,16,128]{2,1,0:T(8,128)S(1)}, u32[]{:S(2)}, u32[]{:S(2)}) collective-permute-start(f32[4,16,128]{2,1,0:T(8,128)} %get-tuple-element.31), channel_id=1, source_target_pairs={{0,1},{1,0},{2,3},{3,2},{4,5},{5,4},{6,7},{7,6},{8,9},{9,8},{10,11... | collective-permute-start | bytes 98312 | tf_op jit(solution)/shard_map/ppermute | solution.py:226
  42.3 6.6 %collective-permute-start.12 = (f32[4,16,128]{2,1,0:T(8,128)}, f32[4,16,128]{2,1,0:T(8,128)S(1)}, u32[]{:S(2)}, u32[]{:S(2)}) collective-permute-start(f32[4,16,128]{2,1,0:T(8,128)} %get-tuple-element.31), channel_id=1, source_target_pairs={{0,2},{1,3},{2,0},{3,1},{4,6},{5,7},{6,4},{7,5},{8,10},{9,11},{10,... | collective-permute-start | bytes 98312 | tf_op jit(solution)/shard_map/ppermute | solution.py:226
  46.7 3.6 %collective-permute-start.13 = (f32[4,16,128]{2,1,0:T(8,128)}, f32[4,16,128]{2,1,0:T(8,128)S(1)}, u32[]{:S(2)}, u32[]{:S(2)}) collective-permute-start(f32[4,16,128]{2,1,0:T(8,128)} %get-tuple-element.31), channel_id=1, source_target_pairs={{0,3},{1,2},{2,1},{3,0},{4,7},{5,6},{6,5},{7,4},{8,11},{9,10},{10,... | collective-permute-start | bytes 98312 | tf_op jit(solution)/shard_map/ppermute | solution.py:226
  (4 other events, 2.5 us)

commit v5 on v4

--- a/solution.py
+++ b/solution.py
@@ -22,12 +22,24 @@
     return jax.ShapeDtypeStruct(shape, jnp.float32)
 
 
-ANY = pl.BlockSpec(memory_space=pl.ANY)
-SMEM = pl.BlockSpec(memory_space=pltpu.SMEM)
-
-
 def column(ref, k, ny, nz):
     return jnp.broadcast_to(ref[:, k : k + 1], (ny, nz))
+
+
+def is_pow2(size):
+    return size & (size - 1) == 0
+
+
+def partner_of(j, k, size):
+    if is_pow2(size):
+        return j ^ k
+    return (j + k) % size
+
+
+def slot_of(g, s, size):
+    if is_pow2(size):
+        return g ^ s
+    return (g - s) % size
 
 
 def edges_kernel(adj_ref, base_ref, xlo_ref, xhi_ref, ylo_ref, yhi_ref):
@@ -41,7 +53,7 @@
             yhi_ref[k, x : x + 1, :] = ref[c, x, ny - 1 : ny, :]
 
 
-def sweep_kernel(G, direct, idx_ref, adj_ref, base_ref, xlo_ref, xhi_ref, ylo_ref, yhi_ref, coef_ref, sw_ref, own_ref, *send_refs):
+def sweep_kernel(adj_ref, base_ref, xlo_ref, xhi_ref, ylo_ref, yhi_ref, coef_ref, sw_ref, pay_ref):
     n, ny, nz = adj_ref.shape[1], adj_ref.shape[2], adj_ref.shape[3]
     metric = column(coef_ref, 0, ny, nz)
     decay = column(coef_ref, 1, ny, nz)
@@ -84,20 +96,14 @@
             back[c] = f if x == n - 1 else f + decay * back[c]
             sw_ref[c, x] = back[c]
     for c in range(3):
-        carry_up = forward[c]
-        carry_down = back[c] + gain * forward[c]
-        own_ref[0, c] = carry_up
-        own_ref[1, c] = carry_down
-        if direct:
-            for k in range(1, G):
-                send_refs[k - 1][c] = jnp.where(idx_ref[k] > 0, carry_up, carry_down)
-
-
-def finish_kernel(G, direct, idx_ref, adj_ref, sw_ref, own_ref, coef_ref, *rest):
-    n, ny = adj_ref.shape[1], adj_ref.shape[2]
+        pay_ref[0, c] = forward[c]
+        pay_ref[1, c] = back[c] + gain * forward[c]
+
+
+def finish_kernel(G, direct, idx_ref, adj_ref, sw_ref, pay_ref, coef_ref, *rest):
+    n, ny, nz = adj_ref.shape[1], adj_ref.shape[2], adj_ref.shape[3]
     out_ref, part_ref = rest[-2], rest[-1]
     got = rest[:-2]
-    nz = adj_ref.shape[3]
     rate = column(coef_ref, 3, ny, nz)
     decay = column(coef_ref, 1, ny, nz)
     shrink = column(coef_ref, 4, ny, nz)
@@ -107,22 +113,28 @@
     near = column(coef_ref, 8, ny, nz)
     ratio = column(coef_ref, 9, ny, nz)
     block_rate = n * rate
+    i = idx_ref[0]
     inflow, later = [], []
+    if direct:
+        weights = []
+        for k in range(1, G):
+            j = lax.bitwise_xor(i, jnp.int32(k))
+            upstream = j < i
+            power = (jnp.maximum(i - j, j - i) - 1).astype(jnp.float32)
+            weights.append((upstream, jnp.exp(-power * block_rate)))
     for c in range(3):
         if direct:
             a = jnp.zeros_like(rate)
             b = jnp.zeros_like(rate)
             for k in range(1, G):
-                upstream = idx_ref[k] == 0
-                power = idx_ref[G - 1 + k].astype(jnp.float32)
-                term = jnp.exp(-power * block_rate) * got[k - 1][c]
-                a = a + jnp.where(upstream, term, 0.0)
-                b = b + jnp.where(upstream, 0.0, term)
+                upstream, w = weights[k - 1]
+                a = a + jnp.where(upstream, w * got[k - 1][0, c], 0.0)
+                b = b + jnp.where(upstream, 0.0, w * got[k - 1][1, c])
         else:
             a = got[0][c]
             b = got[1][c]
         inflow.append(a)
-        later.append(b + near * (own_ref[0, c] + ratio * a))
+        later.append(b + near * (pay_ref[0, c] + ratio * a))
     back_lead = None
     for x in range(n - 1, -1, -1):
         lead = jnp.exp(-(x + 1.0) * rate)
@@ -139,22 +151,6 @@
     part_ref[3] = jnp.broadcast_to(jnp.sum(inverse, axis=0, keepdims=True), part_ref.shape[1:])
 
 
-def is_pow2(size):
-    return size & (size - 1) == 0
-
-
-def partner_of(j, k, size):
-    if is_pow2(size):
-        return j ^ k
-    return (j + k) % size
-
-
-def slot_of(g, s, size):
-    if is_pow2(size):
-        return g ^ s
-    return (g - s) % size
-
-
 def scan_carries(L, U, A, G):
     inflow = shift(L, "gx", G, 1)
     later = shift(U, "gx", G, -1)
@@ -172,11 +168,6 @@
     G, i = lax.axis_size("gx"), lax.axis_index("gx")
     Gy, g = lax.axis_size("gy"), lax.axis_index("gy")
     _, n, ny, nz = adjoint.shape
-    direct = G <= DIRECT_LIMIT and is_pow2(G)
-    partner = [partner_of(i, k, G) for k in range(1, G)] if direct else []
-    sends_up = [(p > i).astype(jnp.int32) for p in partner]
-    powers = [jnp.abs(p - i).astype(jnp.int32) - 1 for p in partner]
-    idx = jnp.stack([jnp.asarray(i, jnp.int32)] + sends_up + powers)
 
     xlo, xhi, ylo, yhi = pl.pallas_call(
         edges_kernel,
@@ -194,33 +185,28 @@
     two_block = jnp.expm1(-2.0 * n * rate)
     downstream = (G - 1 - i).astype(jnp.float32)
     geo_here = jnp.expm1(-2.0 * n * downstream * rate) / two_block
+
     low_w = jnp.where(g == 0, 2.0 * metric[0], 0.0) + jnp.zeros_like(metric)
     high_w = jnp.where(g == Gy - 1, -2.0 * metric[-1], 0.0) + jnp.zeros_like(metric)
     vs = (metric, decay, c * A * geo_here, rate, jnp.expm1(-rate) ** 2, 1.0 / metric, low_w, high_w, c * geo_here, A)
     coef = jnp.stack(vs, axis=1)
-
-    plane = f32((3, ny, nz))
-    sends = G - 1 if direct else 0
-    outs = pl.pallas_call(
-        lambda *r: sweep_kernel(G, direct, *r),
-        out_shape=(f32(adjoint.shape), f32((2, 3, ny, nz))) + (plane,) * sends,
-        in_specs=[SMEM] + [pl.BlockSpec(memory_space=pltpu.VMEM)] * 7,
-    )(idx, adjoint, base_flow, x_before, x_after, y_before, y_after, coef)
-    sw, own = outs[0], outs[1]
-
+    sw, payload = pl.pallas_call(
+        sweep_kernel,
+        out_shape=(f32(adjoint.shape), f32((2, 3, ny, nz))),
+    )(adjoint, base_flow, x_before, x_after, y_before, y_after, coef)
+
+    direct = G <= DIRECT_LIMIT and is_pow2(G)
     if direct:
-        got = [
-            lax.ppermute(outs[1 + k], "gx", [(j, partner_of(j, k, G)) for j in range(G)])
-            for k in range(1, G)
-        ]
+        got = [lax.ppermute(payload, "gx", [(j, j ^ k) for j in range(G)]) for k in range(1, G)]
     else:
-        got = list(scan_carries(own[0], own[1], A[None, :, None], G))
-
+        got = list(scan_carries(payload[0], payload[1], A[None, :, None], G))
+    idx = jnp.reshape(i, (1,)).astype(jnp.int32)
+    nvm = 4 + len(got)
     adjoint_next, part = pl.pallas_call(
         lambda *r: finish_kernel(G, direct, *r),
         out_shape=(f32(adjoint.shape), f32((4, n, nz))),
-        in_specs=[SMEM] + [pl.BlockSpec(memory_space=pltpu.VMEM)] * (4 + len(got)),
-    )(idx, adjoint, sw, own, coef, *got)
+        in_specs=[pl.BlockSpec(memory_space=pltpu.SMEM)] + [pl.BlockSpec()] * nvm,
+    )(idx, adjoint, sw, payload, coef, *got)
 
     pieces = [part] + [
         lax.ppermute(part, "gy", [(j, partner_of(j, k, Gy)) for j in range(Gy)]) for k in range(1, Gy)

time: 51.3 us -> 50.1 us (0.977)
  local copies, waits for them, and re-layouts: 5.66 us -> 4.41 us
  waiting for transfers between devices: 9.35 us -> 9.91 us
    unnamed x28, local copies, waits for them, and re-layouts: 3.1 us -> 2.46 us
    another operation x1 -> x0, local copies, waits for them, and re-layouts: 0.62 us -> none  [local(): idx = jnp.stack([jnp.asarray(i, jnp.int32)] + sends_up + powers)]
    ppermute x7, waiting for transfers between devices: 5.83 us -> 6.38 us  [local(): lax.ppermute(payload, 'gx', [(j, j ^ k) for j in range(G)])]
  transfers between devices with their start and end apart: 14 -> 14, of which waited for: 5 -> 5; matrix products, arithmetic and copies ran while one was open for 5% -> 4% of each run, Pallas kernels for 0% -> 0%
where the time goes in v5:
time: 50.1 us; the launch traced here: 49.8 us
  starting transfers between devices  26 us (52%)
  waiting for transfers between devices  9.91 us (20%)
  Pallas kernels  6.56 us (13%)
  local copies, waits for them, and re-layouts  4.41 us (9%)
  between operations  2.17 us (4%)
  other arithmetic  0.78 us (2%)
    ppermute x7, starting transfers between devices, local(): lax.ppermute(payload, 'gx', [(j, j ^ k) for j in range(G)])  12.8 us
    ppermute x4, starting transfers between devices, shift(): return lax.ppermute(x, axis, pairs)  8.91 us
    ppermute x7, waiting for transfers between devices, local(): lax.ppermute(payload, 'gx', [(j, j ^ k) for j in range(G)])  6.38 us
    ppermute x3, starting transfers between devices, local(): lax.ppermute(part, 'gy', [(j, partner_of(j, k, Gy)) for j in range(Gy)])  4.29 us
    ppermute x3, waiting for transfers between devices, local(): lax.ppermute(part, 'gy', [(j, partner_of(j, k, Gy)) for j in range(Gy)])  3.52 us
    pallas_call x1, Pallas kernels, local(): pl.pallas_call(sweep_kernel, out_shape=(f32(adjoint.shape), f32((2, 3, ny...  2.52 us
    unnamed x28, local copies, waits for them, and re-layouts  2.46 us
    pallas_call x1, Pallas kernels, local(): pl.pallas_call(lambda *r: finish_kernel(G, direct, *r), out_shape=(f32(ad...  2.2 us
  transfers between devices with their start and end apart: 14, of which 5 were waited for; matrix products, arithmetic and copies ran while one was open for 4% of the time, Pallas kernels for 0%

profile of v5, /device:TPU:0, one launch (start us, length us, event | category | flops | bytes accessed | tf_op | source)
XLA Modules:
  0.0 49.8 jit_solution(5068260168561915146)
XLA Ops:
  0.6 1.8 %shard_map.59 = (f32[6,16,128]{2,1,0:T(8,128)}, f32[6,16,128]{2,1,0:T(8,128)}, f32[6,16,128]{2,1,0:T(8,128)}, f32[6,16,128]{2,1,0:T(8,128)}) custom-call(f32[3,16,16,128]{3,2,1,0:T(8,128)} %r_1_.1, f32[3,16,16,128]{3,2,1,0:T(8,128)} %base_ref.3), custom_call_target="tpu_custom_call" | custom-call | tf_op jit(solution)/shard_map/pallas_call | solution.py:172
  2.5 4.9 %collective-permute-start = (f32[6,16,128]{2,1,0:T(8,128)}, f32[6,16,128]{2,1,0:T(8,128)S(1)}, u32[]{:S(2)}, u32[]{:S(2)}) collective-permute-start(f32[6,16,128]{2,1,0:T(8,128)} %get-tuple-element.10), channel_id=1, source_target_pairs={{0,4},{4,8},{8,12},{12,16},{16,20},{20,24},{24,28},{1,5},{5,9},{9,... | collective-permute-start | bytes 147464 | tf_op jit(solution)/shard_map/ppermute | solution.py:18
  7.3 1.3 %collective-permute-start.1 = (f32[6,16,128]{2,1,0:T(8,128)}, f32[6,16,128]{2,1,0:T(8,128)S(1)}, u32[]{:S(2)}, u32[]{:S(2)}) collective-permute-start(f32[6,16,128]{2,1,0:T(8,128)} %get-tuple-element.11), channel_id=1, source_target_pairs={{4,0},{8,4},{12,8},{16,12},{20,16},{24,20},{28,24},{5,1},{9,5},{13... | collective-permute-start | bytes 147464 | tf_op jit(solution)/shard_map/ppermute | solution.py:18
  8.6 1.5 %collective-permute-start.2 = (f32[6,16,128]{2,1,0:T(8,128)}, f32[6,16,128]{2,1,0:T(8,128)S(1)}, u32[]{:S(2)}, u32[]{:S(2)}) collective-permute-start(f32[6,16,128]{2,1,0:T(8,128)} %get-tuple-element.12), channel_id=1, source_target_pairs={{0,1},{1,2},{2,3},{4,5},{5,6},{6,7},{8,9},{9,10},{10,11},{12,13},{... | collective-permute-start | bytes 147464 | tf_op jit(solution)/shard_map/ppermute | solution.py:18
  10.1 1.3 %collective-permute-start.3 = (f32[6,16,128]{2,1,0:T(8,128)}, f32[6,16,128]{2,1,0:T(8,128)S(1)}, u32[]{:S(2)}, u32[]{:S(2)}) collective-permute-start(f32[6,16,128]{2,1,0:T(8,128)} %get-tuple-element.13), channel_id=1, source_target_pairs={{1,0},{2,1},{3,2},{5,4},{6,5},{7,6},{9,8},{10,9},{11,10},{13,12},{... | collective-permute-start | bytes 147464 | tf_op jit(solution)/shard_map/ppermute | solution.py:18
  11.6 0.6 %copy-done.12 = f32[16]{0:T(128)S(1)} copy-done((f32[16]{0:T(128)S(1)}, f32[16]{0:T(128)}, u32[]{:S(2)}) %copy-start.12) | copy-done | bytes 88
  12.2 0.6 %fusion.3 = (f32[1]{0:T(128)}, f32[1]{0:T(128)}) fusion(f32[16]{0:T(128)S(1)} %copy-done.12), kind=kLoop, calls=%fused_computation.17 | loop fusion | bytes 16 | tf_op jit(solution)/shard_map/slice | solution.py:190
  14.8 0.7 %stack.58.coef_ref.r_4_ = f32[16,10]{1,0:T(8,128)} concatenate(f32[16,1]{1,0:T(8,128)S(1)} %copy.14, f32[16,1]{1,0:T(8,128)S(1)} %copy.15, f32[16,1]{1,0:T(8,128)S(1)} %copy.16, f32[16,1]{1,0:T(8,128)S(1)} %copy.17, f32[16,1]{1,0:T(8,128)S(1)} %copy.18, f32[16,1]{1,0:T(8,128)S(1)} %copy.19, f32[16,1]{1,0:T(8,128)S(1)} %stack.54, f32[16,1]{1,0:T(8,128)S(1)} %stack.55, ...), dimensions={1} | concatenate | bytes 1280 | tf_op jit(solution)/shard_map/stack | solution.py:192
  15.6 0.6 %copy-done.7 = f32[6,16,128]{2,1,0:T(8,128)} copy-done((f32[6,16,128]{2,1,0:T(8,128)}, f32[6,16,128]{2,1,0:T(8,128)S(1)}, u32[]{:S(2)}) %copy-start.7) | copy-done | bytes 49176
  16.1 0.6 %copy-done.10 = f32[6,16,128]{2,1,0:T(8,128)} copy-done((f32[6,16,128]{2,1,0:T(8,128)}, f32[6,16,128]{2,1,0:T(8,128)S(1)}, u32[]{:S(2)}) %copy-start.10) | copy-done | bytes 49176
  16.8 2.5 %shard_map.60 = (f32[3,16,16,128]{3,2,1,0:T(8,128)}, f32[2,3,16,128]{3,2,1,0:T(8,128)}) custom-call(f32[3,16,16,128]{3,2,1,0:T(8,128)} %r_1_.1, f32[3,16,16,128]{3,2,1,0:T(8,128)} %base_ref.3, f32[6,16,128]{2,1,0:T(8,128)} %copy-done.7, f32[6,16,128]{2,1,0:T(8,128)} %copy-done.8, f32[6,16,128]{2,1,0:T(8,128)} %copy-done.9, f32[6,16,128]{2,1,0:T(8,128)} %copy-done.10, ...), custom_call_target="tpu_custom_call" | custom-call | tf_op jit(solution)/shard_map/pallas_call | solution.py:193
  19.3 5.5 %collective-permute-start.10 = (f32[2,3,16,128]{3,2,1,0:T(8,128)}, f32[2,3,16,128]{3,2,1,0:T(8,128)S(1)}, u32[]{:S(2)}, u32[]{:S(2)}) collective-permute-start(f32[2,3,16,128]{3,2,1,0:T(8,128)} %get-tuple-element.15.r_3_), channel_id=1, source_target_pairs={{0,28},{4,24},{8,20},{12,16},{16,12},{20,8},{24,4},{28,0},{1,29},{... | collective-permute-start | bytes 147464 | tf_op jit(solution)/shard_map/ppermute | solution.py:200
  24.8 1.4 %collective-permute-start.4 = (f32[2,3,16,128]{3,2,1,0:T(8,128)}, f32[2,3,16,128]{3,2,1,0:T(8,128)S(1)}, u32[]{:S(2)}, u32[]{:S(2)}) collective-permute-start(f32[2,3,16,128]{3,2,1,0:T(8,128)} %get-tuple-element.15.r_3_), channel_id=1, source_target_pairs={{0,4},{4,0},{8,12},{12,8},{16,20},{20,16},{24,28},{28,24},{1,5},{5... | collective-permute-start | bytes 147464 | tf_op jit(solution)/shard_map/ppermute | solution.py:200
  26.2 2.0 %collective-permute-start.6 = (f32[2,3,16,128]{3,2,1,0:T(8,128)}, f32[2,3,16,128]{3,2,1,0:T(8,128)S(1)}, u32[]{:S(2)}, u32[]{:S(2)}) collective-permute-start(f32[2,3,16,128]{3,2,1,0:T(8,128)} %get-tuple-element.15.r_3_), channel_id=1, source_target_pairs={{0,12},{4,8},{8,4},{12,0},{16,28},{20,24},{24,20},{28,16},{1,13},{... | collective-permute-start | bytes 147464 | tf_op jit(solution)/shard_map/ppermute | solution.py:200
  28.3 3.8 %collective-permute-start.8 = (f32[2,3,16,128]{3,2,1,0:T(8,128)}, f32[2,3,16,128]{3,2,1,0:T(8,128)S(1)}, u32[]{:S(2)}, u32[]{:S(2)}) collective-permute-start(f32[2,3,16,128]{3,2,1,0:T(8,128)} %get-tuple-element.15.r_3_), channel_id=1, source_target_pairs={{0,20},{4,16},{8,28},{12,24},{16,4},{20,0},{24,12},{28,8},{1,21},{... | collective-permute-start | bytes 147464 | tf_op jit(solution)/shard_map/ppermute | solution.py:200
  32.1 1.4 %collective-permute-done.7.r_8_ = f32[2,3,16,128]{3,2,1,0:T(8,128)S(1)} collective-permute-done((f32[2,3,16,128]{3,2,1,0:T(8,128)}, f32[2,3,16,128]{3,2,1,0:T(8,128)S(1)}, u32[]{:S(2)}, u32[]{:S(2)}) %collective-permute-start.7) | collective-permute-done | bytes 49184 | tf_op jit(solution)/shard_map/ppermute | solution.py:200
  33.5 3.7 %collective-permute-done.8.r_9_ = f32[2,3,16,128]{3,2,1,0:T(8,128)S(1)} collective-permute-done((f32[2,3,16,128]{3,2,1,0:T(8,128)}, f32[2,3,16,128]{3,2,1,0:T(8,128)S(1)}, u32[]{:S(2)}, u32[]{:S(2)}) %collective-permute-start.8) | collective-permute-done | bytes 49184 | tf_op jit(solution)/shard_map/ppermute | solution.py:200
  37.2 1.4 %collective-permute-done.9.r_10_ = f32[2,3,16,128]{3,2,1,0:T(8,128)S(1)} collective-permute-done((f32[2,3,16,128]{3,2,1,0:T(8,128)}, f32[2,3,16,128]{3,2,1,0:T(8,128)S(1)}, u32[]{:S(2)}, u32[]{:S(2)}) %collective-permute-start.9) | collective-permute-done | bytes 49184 | tf_op jit(solution)/shard_map/ppermute | solution.py:200
  38.6 0.6 %copy-done.6 = f32[2,3,16,128]{3,2,1,0:T(8,128)} copy-done((f32[2,3,16,128]{3,2,1,0:T(8,128)}, f32[2,3,16,128]{3,2,1,0:T(8,128)S(1)}, u32[]{:S(2)}) %copy-start.6) | copy-done | bytes 49176
  39.1 2.2 %shard_map.61 = (f32[3,16,16,128]{3,2,1,0:T(8,128)}, f32[4,16,128]{2,1,0:T(8,128)}) custom-call(s32[1]{0:T(128)} %bitcast.r_0_, f32[3,16,16,128]{3,2,1,0:T(8,128)} %r_1_.1, f32[3,16,16,128]{3,2,1,0:T(8,128)} %get-tuple-element.14.r_2_, f32[2,3,16,128]{3,2,1,0:T(8,128)} %get-tuple-element.15.r_3_, f32[16,10]{1,0:T(8,128)} %stack.58.coef_ref.r_4_, ...), custom_call_target="tpu_custom_call" | custom-call | tf_op jit(solution)/shard_map/pallas_call | solution.py:205
  41.6 4.0 %collective-permute-start.12 = (f32[4,16,128]{2,1,0:T(8,128)}, f32[4,16,128]{2,1,0:T(8,128)S(1)}, u32[]{:S(2)}, u32[]{:S(2)}) collective-permute-start(f32[4,16,128]{2,1,0:T(8,128)} %get-tuple-element.17), channel_id=1, source_target_pairs={{0,2},{1,3},{2,0},{3,1},{4,6},{5,7},{6,4},{7,5},{8,10},{9,11},{10,... | collective-permute-start | bytes 98312 | tf_op jit(solution)/shard_map/ppermute | solution.py:212
  45.6 2.2 %collective-permute-done.12 = f32[4,16,128]{2,1,0:T(8,128)S(1)} collective-permute-done((f32[4,16,128]{2,1,0:T(8,128)}, f32[4,16,128]{2,1,0:T(8,128)S(1)}, u32[]{:S(2)}, u32[]{:S(2)}) %collective-permute-start.12) | collective-permute-done | bytes 32800 | tf_op jit(solution)/shard_map/ppermute | solution.py:212
  47.8 1.4 %collective-permute-done.13 = f32[4,16,128]{2,1,0:T(8,128)S(1)} collective-permute-done((f32[4,16,128]{2,1,0:T(8,128)}, f32[4,16,128]{2,1,0:T(8,128)S(1)}, u32[]{:S(2)}, u32[]{:S(2)}) %collective-permute-start.13) | collective-permute-done | bytes 32800 | tf_op jit(solution)/shard_map/ppermute | solution.py:212
  49.2 0.6 %fusion = f32[2,16,128]{2,1,0:T(8,128)} fusion(f32[1,4,16,128]{3,2,1,0:T(8,128)S(1)} %dynamic-slice_add_fusion, f32[16,128]{1,0:T(8,128)S(1)} %fusion.1), kind=kLoop, calls=%fused_computation.3 | loop fusion | flops 4096 | bytes 40960 | tf_op jit(solution)/shard_map/add | solution.py:220
  (56 shorter events, 1.2 us)
Async XLA Ops:
  2.5 13.0 %collective-permute-start = (f32[6,16,128]{2,1,0:T(8,128)}, f32[6,16,128]{2,1,0:T(8,128)S(1)}, u32[]{:S(2)}, u32[]{:S(2)}) collective-permute-start(f32[6,16,128]{2,1,0:T(8,128)} %get-tuple-element.10), channel_id=1, source_target_pairs={{0,4},{4,8},{8,12},{12,16},{16,20},{20,24},{24,28},{1,5},{5,9},{9,... | collective-permute-start | bytes 147464 | tf_op jit(solution)/shard_map/ppermute | solution.py:18
  7.3 8.2 %collective-permute-start.1 = (f32[6,16,128]{2,1,0:T(8,128)}, f32[6,16,128]{2,1,0:T(8,128)S(1)}, u32[]{:S(2)}, u32[]{:S(2)}) collective-permute-start(f32[6,16,128]{2,1,0:T(8,128)} %get-tuple-element.11), channel_id=1, source_target_pairs={{4,0},{8,4},{12,8},{16,12},{20,16},{24,20},{28,24},{5,1},{9,5},{13... | collective-permute-start | bytes 147464 | tf_op jit(solution)/shard_map/ppermute | solution.py:18
  8.6 6.9 %collective-permute-start.2 = (f32[6,16,128]{2,1,0:T(8,128)}, f32[6,16,128]{2,1,0:T(8,128)S(1)}, u32[]{:S(2)}, u32[]{:S(2)}) collective-permute-start(f32[6,16,128]{2,1,0:T(8,128)} %get-tuple-element.12), channel_id=1, source_target_pairs={{0,1},{1,2},{2,3},{4,5},{5,6},{6,7},{8,9},{9,10},{10,11},{12,13},{... | collective-permute-start | bytes 147464 | tf_op jit(solution)/shard_map/ppermute | solution.py:18
  10.1 1.3 %copy-start.13 = (f32[16]{0:T(128)S(1)}, f32[16]{0:T(128)}, u32[]{:S(2)}) copy-start(f32[16]{0:T(128)} %param.7) | copy-start | bytes 196
  10.1 5.4 %collective-permute-start.3 = (f32[6,16,128]{2,1,0:T(8,128)}, f32[6,16,128]{2,1,0:T(8,128)S(1)}, u32[]{:S(2)}, u32[]{:S(2)}) collective-permute-start(f32[6,16,128]{2,1,0:T(8,128)} %get-tuple-element.13), channel_id=1, source_target_pairs={{1,0},{2,1},{3,2},{5,4},{6,5},{7,6},{9,8},{10,9},{11,10},{13,12},{... | collective-permute-start | bytes 147464 | tf_op jit(solution)/shard_map/ppermute | solution.py:18
  11.6 0.7 %copy-start.12 = (f32[16]{0:T(128)S(1)}, f32[16]{0:T(128)}, u32[]{:S(2)}) copy-start(f32[16]{0:T(128)} %param.6) | copy-start | bytes 196
  15.5 0.6 %copy-start.8 = (f32[6,16,128]{2,1,0:T(8,128)}, f32[6,16,128]{2,1,0:T(8,128)S(1)}, u32[]{:S(2)}) copy-start(f32[6,16,128]{2,1,0:T(8,128)S(1)} %collective-permute-done.1.xhi_ref) | copy-start | bytes 147460
  19.3 9.0 %collective-permute-start.10 = (f32[2,3,16,128]{3,2,1,0:T(8,128)}, f32[2,3,16,128]{3,2,1,0:T(8,128)S(1)}, u32[]{:S(2)}, u32[]{:S(2)}) collective-permute-start(f32[2,3,16,128]{3,2,1,0:T(8,128)} %get-tuple-element.15.r_3_), channel_id=1, source_target_pairs={{0,28},{4,24},{8,20},{12,16},{16,12},{20,8},{24,4},{28,0},{1,29},{... | collective-permute-start | bytes 147464 | tf_op jit(solution)/shard_map/ppermute | solution.py:200
  24.8 7.3 %collective-permute-start.4 = (f32[2,3,16,128]{3,2,1,0:T(8,128)}, f32[2,3,16,128]{3,2,1,0:T(8,128)S(1)}, u32[]{:S(2)}, u32[]{:S(2)}) collective-permute-start(f32[2,3,16,128]{3,2,1,0:T(8,128)} %get-tuple-element.15.r_3_), channel_id=1, source_target_pairs={{0,4},{4,0},{8,12},{12,8},{16,20},{20,16},{24,28},{28,24},{1,5},{5... | collective-permute-start | bytes 147464 | tf_op jit(solution)/shard_map/ppermute | solution.py:200
  26.2 5.9 %collective-permute-start.5 = (f32[2,3,16,128]{3,2,1,0:T(8,128)}, f32[2,3,16,128]{3,2,1,0:T(8,128)S(1)}, u32[]{:S(2)}, u32[]{:S(2)}) collective-permute-start(f32[2,3,16,128]{3,2,1,0:T(8,128)} %get-tuple-element.15.r_3_), channel_id=1, source_target_pairs={{0,8},{4,12},{8,0},{12,4},{16,24},{20,28},{24,16},{28,20},{1,9},{5... | collective-permute-start | bytes 147464 | tf_op jit(solution)/shard_map/ppermute | solution.py:200
  26.2 5.9 %collective-permute-start.6 = (f32[2,3,16,128]{3,2,1,0:T(8,128)}, f32[2,3,16,128]{3,2,1,0:T(8,128)S(1)}, u32[]{:S(2)}, u32[]{:S(2)}) collective-permute-start(f32[2,3,16,128]{3,2,1,0:T(8,128)} %get-tuple-element.15.r_3_), channel_id=1, source_target_pairs={{0,12},{4,8},{8,4},{12,0},{16,28},{20,24},{24,20},{28,16},{1,13},{... | collective-permute-start | bytes 147464 | tf_op jit(solution)/shard_map/ppermute | solution.py:200
  28.3 5.2 %collective-permute-start.7 = (f32[2,3,16,128]{3,2,1,0:T(8,128)}, f32[2,3,16,128]{3,2,1,0:T(8,128)S(1)}, u32[]{:S(2)}, u32[]{:S(2)}) collective-permute-start(f32[2,3,16,128]{3,2,1,0:T(8,128)} %get-tuple-element.15.r_3_), channel_id=1, source_target_pairs={{0,16},{4,20},{8,24},{12,28},{16,0},{20,4},{24,8},{28,12},{1,17},{... | collective-permute-start | bytes 147464 | tf_op jit(solution)/shard_map/ppermute | solution.py:200
  28.3 10.2 %copy-start = (f32[2,3,16,128]{3,2,1,0:T(8,128)}, f32[2,3,16,128]{3,2,1,0:T(8,128)S(1)}, u32[]{:S(2)}) copy-start(f32[2,3,16,128]{3,2,1,0:T(8,128)S(1)} %collective-permute-done.10.r_11_) | copy-start | bytes 147460
  28.3 8.9 %collective-permute-start.8 = (f32[2,3,16,128]{3,2,1,0:T(8,128)}, f32[2,3,16,128]{3,2,1,0:T(8,128)S(1)}, u32[]{:S(2)}, u32[]{:S(2)}) collective-permute-start(f32[2,3,16,128]{3,2,1,0:T(8,128)} %get-tuple-element.15.r_3_), channel_id=1, source_target_pairs={{0,20},{4,16},{8,28},{12,24},{16,4},{20,0},{24,12},{28,8},{1,21},{... | collective-permute-start | bytes 147464 | tf_op jit(solution)/shard_map/ppermute | solution.py:200
  32.1 6.4 %copy-start.1 = (f32[2,3,16,128]{3,2,1,0:T(8,128)}, f32[2,3,16,128]{3,2,1,0:T(8,128)S(1)}, u32[]{:S(2)}) copy-start(f32[2,3,16,128]{3,2,1,0:T(8,128)S(1)} %collective-permute-done.4.r_5_) | copy-start | bytes 147460
  32.1 6.4 %collective-permute-start.9 = (f32[2,3,16,128]{3,2,1,0:T(8,128)}, f32[2,3,16,128]{3,2,1,0:T(8,128)S(1)}, u32[]{:S(2)}, u32[]{:S(2)}) collective-permute-start(f32[2,3,16,128]{3,2,1,0:T(8,128)} %get-tuple-element.15.r_3_), channel_id=1, source_target_pairs={{0,24},{4,28},{8,16},{12,20},{16,8},{20,12},{24,0},{28,4},{1,25},{... | collective-permute-start | bytes 147464 | tf_op jit(solution)/shard_map/ppermute | solution.py:200
  32.1 6.4 %copy-start.2 = (f32[2,3,16,128]{3,2,1,0:T(8,128)}, f32[2,3,16,128]{3,2,1,0:T(8,128)S(1)}, u32[]{:S(2)}) copy-start(f32[2,3,16,128]{3,2,1,0:T(8,128)S(1)} %collective-permute-done.5.r_6_) | copy-start | bytes 147460
  32.1 6.4 %copy-start.3 = (f32[2,3,16,128]{3,2,1,0:T(8,128)}, f32[2,3,16,128]{3,2,1,0:T(8,128)S(1)}, u32[]{:S(2)}) copy-start(f32[2,3,16,128]{3,2,1,0:T(8,128)S(1)} %collective-permute-done.6.r_7_) | copy-start | bytes 147460
  33.5 5.1 %copy-start.4 = (f32[2,3,16,128]{3,2,1,0:T(8,128)}, f32[2,3,16,128]{3,2,1,0:T(8,128)S(1)}, u32[]{:S(2)}) copy-start(f32[2,3,16,128]{3,2,1,0:T(8,128)S(1)} %collective-permute-done.7.r_8_) | copy-start | bytes 147460
  37.2 1.4 %copy-start.5 = (f32[2,3,16,128]{3,2,1,0:T(8,128)}, f32[2,3,16,128]{3,2,1,0:T(8,128)S(1)}, u32[]{:S(2)}) copy-start(f32[2,3,16,128]{3,2,1,0:T(8,128)S(1)} %collective-permute-done.8.r_9_) | copy-start | bytes 147460
  41.3 7.8 %copy-start.11 = (f32[4,16,128]{2,1,0:T(8,128)S(1)}, f32[4,16,128]{2,1,0:T(8,128)}, u32[]{:S(2)}) copy-start(f32[4,16,128]{2,1,0:T(8,128)} %get-tuple-element.17) | copy-start | bytes 98308
  41.3 4.3 %collective-permute-start.11 = (f32[4,16,128]{2,1,0:T(8,128)}, f32[4,16,128]{2,1,0:T(8,128)S(1)}, u32[]{:S(2)}, u32[]{:S(2)}) collective-permute-start(f32[4,16,128]{2,1,0:T(8,128)} %get-tuple-element.17), channel_id=1, source_target_pairs={{0,1},{1,0},{2,3},{3,2},{4,5},{5,4},{6,7},{7,6},{8,9},{9,8},{10,11... | collective-permute-start | bytes 98312 | tf_op jit(solution)/shard_map/ppermute | solution.py:212
  41.6 6.2 %collective-permute-start.12 = (f32[4,16,128]{2,1,0:T(8,128)}, f32[4,16,128]{2,1,0:T(8,128)S(1)}, u32[]{:S(2)}, u32[]{:S(2)}) collective-permute-start(f32[4,16,128]{2,1,0:T(8,128)} %get-tuple-element.17), channel_id=1, source_target_pairs={{0,2},{1,3},{2,0},{3,1},{4,6},{5,7},{6,4},{7,5},{8,10},{9,11},{10,... | collective-permute-start | bytes 98312 | tf_op jit(solution)/shard_map/ppermute | solution.py:212
  45.6 3.6 %collective-permute-start.13 = (f32[4,16,128]{2,1,0:T(8,128)}, f32[4,16,128]{2,1,0:T(8,128)S(1)}, u32[]{:S(2)}, u32[]{:S(2)}) collective-permute-start(f32[4,16,128]{2,1,0:T(8,128)} %get-tuple-element.17), channel_id=1, source_target_pairs={{0,3},{1,2},{2,1},{3,0},{4,7},{5,6},{6,5},{7,4},{8,11},{9,10},{10,... | collective-permute-start | bytes 98312 | tf_op jit(solution)/shard_map/ppermute | solution.py:212
  (4 other events, 2.5 us)

commit v6 on v5

--- a/solution.py
+++ b/solution.py
@@ -23,7 +23,7 @@
 
 
 def column(ref, k, ny, nz):
-    return jnp.broadcast_to(ref[:, k : k + 1], (ny, nz))
+    return ref[k]
 
 
 def is_pow2(size):
@@ -42,8 +42,15 @@
     return (g - s) % size
 
 
-def edges_kernel(adj_ref, base_ref, xlo_ref, xhi_ref, ylo_ref, yhi_ref):
-    n, ny = adj_ref.shape[1], adj_ref.shape[2]
+def expm1(x):
+    t = jnp.ones_like(x)
+    for k in range(12, 1, -1):
+        t = 1.0 + x * t / k
+    return jnp.where(jnp.abs(x) < 0.5, x * t, jnp.exp(x) - 1.0)
+
+
+def edges_kernel(metric_ref, smooth_ref, adj_ref, base_ref, xlo_ref, xhi_ref, ylo_ref, yhi_ref, coef_ref):
+    n, ny, nz = adj_ref.shape[1], adj_ref.shape[2], adj_ref.shape[3]
     for k in range(6):
         ref, c = (adj_ref, k) if k < 3 else (base_ref, k - 3)
         xlo_ref[k] = ref[c, 0]
@@ -51,6 +58,30 @@
         for x in range(n):
             ylo_ref[k, x : x + 1, :] = ref[c, x, 0:1, :]
             yhi_ref[k, x : x + 1, :] = ref[c, x, ny - 1 : ny, :]
+    G, i = lax.axis_size("gx"), lax.axis_index("gx")
+    Gy, g = lax.axis_size("gy"), lax.axis_index("gy")
+    row = lax.broadcasted_iota(jnp.int32, (ny, nz), 0)
+    metric = jnp.zeros((ny, nz), jnp.float32)
+    smooth = jnp.zeros((ny, nz), jnp.float32)
+    for y in range(ny):
+        metric = jnp.where(row == y, metric_ref[y], metric)
+        smooth = jnp.where(row == y, smooth_ref[y], smooth)
+    rate = 1.0 / (CX * smooth)
+    decay = jnp.exp(-rate)
+    ratio = jnp.exp(-n * rate)
+    c = None
+    for k in range(n):
+        term = jnp.exp(-(2.0 * k + 1.0) * rate)
+        c = term if c is None else c + term
+    downstream = (G - 1 - i).astype(jnp.float32)
+    geo_here = expm1(-2.0 * n * downstream * rate) / expm1(-2.0 * n * rate)
+    low = jnp.where(g == 0, 2.0 * metric_ref[0], 0.0)
+    high = jnp.where(g == Gy - 1, -2.0 * metric_ref[ny - 1], 0.0)
+    shrink = expm1(-rate)
+    rows = (metric, decay, c * ratio * geo_here, rate, shrink * shrink, 1.0 / metric,
+            jnp.broadcast_to(low, (ny, nz)), jnp.broadcast_to(high, (ny, nz)), c * geo_here, ratio)
+    for k, v in enumerate(rows):
+        coef_ref[k] = v
 
 
 def sweep_kernel(adj_ref, base_ref, xlo_ref, xhi_ref, ylo_ref, yhi_ref, coef_ref, sw_ref, pay_ref):
@@ -100,7 +131,7 @@
         pay_ref[1, c] = back[c] + gain * forward[c]
 
 
-def finish_kernel(G, direct, idx_ref, adj_ref, sw_ref, pay_ref, coef_ref, *rest):
+def finish_kernel(G, direct, adj_ref, sw_ref, pay_ref, coef_ref, *rest):
     n, ny, nz = adj_ref.shape[1], adj_ref.shape[2], adj_ref.shape[3]
     out_ref, part_ref = rest[-2], rest[-1]
     got = rest[:-2]
@@ -113,7 +144,7 @@
     near = column(coef_ref, 8, ny, nz)
     ratio = column(coef_ref, 9, ny, nz)
     block_rate = n * rate
-    i = idx_ref[0]
+    i = lax.axis_index("gx")
     inflow, later = [], []
     if direct:
         weights = []
@@ -169,27 +200,17 @@
     Gy, g = lax.axis_size("gy"), lax.axis_index("gy")
     _, n, ny, nz = adjoint.shape
 
-    xlo, xhi, ylo, yhi = pl.pallas_call(
+    smem = pl.BlockSpec(memory_space=pltpu.SMEM)
+    xlo, xhi, ylo, yhi, coef = pl.pallas_call(
         edges_kernel,
-        out_shape=(f32((6, ny, nz)), f32((6, ny, nz)), f32((6, n, nz)), f32((6, n, nz))),
-    )(adjoint, base_flow)
+        out_shape=(f32((6, ny, nz)), f32((6, ny, nz)), f32((6, n, nz)), f32((6, n, nz)), f32((10, ny, nz))),
+        in_specs=[smem, smem, pl.BlockSpec(), pl.BlockSpec()],
+    )(metric, smoothing, adjoint, base_flow)
     x_before = shift(xhi, "gx", G, 1)
     x_after = shift(xlo, "gx", G, -1)
     y_before = shift(yhi, "gy", Gy, 1)
     y_after = shift(ylo, "gy", Gy, -1)
 
-    rate = 1.0 / (CX * smoothing)
-    decay = jnp.exp(-rate)
-    A = jnp.exp(-n * rate)
-    c = jnp.sum(jnp.exp(-(2.0 * jnp.arange(n, dtype=jnp.float32)[:, None] + 1.0) * rate[None, :]), axis=0)
-    two_block = jnp.expm1(-2.0 * n * rate)
-    downstream = (G - 1 - i).astype(jnp.float32)
-    geo_here = jnp.expm1(-2.0 * n * downstream * rate) / two_block
-
-    low_w = jnp.where(g == 0, 2.0 * metric[0], 0.0) + jnp.zeros_like(metric)
-    high_w = jnp.where(g == Gy - 1, -2.0 * metric[-1], 0.0) + jnp.zeros_like(metric)
-    vs = (metric, decay, c * A * geo_here, rate, jnp.expm1(-rate) ** 2, 1.0 / metric, low_w, high_w, c * geo_here, A)
-    coef = jnp.stack(vs, axis=1)
     sw, payload = pl.pallas_call(
         sweep_kernel,
         out_shape=(f32(adjoint.shape), f32((2, 3, ny, nz))),
@@ -199,22 +220,20 @@
     if direct:
         got = [lax.ppermute(payload, "gx", [(j, j ^ k) for j in range(G)]) for k in range(1, G)]
     else:
-        got = list(scan_carries(payload[0], payload[1], A[None, :, None], G))
-    idx = jnp.reshape(i, (1,)).astype(jnp.int32)
-    nvm = 4 + len(got)
+        A = coef[9]
+        got = list(scan_carries(payload[0], payload[1], A[None], G))
     adjoint_next, part = pl.pallas_call(
         lambda *r: finish_kernel(G, direct, *r),
         out_shape=(f32(adjoint.shape), f32((4, n, nz))),
-        in_specs=[pl.BlockSpec(memory_space=pltpu.SMEM)] + [pl.BlockSpec()] * nvm,
-    )(idx, adjoint, sw, payload, coef, *got)
+    )(adjoint, sw, payload, coef, *got)
 
     pieces = [part] + [
-        lax.ppermute(part, "gy", [(j, partner_of(j, k, Gy)) for j in range(Gy)]) for k in range(1, Gy)
+        lax.ppermute(part, "gy", [(j, (j + k) % Gy) for j in range(Gy)]) for k in range(1, Gy)
     ]
     stacked = jnp.stack(pieces)
     total = None
     for s in range(Gy):
-        piece = lax.dynamic_index_in_dim(stacked, slot_of(g, s, Gy), axis=0, keepdims=False)
+        piece = lax.dynamic_index_in_dim(stacked, (g - s) % Gy, axis=0, keepdims=False)
         total = piece if total is None else total + piece
     bulk_mean = total[2] / total[3]
     wall_gradient = total[:2] + bulk_mean[None]

time: 50.1 us -> 47.2 us (0.942)
  local copies, waits for them, and re-layouts: 4.41 us -> 1.22 us
  waiting for transfers between devices: 9.91 us -> 12 us
  between operations: 2.17 us -> 0.78 us
    ppermute x4, waiting for transfers between devices: 0.01 us -> 3.6 us  [shift(): return lax.ppermute(x, axis, pairs)]
    ppermute x3, waiting for transfers between devices: 3.52 us -> 1.91 us  [local(): lax.ppermute(part, 'gy', [(j, (j + k) % Gy) for j in range(Gy)])]
    another operation x11 -> x0, local copies, waits for them, and re-layouts: 1.35 us -> none  [local(): coef = jnp.stack(vs, axis=1)]
    unnamed x28 -> x24, local copies, waits for them, and re-layouts: 2.46 us -> 1.22 us
    slice x1 -> x0, local copies, waits for them, and re-layouts: 0.59 us -> none  [local(): metric[-1]]
  transfers between devices with their start and end apart: 14 -> 14, of which waited for: 5 -> 7; matrix products, arithmetic and copies ran while one was open for 4% -> 0% of each run, Pallas kernels for 0% -> 0%
where the time goes in v6:
time: 47.2 us; the launch traced here: 46.9 us
  starting transfers between devices  25.7 us (54%)
  waiting for transfers between devices  12 us (25%)
  Pallas kernels  6.62 us (14%)
  local copies, waits for them, and re-layouts  1.22 us (3%)
  between operations  0.78 us (2%)
  other arithmetic  0.64 us (1%)
    ppermute x7, starting transfers between devices, local(): lax.ppermute(payload, 'gx', [(j, j ^ k) for j in range(G)])  13 us
    ppermute x4, starting transfers between devices, shift(): return lax.ppermute(x, axis, pairs)  8.91 us
    ppermute x7, waiting for transfers between devices, local(): lax.ppermute(payload, 'gx', [(j, j ^ k) for j in range(G)])  6.48 us
    ppermute x3, starting transfers between devices, local(): lax.ppermute(part, 'gy', [(j, (j + k) % Gy) for j in range(Gy)])  3.8 us
    ppermute x4, waiting for transfers between devices, shift(): return lax.ppermute(x, axis, pairs)  3.6 us
    pallas_call x1, Pallas kernels, local(): pl.pallas_call(sweep_kernel, out_shape=(f32(adjoint.shape), f32((2, 3, ny...  2.56 us
    pallas_call x1, Pallas kernels, local(): pl.pallas_call(lambda *r: finish_kernel(G, direct, *r), out_shape=(f32(ad...  2.15 us
    pallas_call x1, Pallas kernels, local(): pl.pallas_call(edges_kernel, out_shape=(f32((6, ny, nz)), f32((6, ny, nz)...  1.91 us
  transfers between devices with their start and end apart: 14, of which 7 were waited for; matrix products, arithmetic and copies ran while one was open for 0% of the time, Pallas kernels for 0%

profile of v6, /device:TPU:0, one launch (start us, length us, event | category | flops | bytes accessed | tf_op | source)
XLA Modules:
  0.0 46.9 jit_solution(3232980799976051139)
XLA Ops:
  0.6 1.9 %shard_map.59 = (f32[6,16,128]{2,1,0:T(8,128)}, f32[6,16,128]{2,1,0:T(8,128)}, f32[6,16,128]{2,1,0:T(8,128)}, f32[6,16,128]{2,1,0:T(8,128)}, f32[10,16,128]{2,1,0:T(8,128)}) custom-call(f32[16]{0:T(128)} %metric_ref.1, f32[16]{0:T(128)} %smooth_ref.1, f32[3,16,16,128]{3,2,1,0:T(8,128)} %r_0_.1, f32[3,16,16,128]{3,2,1,0:T(8,128)} %base_ref.3), custom_call_target="tpu_custom_call" | custom-call | tf_op jit(solution)/shard_map/pallas_call | solution.py:204
  2.5 4.9 %collective-permute-start = (f32[6,16,128]{2,1,0:T(8,128)}, f32[6,16,128]{2,1,0:T(8,128)S(1)}, u32[]{:S(2)}, u32[]{:S(2)}) collective-permute-start(f32[6,16,128]{2,1,0:T(8,128)} %get-tuple-element.11), channel_id=1, source_target_pairs={{0,4},{4,8},{8,12},{12,16},{16,20},{20,24},{24,28},{1,5},{5,9},{9,... | collective-permute-start | bytes 147464 | tf_op jit(solution)/shard_map/ppermute | solution.py:18
  7.4 1.3 %collective-permute-start.1 = (f32[6,16,128]{2,1,0:T(8,128)}, f32[6,16,128]{2,1,0:T(8,128)S(1)}, u32[]{:S(2)}, u32[]{:S(2)}) collective-permute-start(f32[6,16,128]{2,1,0:T(8,128)} %get-tuple-element.12), channel_id=1, source_target_pairs={{4,0},{8,4},{12,8},{16,12},{20,16},{24,20},{28,24},{5,1},{9,5},{13... | collective-permute-start | bytes 147464 | tf_op jit(solution)/shard_map/ppermute | solution.py:18
  8.7 1.5 %collective-permute-start.2 = (f32[6,16,128]{2,1,0:T(8,128)}, f32[6,16,128]{2,1,0:T(8,128)S(1)}, u32[]{:S(2)}, u32[]{:S(2)}) collective-permute-start(f32[6,16,128]{2,1,0:T(8,128)} %get-tuple-element.13), channel_id=1, source_target_pairs={{0,1},{1,2},{2,3},{4,5},{5,6},{6,7},{8,9},{9,10},{10,11},{12,13},{... | collective-permute-start | bytes 147464 | tf_op jit(solution)/shard_map/ppermute | solution.py:18
  10.2 1.3 %collective-permute-start.3 = (f32[6,16,128]{2,1,0:T(8,128)}, f32[6,16,128]{2,1,0:T(8,128)S(1)}, u32[]{:S(2)}, u32[]{:S(2)}) collective-permute-start(f32[6,16,128]{2,1,0:T(8,128)} %get-tuple-element.14), channel_id=1, source_target_pairs={{1,0},{2,1},{3,2},{5,4},{6,5},{7,6},{9,8},{10,9},{11,10},{13,12},{... | collective-permute-start | bytes 147464 | tf_op jit(solution)/shard_map/ppermute | solution.py:18
  11.5 2.1 %collective-permute-done.1.xhi_ref = f32[6,16,128]{2,1,0:T(8,128)S(1)} collective-permute-done((f32[6,16,128]{2,1,0:T(8,128)}, f32[6,16,128]{2,1,0:T(8,128)S(1)}, u32[]{:S(2)}, u32[]{:S(2)}) %collective-permute-start.1) | collective-permute-done | bytes 49184 | tf_op jit(solution)/shard_map/ppermute | solution.py:18
  13.6 1.5 %collective-permute-done.3.yhi_ref = f32[6,16,128]{2,1,0:T(8,128)S(1)} collective-permute-done((f32[6,16,128]{2,1,0:T(8,128)}, f32[6,16,128]{2,1,0:T(8,128)S(1)}, u32[]{:S(2)}, u32[]{:S(2)}) %collective-permute-start.3) | collective-permute-done | bytes 49184 | tf_op jit(solution)/shard_map/ppermute | solution.py:18
  15.1 0.6 %copy-done.10 = f32[6,16,128]{2,1,0:T(8,128)} copy-done((f32[6,16,128]{2,1,0:T(8,128)}, f32[6,16,128]{2,1,0:T(8,128)S(1)}, u32[]{:S(2)}) %copy-start.10) | copy-done | bytes 49176
  15.7 2.6 %shard_map.60 = (f32[3,16,16,128]{3,2,1,0:T(8,128)}, f32[2,3,16,128]{3,2,1,0:T(8,128)}) custom-call(f32[3,16,16,128]{3,2,1,0:T(8,128)} %r_0_.1, f32[3,16,16,128]{3,2,1,0:T(8,128)} %base_ref.3, f32[6,16,128]{2,1,0:T(8,128)} %copy-done.6, f32[6,16,128]{2,1,0:T(8,128)} %copy-done.7, f32[6,16,128]{2,1,0:T(8,128)} %copy-done.9, f32[6,16,128]{2,1,0:T(8,128)} %copy-done.10, ...), custom_call_target="tpu_custom_call" | custom-call | tf_op jit(solution)/shard_map/pallas_call | solution.py:214
  18.3 5.7 %collective-permute-start.10 = (f32[2,3,16,128]{3,2,1,0:T(8,128)}, f32[2,3,16,128]{3,2,1,0:T(8,128)S(1)}, u32[]{:S(2)}, u32[]{:S(2)}) collective-permute-start(f32[2,3,16,128]{3,2,1,0:T(8,128)} %get-tuple-element.17.r_2_), channel_id=1, source_target_pairs={{0,28},{4,24},{8,20},{12,16},{16,12},{20,8},{24,4},{28,0},{1,29},{... | collective-permute-start | bytes 147464 | tf_op jit(solution)/shard_map/ppermute | solution.py:221
  24.0 1.4 %collective-permute-start.4 = (f32[2,3,16,128]{3,2,1,0:T(8,128)}, f32[2,3,16,128]{3,2,1,0:T(8,128)S(1)}, u32[]{:S(2)}, u32[]{:S(2)}) collective-permute-start(f32[2,3,16,128]{3,2,1,0:T(8,128)} %get-tuple-element.17.r_2_), channel_id=1, source_target_pairs={{0,4},{4,0},{8,12},{12,8},{16,20},{20,16},{24,28},{28,24},{1,5},{5... | collective-permute-start | bytes 147464 | tf_op jit(solution)/shard_map/ppermute | solution.py:221
  25.4 2.0 %collective-permute-start.6 = (f32[2,3,16,128]{3,2,1,0:T(8,128)}, f32[2,3,16,128]{3,2,1,0:T(8,128)S(1)}, u32[]{:S(2)}, u32[]{:S(2)}) collective-permute-start(f32[2,3,16,128]{3,2,1,0:T(8,128)} %get-tuple-element.17.r_2_), channel_id=1, source_target_pairs={{0,12},{4,8},{8,4},{12,0},{16,28},{20,24},{24,20},{28,16},{1,13},{... | collective-permute-start | bytes 147464 | tf_op jit(solution)/shard_map/ppermute | solution.py:221
  27.5 3.8 %collective-permute-start.8 = (f32[2,3,16,128]{3,2,1,0:T(8,128)}, f32[2,3,16,128]{3,2,1,0:T(8,128)S(1)}, u32[]{:S(2)}, u32[]{:S(2)}) collective-permute-start(f32[2,3,16,128]{3,2,1,0:T(8,128)} %get-tuple-element.17.r_2_), channel_id=1, source_target_pairs={{0,20},{4,16},{8,28},{12,24},{16,4},{20,0},{24,12},{28,8},{1,21},{... | collective-permute-start | bytes 147464 | tf_op jit(solution)/shard_map/ppermute | solution.py:221
  31.3 2.4 %collective-permute-done.7.r_7_ = f32[2,3,16,128]{3,2,1,0:T(8,128)S(1)} collective-permute-done((f32[2,3,16,128]{3,2,1,0:T(8,128)}, f32[2,3,16,128]{3,2,1,0:T(8,128)S(1)}, u32[]{:S(2)}, u32[]{:S(2)}) %collective-permute-start.7) | collective-permute-done | bytes 49184 | tf_op jit(solution)/shard_map/ppermute | solution.py:221
  33.7 2.6 %collective-permute-done.8.r_8_ = f32[2,3,16,128]{3,2,1,0:T(8,128)S(1)} collective-permute-done((f32[2,3,16,128]{3,2,1,0:T(8,128)}, f32[2,3,16,128]{3,2,1,0:T(8,128)S(1)}, u32[]{:S(2)}, u32[]{:S(2)}) %collective-permute-start.8) | collective-permute-done | bytes 49184 | tf_op jit(solution)/shard_map/ppermute | solution.py:221
  36.3 1.4 %collective-permute-done.9.r_9_ = f32[2,3,16,128]{3,2,1,0:T(8,128)S(1)} collective-permute-done((f32[2,3,16,128]{3,2,1,0:T(8,128)}, f32[2,3,16,128]{3,2,1,0:T(8,128)S(1)}, u32[]{:S(2)}, u32[]{:S(2)}) %collective-permute-start.9) | collective-permute-done | bytes 49184 | tf_op jit(solution)/shard_map/ppermute | solution.py:221
  37.8 0.6 %copy-done.8 = f32[2,3,16,128]{3,2,1,0:T(8,128)} copy-done((f32[2,3,16,128]{3,2,1,0:T(8,128)}, f32[2,3,16,128]{3,2,1,0:T(8,128)S(1)}, u32[]{:S(2)}) %copy-start.8) | copy-done | bytes 49176
  38.4 2.1 %shard_map.61 = (f32[3,16,16,128]{3,2,1,0:T(8,128)}, f32[4,16,128]{2,1,0:T(8,128)}) custom-call(f32[3,16,16,128]{3,2,1,0:T(8,128)} %r_0_.1, f32[3,16,16,128]{3,2,1,0:T(8,128)} %get-tuple-element.16.r_1_, f32[2,3,16,128]{3,2,1,0:T(8,128)} %get-tuple-element.17.r_2_, f32[10,16,128]{2,1,0:T(8,128)} %get-tuple-element.15.coef_ref.r_3_, ...), custom_call_target="tpu_custom_call" | custom-call | tf_op jit(solution)/shard_map/pallas_call | solution.py:225
  40.5 0.2 collective-permute-start.11
  40.7 2.2 %collective-permute-start.12 = (f32[4,16,128]{2,1,0:T(8,128)}, f32[4,16,128]{2,1,0:T(8,128)S(1)}, u32[]{:S(2)}, u32[]{:S(2)}) collective-permute-start(f32[4,16,128]{2,1,0:T(8,128)} %get-tuple-element.19), channel_id=1, source_target_pairs={{0,2},{1,3},{2,0},{3,1},{4,6},{5,7},{6,4},{7,5},{8,10},{9,11},{10,... | collective-permute-start | bytes 98312 | tf_op jit(solution)/shard_map/ppermute | solution.py:231
  42.9 1.4 %collective-permute-start.13 = (f32[4,16,128]{2,1,0:T(8,128)}, f32[4,16,128]{2,1,0:T(8,128)S(1)}, u32[]{:S(2)}, u32[]{:S(2)}) collective-permute-start(f32[4,16,128]{2,1,0:T(8,128)} %get-tuple-element.19), channel_id=1, source_target_pairs={{0,3},{1,0},{2,1},{3,2},{4,7},{5,4},{6,5},{7,6},{8,11},{9,8},{10,9... | collective-permute-start | bytes 98312 | tf_op jit(solution)/shard_map/ppermute | solution.py:231
  44.3 0.7 %collective-permute-done.12 = f32[4,16,128]{2,1,0:T(8,128)S(1)} collective-permute-done((f32[4,16,128]{2,1,0:T(8,128)}, f32[4,16,128]{2,1,0:T(8,128)S(1)}, u32[]{:S(2)}, u32[]{:S(2)}) %collective-permute-start.12) | collective-permute-done | bytes 32800 | tf_op jit(solution)/shard_map/ppermute | solution.py:231
  45.0 1.2 %collective-permute-done.13 = f32[4,16,128]{2,1,0:T(8,128)S(1)} collective-permute-done((f32[4,16,128]{2,1,0:T(8,128)}, f32[4,16,128]{2,1,0:T(8,128)S(1)}, u32[]{:S(2)}, u32[]{:S(2)}) %collective-permute-start.13) | collective-permute-done | bytes 32800 | tf_op jit(solution)/shard_map/ppermute | solution.py:231
  46.3 0.6 %fusion = f32[2,16,128]{2,1,0:T(8,128)} fusion(f32[1,4,16,128]{3,2,1,0:T(8,128)S(1)} %dynamic-slice_add_fusion, f32[16,128]{1,0:T(8,128)S(1)} %fusion.1), kind=kLoop, calls=%fused_computation.3 | loop fusion | flops 4096 | bytes 40960 | tf_op jit(solution)/shard_map/add | solution.py:239
  (35 shorter events, 0.1 us)
Async XLA Ops:
  2.5 8.9 %collective-permute-start = (f32[6,16,128]{2,1,0:T(8,128)}, f32[6,16,128]{2,1,0:T(8,128)S(1)}, u32[]{:S(2)}, u32[]{:S(2)}) collective-permute-start(f32[6,16,128]{2,1,0:T(8,128)} %get-tuple-element.11), channel_id=1, source_target_pairs={{0,4},{4,8},{8,12},{12,16},{16,20},{20,24},{24,28},{1,5},{5,9},{9,... | collective-permute-start | bytes 147464 | tf_op jit(solution)/shard_map/ppermute | solution.py:18
  7.4 6.2 %collective-permute-start.1 = (f32[6,16,128]{2,1,0:T(8,128)}, f32[6,16,128]{2,1,0:T(8,128)S(1)}, u32[]{:S(2)}, u32[]{:S(2)}) collective-permute-start(f32[6,16,128]{2,1,0:T(8,128)} %get-tuple-element.12), channel_id=1, source_target_pairs={{4,0},{8,4},{12,8},{16,12},{20,16},{24,20},{28,24},{5,1},{9,5},{13... | collective-permute-start | bytes 147464 | tf_op jit(solution)/shard_map/ppermute | solution.py:18
  8.7 4.9 %collective-permute-start.2 = (f32[6,16,128]{2,1,0:T(8,128)}, f32[6,16,128]{2,1,0:T(8,128)S(1)}, u32[]{:S(2)}, u32[]{:S(2)}) collective-permute-start(f32[6,16,128]{2,1,0:T(8,128)} %get-tuple-element.13), channel_id=1, source_target_pairs={{0,1},{1,2},{2,3},{4,5},{5,6},{6,7},{8,9},{9,10},{10,11},{12,13},{... | collective-permute-start | bytes 147464 | tf_op jit(solution)/shard_map/ppermute | solution.py:18
  10.2 4.9 %collective-permute-start.3 = (f32[6,16,128]{2,1,0:T(8,128)}, f32[6,16,128]{2,1,0:T(8,128)S(1)}, u32[]{:S(2)}, u32[]{:S(2)}) collective-permute-start(f32[6,16,128]{2,1,0:T(8,128)} %get-tuple-element.14), channel_id=1, source_target_pairs={{1,0},{2,1},{3,2},{5,4},{6,5},{7,6},{9,8},{10,9},{11,10},{13,12},{... | collective-permute-start | bytes 147464 | tf_op jit(solution)/shard_map/ppermute | solution.py:18
  11.5 3.6 %copy-start.6 = (f32[6,16,128]{2,1,0:T(8,128)}, f32[6,16,128]{2,1,0:T(8,128)S(1)}, u32[]{:S(2)}) copy-start(f32[6,16,128]{2,1,0:T(8,128)S(1)} %collective-permute-done.xlo_ref) | copy-start | bytes 147460
  13.6 1.5 %copy-start.7 = (f32[6,16,128]{2,1,0:T(8,128)}, f32[6,16,128]{2,1,0:T(8,128)S(1)}, u32[]{:S(2)}) copy-start(f32[6,16,128]{2,1,0:T(8,128)S(1)} %collective-permute-done.1.xhi_ref) | copy-start | bytes 147460
  13.6 1.5 %copy-start.9 = (f32[6,16,128]{2,1,0:T(8,128)}, f32[6,16,128]{2,1,0:T(8,128)S(1)}, u32[]{:S(2)}) copy-start(f32[6,16,128]{2,1,0:T(8,128)S(1)} %collective-permute-done.2.ylo_ref) | copy-start | bytes 147460
  18.3 9.2 %collective-permute-start.10 = (f32[2,3,16,128]{3,2,1,0:T(8,128)}, f32[2,3,16,128]{3,2,1,0:T(8,128)S(1)}, u32[]{:S(2)}, u32[]{:S(2)}) collective-permute-start(f32[2,3,16,128]{3,2,1,0:T(8,128)} %get-tuple-element.17.r_2_), channel_id=1, source_target_pairs={{0,28},{4,24},{8,20},{12,16},{16,12},{20,8},{24,4},{28,0},{1,29},{... | collective-permute-start | bytes 147464 | tf_op jit(solution)/shard_map/ppermute | solution.py:221
  24.0 7.3 %collective-permute-start.4 = (f32[2,3,16,128]{3,2,1,0:T(8,128)}, f32[2,3,16,128]{3,2,1,0:T(8,128)S(1)}, u32[]{:S(2)}, u32[]{:S(2)}) collective-permute-start(f32[2,3,16,128]{3,2,1,0:T(8,128)} %get-tuple-element.17.r_2_), channel_id=1, source_target_pairs={{0,4},{4,0},{8,12},{12,8},{16,20},{20,16},{24,28},{28,24},{1,5},{5... | collective-permute-start | bytes 147464 | tf_op jit(solution)/shard_map/ppermute | solution.py:221
  25.4 5.9 %collective-permute-start.5 = (f32[2,3,16,128]{3,2,1,0:T(8,128)}, f32[2,3,16,128]{3,2,1,0:T(8,128)S(1)}, u32[]{:S(2)}, u32[]{:S(2)}) collective-permute-start(f32[2,3,16,128]{3,2,1,0:T(8,128)} %get-tuple-element.17.r_2_), channel_id=1, source_target_pairs={{0,8},{4,12},{8,0},{12,4},{16,24},{20,28},{24,16},{28,20},{1,9},{5... | collective-permute-start | bytes 147464 | tf_op jit(solution)/shard_map/ppermute | solution.py:221
  25.4 5.9 %collective-permute-start.6 = (f32[2,3,16,128]{3,2,1,0:T(8,128)}, f32[2,3,16,128]{3,2,1,0:T(8,128)S(1)}, u32[]{:S(2)}, u32[]{:S(2)}) collective-permute-start(f32[2,3,16,128]{3,2,1,0:T(8,128)} %get-tuple-element.17.r_2_), channel_id=1, source_target_pairs={{0,12},{4,8},{8,4},{12,0},{16,28},{20,24},{24,20},{28,16},{1,13},{... | collective-permute-start | bytes 147464 | tf_op jit(solution)/shard_map/ppermute | solution.py:221
  27.4 6.3 %collective-permute-start.7 = (f32[2,3,16,128]{3,2,1,0:T(8,128)}, f32[2,3,16,128]{3,2,1,0:T(8,128)S(1)}, u32[]{:S(2)}, u32[]{:S(2)}) collective-permute-start(f32[2,3,16,128]{3,2,1,0:T(8,128)} %get-tuple-element.17.r_2_), channel_id=1, source_target_pairs={{0,16},{4,20},{8,24},{12,28},{16,0},{20,4},{24,8},{28,12},{1,17},{... | collective-permute-start | bytes 147464 | tf_op jit(solution)/shard_map/ppermute | solution.py:221
  27.5 10.3 %copy-start = (f32[2,3,16,128]{3,2,1,0:T(8,128)}, f32[2,3,16,128]{3,2,1,0:T(8,128)S(1)}, u32[]{:S(2)}) copy-start(f32[2,3,16,128]{3,2,1,0:T(8,128)S(1)} %collective-permute-done.10.r_10_) | copy-start | bytes 147460
  27.5 8.9 %collective-permute-start.8 = (f32[2,3,16,128]{3,2,1,0:T(8,128)}, f32[2,3,16,128]{3,2,1,0:T(8,128)S(1)}, u32[]{:S(2)}, u32[]{:S(2)}) collective-permute-start(f32[2,3,16,128]{3,2,1,0:T(8,128)} %get-tuple-element.17.r_2_), channel_id=1, source_target_pairs={{0,20},{4,16},{8,28},{12,24},{16,4},{20,0},{24,12},{28,8},{1,21},{... | collective-permute-start | bytes 147464 | tf_op jit(solution)/shard_map/ppermute | solution.py:221
  31.3 6.5 %copy-start.1 = (f32[2,3,16,128]{3,2,1,0:T(8,128)}, f32[2,3,16,128]{3,2,1,0:T(8,128)S(1)}, u32[]{:S(2)}) copy-start(f32[2,3,16,128]{3,2,1,0:T(8,128)S(1)} %collective-permute-done.4.r_4_) | copy-start | bytes 147460
  31.3 6.5 %collective-permute-start.9 = (f32[2,3,16,128]{3,2,1,0:T(8,128)}, f32[2,3,16,128]{3,2,1,0:T(8,128)S(1)}, u32[]{:S(2)}, u32[]{:S(2)}) collective-permute-start(f32[2,3,16,128]{3,2,1,0:T(8,128)} %get-tuple-element.17.r_2_), channel_id=1, source_target_pairs={{0,24},{4,28},{8,16},{12,20},{16,8},{20,12},{24,0},{28,4},{1,25},{... | collective-permute-start | bytes 147464 | tf_op jit(solution)/shard_map/ppermute | solution.py:221
  31.3 6.5 %copy-start.2 = (f32[2,3,16,128]{3,2,1,0:T(8,128)}, f32[2,3,16,128]{3,2,1,0:T(8,128)S(1)}, u32[]{:S(2)}) copy-start(f32[2,3,16,128]{3,2,1,0:T(8,128)S(1)} %collective-permute-done.5.r_5_) | copy-start | bytes 147460
  31.3 6.5 %copy-start.3 = (f32[2,3,16,128]{3,2,1,0:T(8,128)}, f32[2,3,16,128]{3,2,1,0:T(8,128)S(1)}, u32[]{:S(2)}) copy-start(f32[2,3,16,128]{3,2,1,0:T(8,128)S(1)} %collective-permute-done.6.r_6_) | copy-start | bytes 147460
  33.7 4.1 %copy-start.4 = (f32[2,3,16,128]{3,2,1,0:T(8,128)}, f32[2,3,16,128]{3,2,1,0:T(8,128)S(1)}, u32[]{:S(2)}) copy-start(f32[2,3,16,128]{3,2,1,0:T(8,128)S(1)} %collective-permute-done.7.r_7_) | copy-start | bytes 147460
  36.3 1.5 %copy-start.5 = (f32[2,3,16,128]{3,2,1,0:T(8,128)}, f32[2,3,16,128]{3,2,1,0:T(8,128)S(1)}, u32[]{:S(2)}) copy-start(f32[2,3,16,128]{3,2,1,0:T(8,128)S(1)} %collective-permute-done.8.r_8_) | copy-start | bytes 147460
  40.5 3.8 %collective-permute-start.11 = (f32[4,16,128]{2,1,0:T(8,128)}, f32[4,16,128]{2,1,0:T(8,128)S(1)}, u32[]{:S(2)}, u32[]{:S(2)}) collective-permute-start(f32[4,16,128]{2,1,0:T(8,128)} %get-tuple-element.19), channel_id=1, source_target_pairs={{0,1},{1,2},{2,3},{3,0},{4,5},{5,6},{6,7},{7,4},{8,9},{9,10},{10,1... | collective-permute-start | bytes 98312 | tf_op jit(solution)/shard_map/ppermute | solution.py:231
  40.7 4.3 %collective-permute-start.12 = (f32[4,16,128]{2,1,0:T(8,128)}, f32[4,16,128]{2,1,0:T(8,128)S(1)}, u32[]{:S(2)}, u32[]{:S(2)}) collective-permute-start(f32[4,16,128]{2,1,0:T(8,128)} %get-tuple-element.19), channel_id=1, source_target_pairs={{0,2},{1,3},{2,0},{3,1},{4,6},{5,7},{6,4},{7,5},{8,10},{9,11},{10,... | collective-permute-start | bytes 98312 | tf_op jit(solution)/shard_map/ppermute | solution.py:231
  42.9 3.3 %collective-permute-start.13 = (f32[4,16,128]{2,1,0:T(8,128)}, f32[4,16,128]{2,1,0:T(8,128)S(1)}, u32[]{:S(2)}, u32[]{:S(2)}) collective-permute-start(f32[4,16,128]{2,1,0:T(8,128)} %get-tuple-element.19), channel_id=1, source_target_pairs={{0,3},{1,0},{2,1},{3,2},{4,7},{5,4},{6,5},{7,6},{8,11},{9,8},{10,9... | collective-permute-start | bytes 98312 | tf_op jit(solution)/shard_map/ppermute | solution.py:231
  44.3 1.9 %copy-start.11 = (f32[4,16,128]{2,1,0:T(8,128)S(1)}, f32[4,16,128]{2,1,0:T(8,128)}, u32[]{:S(2)}) copy-start(f32[4,16,128]{2,1,0:T(8,128)} %get-tuple-element.19) | copy-start | bytes 98308
  (2 other events, 1.2 us)
